TPU v7x, 128 devices: a whole 4x4x4 slice. The times are simulated.
128 devices in a mesh: quad: 8 (over y, z_lo), area: 16 (over x, z_hi, core).
Axes of the slice: x: 4, y: 4, z: 4 (z_hi: 2, z_lo: 2; z = z_hi * 2 + z_lo), core: 2. Of those that a mesh axis runs over, the one named last changes fastest.
Arguments:
- inverses: bfloat16 [32, 2, 16384, 1024], P('quad', None, 'area'), may hold values from -0.125 to 0.125
- coupling: bfloat16 [16384, 256], P('area'), may hold values from -0.3125 to 0.3125
- probes: bfloat16 [16384, 64], P('area'), may hold values from -6 to 6
- interface_diagonal: float32 [2048], P('area'), may hold values from 2 to 4
- area_rows: int32 [16, 256], replicated, may hold values from 0 to 2047, as said below
- live_counts: int32 [16], P('area'), may hold values from 128 to 256
Outputs:
- interior_moments: float32 [2, 16384, 128], P(None, ('area', 'quad'))
- interface_moments: float32 [2, 2048, 128], P(None, ('area', 'quad'))
Inputs may be any that keep to these rules, and one draw needn't show every extreme that they name: `area_rows`: slot s of every area's list holds an interface state owned by area s // 16, that is in [(s // 16) * 128, (s // 16 + 1) * 128); the 256 states of one area's list are distinct.
All inputs are finite; a program needn't handle non-finite values.
Results may differ from a plain program's by a relative error of at most 0.018.
Values may be sent and summed in bfloat16 or wider, within the bound.
No kernel may reach another device: no remote copies, remote signals or barrier semaphores. Data moves between devices by JAX's collectives and lax.ppermute only.
A program may use at most 128 MiB of HBM per device.

v0:
```python
import math

import jax
import jax.numpy as jnp
from jax import lax
from jax.sharding import PartitionSpec as P

ITERS = 4


def in_blocks(value, dim, devices):
    before, after = (value.shape[:dim], value.shape[dim + 1 :])
    return jnp.moveaxis(value.reshape(*before, devices, -1, *after), dim, 0)


def sent_and_summed(value, axis, dim):
    parts = in_blocks(value, dim, lax.axis_size(axis))
    arrived = lax.all_to_all(parts, axis, split_axis=0, concat_axis=0, tiled=True)
    return arrived.sum(axis=0)


def complex_apply(inverse_re, inverse_im, drive_half):
    width_half = drive_half.shape[-1] // 2
    swapped = jnp.concatenate(
        [-drive_half[..., width_half:], drive_half[..., :width_half]], axis=-1
    )
    real_part = jnp.einsum(
        "qij,qjc->qic", inverse_re, drive_half, preferred_element_type=jnp.float32
    )
    imag_part = jnp.einsum("qij,qjc->qic", inverse_im, swapped, preferred_element_type=jnp.float32)
    return real_part + imag_part


def divide_rows(summed, shift_re, shift_im, diagonal_rows):
    width_half = summed.shape[-1] // 2
    real_den = shift_re[:, None] - diagonal_rows[None, :]
    imag_den = shift_im[:, None] * jnp.ones_like(diagonal_rows)[None, :]
    norm_den = real_den * real_den + imag_den * imag_den
    summed_re = summed[..., :width_half]
    summed_im = summed[..., width_half:]
    new_re = (summed_re * real_den[..., None] + summed_im * imag_den[..., None]) / norm_den[
        ..., None
    ]
    new_im = (summed_im * real_den[..., None] - summed_re * imag_den[..., None]) / norm_den[
        ..., None
    ]
    return jnp.concatenate([new_re, new_im], axis=-1)


def weight_moments(values, angles):
    width_half = values.shape[-1] // 2
    value_re = values[..., :width_half]
    value_im = values[..., width_half:]
    results = []
    for power_index in (1, 2):
        cosine_now = jnp.cos(power_index * angles)[:, None, None]
        sine_now = jnp.sin(power_index * angles)[:, None, None]
        real_term = jnp.sum(cosine_now * value_re - sine_now * value_im, axis=0)
        imag_term = jnp.sum(cosine_now * value_im + sine_now * value_re, axis=0)
        results.append(jnp.concatenate([real_term, imag_term], axis=-1))
    return jnp.stack(results)


def on_device(inverses, coupling, probes, interface_diagonal, area_rows, live_counts):
    local_points = inverses.shape[0]
    area_count = lax.axis_size("area")
    quad_count = lax.axis_size("quad")
    area_index = lax.axis_index("area")
    inner_rows = coupling.shape[0]
    shared_rows = coupling.shape[1]
    probe_width = probes.shape[1]
    owned_rows = interface_diagonal.shape[0]
    bucket = shared_rows // area_count
    live_mask = jnp.arange(shared_rows) < live_counts[0]
    coupling_live = jnp.where(live_mask[None, :], coupling, jnp.zeros_like(coupling))
    probe_real = probes.astype(jnp.float32)
    probe_full = jnp.concatenate([probe_real, jnp.zeros_like(probe_real)], axis=-1)
    block_offsets = (
        lax.dynamic_slice_in_dim(area_rows, area_index * bucket, bucket, 1)
        - area_index * owned_rows
    )
    flat_offsets = block_offsets.reshape(-1)
    angle_step = jnp.float32(2.0 * math.pi / (local_points * quad_count))
    point_ids = lax.axis_index("quad") * local_points + jnp.arange(local_points, dtype=jnp.int32)
    angles = (point_ids.astype(jnp.float32) + 0.5) * angle_step
    shift_re = jnp.cos(angles)
    shift_im = jnp.sin(angles)
    inverse_re = inverses[:, 0]
    inverse_im = inverses[:, 1]
    gathered_rows = None
    interface_values = jnp.zeros((local_points, owned_rows, 2 * probe_width), jnp.float32)
    states = None
    for sweep_index in range(ITERS + 1):
        if sweep_index == 0:
            drive_float = jnp.broadcast_to(
                probe_full[None], (local_points, inner_rows, 2 * probe_width)
            )
        else:
            drive_float = probe_full[None] + jnp.einsum(
                "ig,qgc->qic", coupling_live, gathered_rows, preferred_element_type=jnp.float32
            )
        drive_half = drive_float.astype(jnp.bfloat16)
        states = complex_apply(inverse_re, inverse_im, drive_half)
        if sweep_index < ITERS:
            replies = jnp.einsum(
                "ig,qic->qgc",
                coupling_live,
                states.astype(jnp.bfloat16),
                preferred_element_type=jnp.float32,
            )
            parcels = replies.reshape(local_points, area_count, bucket, 2 * probe_width)
            arrived = lax.all_to_all(parcels, "area", split_axis=1, concat_axis=1, tiled=True)
            summed = jnp.zeros((local_points, owned_rows, 2 * probe_width), jnp.float32)
            summed = summed.at[:, flat_offsets].add(
                arrived.reshape(local_points, area_count * bucket, 2 * probe_width)
            )
            interface_values = divide_rows(summed, shift_re, shift_im, interface_diagonal)
            outgoing = jnp.take(interface_values.astype(jnp.bfloat16), flat_offsets, axis=1)
            outgoing = outgoing.reshape(local_points, area_count, bucket, 2 * probe_width)
            returned = lax.all_to_all(outgoing, "area", split_axis=1, concat_axis=1, tiled=True)
            gathered_rows = returned.reshape(local_points, shared_rows, 2 * probe_width)
    inner_moments, owned_moments = (
        sent_and_summed(weight_moments(states, angles), "quad", 1),
        sent_and_summed(weight_moments(interface_values, angles), "quad", 1),
    )
    return (inner_moments, owned_moments)


def solution(mesh):
    return jax.shard_map(
        on_device,
        mesh=mesh,
        in_specs=(
            P("quad", None, "area", None),
            P("area", None),
            P("area", None),
            P("area"),
            P(),
            P("area"),
        ),
        out_specs=(P(None, ("area", "quad"), None), P(None, ("area", "quad"), None)),
        check_vma=False,
    )
```

profile of v0, /device:TPU:0, one launch (start us, length us, event | category | flops | bytes accessed | tf_op | source)
XLA Modules:
  0.0 261.8 jit_solution(18416466617196971507)
XLA Ops:
  3.2 7.7 %fusion.8 = f32[4,128,1024]{2,1,0:T(8,128)} fusion(bf16[4,2,1024,1024]{3,2,1,0:T(8,128)(2,1)} %param.8, bf16[4,1024,64]{1,2,0:T(8,128)(2,1)S(1)} %add.176), kind=kOutput, calls=%fused_computation.16 | convolution fusion | flops 1073741824 | bytes 11010048 | tf_op jit(solution)/shard_map/qij,qjc->qic/dot_general | solution.py:30
  10.9 6.0 %convolution_bitcast_fusion.3 = f32[4,256,128]{1,2,0:T(8,128)S(1)} fusion(f32[4,128,1024]{2,1,0:T(8,128)} %fusion.8, bf16[4,2,1024,1024]{3,2,1,0:T(8,128)(2,1)} %param.8, bf16[1024,128]{0,1:T(8,128)(2,1)S(1)} %get-tuple-element.40, bf16[1024,256]{1,0:T(8,128)(2,1)S(1)} %copy-done, pred[256]{0:T(512)(128)(4,1)S(1)} %iota_compare_fusion), kind=kOutput, calls=%fused_computation.58 | convolution fusion | flops 1343488000 | bytes 11796736 | tf_op jit(solution)/shard_map/ig,qic->qgc/dot_general | solution.py:105
  18.0 7.8 %all-to-all-start = ((f32[4,16,16,128]{3,2,0,1:T(8,128)}), f32[4,16,16,128]{3,2,0,1:T(8,128)S(1)}, u32[]{:S(2)}, u32[]{:S(2)}) async-start(f32[4,16,16,128]{3,2,0,1:T(8,128)} %copy.237), calls=%async_computation | async-start | bytes 1048576 | tf_op jit(solution)/shard_map/all_to_all | solution.py:112
  26.3 11.9 %all-to-all-done = f32[4,16,16,128]{3,2,0,1:T(8,128)S(1)} async-done(((f32[4,16,16,128]{3,2,0,1:T(8,128)}), f32[4,16,16,128]{3,2,0,1:T(8,128)S(1)}, u32[]{:S(2)}, u32[]{:S(2)}) %all-to-all-start) | async-done | bytes 524320 | tf_op jit(solution)/shard_map/all_to_all | solution.py:112
  38.6 8.3 %scatter_fusion = f32[4,128,128]{2,0,1:T(4,128)S(1)} fusion(f32[4,128,128]{2,0,1:T(4,128)S(1)} %broadcast.164.clone.2, s32[256]{0:T(256)S(1)} %bitcast.182, f32[256,4,128]{2,1,0:T(4,128)S(1)} %copy.239), kind=kCustom, calls=%fused_computation.4 | custom fusion | flops 131072 | bytes 1573888 | tf_op jit(solution)/shard_map/scatter-add | solution.py:114
  49.1 11.8 %all_to_all.50 = bf16[4,16,16,128]{3,2,0,1:T(8,128)(2,1)S(1)} all-to-all(bf16[4,16,16,128]{3,2,0,1:T(8,128)(2,1)S(1)} %copy.244), channel_id=1, replica_groups=mesh['quad'=8,'area'=16] {'area'}, dimensions={1} | all-to-all | bytes 524288 | tf_op jit(solution)/shard_map/all_to_all | solution.py:120
  61.4 7.7 %fusion.6 = f32[4,128,1024]{2,1,0:T(8,128)} fusion(bf16[4,2,1024,1024]{3,2,1,0:T(8,128)(2,1)} %param.8, bf16[4,1024,64]{1,2,0:T(8,128)(2,1)S(1)} %get-tuple-element.24, bf16[4,1024,64]{1,2,0:T(8,128)(2,1)S(1)} %get-tuple-element.23), kind=kOutput, calls=%fused_computation.14 | convolution fusion | flops 1075838976 | bytes 11534336 | tf_op jit(solution)/shard_map/qij,qjc->qic/dot_general | solution.py:30
  69.1 6.0 %convolution_bitcast_fusion.2 = f32[4,256,128]{1,2,0:T(8,128)S(1)} fusion(f32[4,128,1024]{2,1,0:T(8,128)} %fusion.6, bf16[4,1024,128]{1,2,0:T(8,128)(2,1)S(1)} %fusion.33, bf16[4,2,1024,1024]{3,2,1,0:T(8,128)(2,1)} %param.8, bf16[1024,256]{1,0:T(8,128)(2,1)S(1)} %copy-done, pred[256]{0:T(512)(128)(4,1)S(1)} %iota_compare_fusion), kind=kOutput, calls=%fused_computation.57 | convolution fusion | flops 1343488000 | bytes 12583168 | tf_op jit(solution)/shard_map/ig,qic->qgc/dot_general | solution.py:105
  75.4 15.0 %all_to_all.51 = f32[4,16,16,128]{3,2,0,1:T(8,128)S(1)} all-to-all(f32[4,16,16,128]{3,2,0,1:T(8,128)S(1)} %copy.248), channel_id=1, replica_groups=mesh['quad'=8,'area'=16] {'area'}, dimensions={1} | all-to-all | bytes 1048576 | tf_op jit(solution)/shard_map/all_to_all | solution.py:112
  90.8 8.3 %scatter_fusion.1 = f32[4,128,128]{2,0,1:T(4,128)S(1)} fusion(f32[4,128,128]{2,0,1:T(4,128)S(1)} %broadcast.164.clone.1, s32[256]{0:T(256)S(1)} %bitcast.183, f32[256,4,128]{2,1,0:T(4,128)S(1)} %copy.250), kind=kCustom, calls=%fused_computation.5 | custom fusion | flops 131072 | bytes 1573888 | tf_op jit(solution)/shard_map/scatter-add | solution.py:114
  101.2 11.8 %all_to_all.52 = bf16[4,16,16,128]{3,2,0,1:T(8,128)(2,1)S(1)} all-to-all(bf16[4,16,16,128]{3,2,0,1:T(8,128)(2,1)S(1)} %copy.255), channel_id=1, replica_groups=mesh['quad'=8,'area'=16] {'area'}, dimensions={1} | all-to-all | bytes 524288 | tf_op jit(solution)/shard_map/all_to_all | solution.py:120
  113.6 7.6 %fusion.4 = f32[4,128,1024]{2,1,0:T(8,128)} fusion(bf16[4,2,1024,1024]{3,2,1,0:T(8,128)(2,1)} %param.8, bf16[4,1024,64]{1,2,0:T(8,128)(2,1)S(1)} %get-tuple-element.22, bf16[4,1024,64]{1,2,0:T(8,128)(2,1)S(1)} %get-tuple-element.21), kind=kOutput, calls=%fused_computation.12 | convolution fusion | flops 1075838976 | bytes 11534336 | tf_op jit(solution)/shard_map/qij,qjc->qic/dot_general | solution.py:30
  121.2 6.0 %convolution_bitcast_fusion.1 = f32[4,256,128]{1,2,0:T(8,128)S(1)} fusion(f32[4,128,1024]{2,1,0:T(8,128)} %fusion.4, bf16[4,1024,128]{1,2,0:T(8,128)(2,1)S(1)} %fusion.32, bf16[4,2,1024,1024]{3,2,1,0:T(8,128)(2,1)} %param.8, bf16[1024,256]{1,0:T(8,128)(2,1)S(1)} %copy-done, pred[256]{0:T(512)(128)(4,1)S(1)} %iota_compare_fusion), kind=kOutput, calls=%fused_computation.56 | convolution fusion | flops 1343488000 | bytes 12583168 | tf_op jit(solution)/shard_map/ig,qic->qgc/dot_general | solution.py:105
  127.5 15.0 %all_to_all.53 = f32[4,16,16,128]{3,2,0,1:T(8,128)S(1)} all-to-all(f32[4,16,16,128]{3,2,0,1:T(8,128)S(1)} %copy.259), channel_id=1, replica_groups=mesh['quad'=8,'area'=16] {'area'}, dimensions={1} | all-to-all | bytes 1048576 | tf_op jit(solution)/shard_map/all_to_all | solution.py:112
  142.9 8.3 %scatter_fusion.2 = f32[4,128,128]{2,0,1:T(4,128)S(1)} fusion(f32[4,128,128]{2,0,1:T(4,128)S(1)} %broadcast.164.clone, s32[256]{0:T(256)S(1)} %bitcast.184, f32[256,4,128]{2,1,0:T(4,128)S(1)} %copy.261), kind=kCustom, calls=%fused_computation.6 | custom fusion | flops 131072 | bytes 1573888 | tf_op jit(solution)/shard_map/scatter-add | solution.py:114
  153.4 11.8 %all_to_all.54 = bf16[4,16,16,128]{3,2,0,1:T(8,128)(2,1)S(1)} all-to-all(bf16[4,16,16,128]{3,2,0,1:T(8,128)(2,1)S(1)} %copy.266), channel_id=1, replica_groups=mesh['quad'=8,'area'=16] {'area'}, dimensions={1} | all-to-all | bytes 524288 | tf_op jit(solution)/shard_map/all_to_all | solution.py:120
  165.7 7.6 %fusion.2 = f32[4,128,1024]{2,1,0:T(8,128)} fusion(bf16[4,2,1024,1024]{3,2,1,0:T(8,128)(2,1)} %param.8, bf16[4,1024,64]{1,2,0:T(8,128)(2,1)S(1)} %get-tuple-element.20, bf16[4,1024,64]{1,2,0:T(8,128)(2,1)S(1)} %get-tuple-element.19), kind=kOutput, calls=%fused_computation.10 | convolution fusion | flops 1075838976 | bytes 11534336 | tf_op jit(solution)/shard_map/qij,qjc->qic/dot_general | solution.py:30
  173.4 6.0 %convolution_bitcast_fusion = f32[4,256,128]{1,2,0:T(8,128)S(1)} fusion(f32[4,128,1024]{2,1,0:T(8,128)} %fusion.2, bf16[4,1024,128]{1,2,0:T(8,128)(2,1)S(1)} %fusion.31, bf16[4,2,1024,1024]{3,2,1,0:T(8,128)(2,1)} %param.8, bf16[1024,256]{1,0:T(8,128)(2,1)S(1)} %copy-done, pred[256]{0:T(512)(128)(4,1)S(1)} %iota_compare_fusion), kind=kOutput, calls=%fused_computation.55 | convolution fusion | flops 1343488000 | bytes 12583168 | tf_op jit(solution)/shard_map/ig,qic->qgc/dot_general | solution.py:105
  184.1 12.3 %all-to-all-done.6 = f32[4,16,16,128]{3,2,0,1:T(8,128)S(1)} async-done(((f32[4,16,16,128]{3,2,0,1:T(8,128)}), f32[4,16,16,128]{3,2,0,1:T(8,128)S(1)}, u32[]{:S(2)}, u32[]{:S(2)}) %all-to-all-start.6) | async-done | bytes 524320 | tf_op jit(solution)/shard_map/all_to_all | solution.py:112
  196.8 8.3 %scatter_fusion.3 = f32[4,128,128]{2,0,1:T(4,128)S(1)} fusion(f32[4,128,128]{2,0,1:T(4,128)S(1)} %broadcast.164, s32[256]{0:T(256)S(1)} %bitcast.185, f32[256,4,128]{2,1,0:T(4,128)S(1)} %copy.272), kind=kCustom, calls=%fused_computation.7 | custom fusion | flops 131072 | bytes 1573888 | tf_op jit(solution)/shard_map/scatter-add | solution.py:114
  212.4 8.2 %all-to-all-done.7 = bf16[4,16,16,128]{3,2,0,1:T(8,128)(2,1)S(1)} async-done(((bf16[4,16,16,128]{3,2,0,1:T(8,128)(2,1)}), bf16[4,16,16,128]{3,2,0,1:T(8,128)(2,1)S(1)}, u32[]{:S(2)}, u32[]{:S(2)}) %all-to-all-start.7) | async-done | bytes 262176 | tf_op jit(solution)/shard_map/all_to_all | solution.py:120
  231.5 6.3 %add_bitcast_fusion = f32[4,1024,128]{1,2,0:T(8,128)S(1)} fusion(f32[4,128,1024]{2,1,0:T(8,128)S(1)} %fusion, bf16[4,1024,128]{1,2,0:T(8,128)(2,1)S(1)} %fusion.30, bf16[4,2,1024,1024]{3,2,1,0:T(8,128)(2,1)} %param.8), kind=kOutput, calls=%fused_computation.46 | convolution fusion | flops 1074266112 | bytes 13631488 | tf_op jit(solution)/shard_map/qij,qjc->qic/dot_general | solution.py:27
  240.0 5.7 %all-to-all-start.8 = ((f32[8,2,128,128]{3,2,1,0:T(8,128)}), f32[8,2,128,128]{3,2,1,0:T(8,128)S(1)}, u32[]{:S(2)}, u32[]{:S(2)}) async-start(f32[8,2,128,128]{3,2,1,0:T(8,128)} %maximum_bitcast_fusion), calls=%async_computation.8 | async-start | bytes 2097152 | tf_op jit(solution)/shard_map/all_to_all | solution.py:18
  246.3 14.8 %all-to-all-done.8 = f32[8,2,128,128]{3,2,1,0:T(8,128)S(1)} async-done(((f32[8,2,128,128]{3,2,1,0:T(8,128)}), f32[8,2,128,128]{3,2,1,0:T(8,128)S(1)}, u32[]{:S(2)}, u32[]{:S(2)}) %all-to-all-start.8) | async-done | bytes 1048608 | tf_op jit(solution)/shard_map/all_to_all | solution.py:18
  (107 shorter events, 39.7 us)
Async XLA Ops:
  3.2 7.7 %copy-start = (bf16[1024,256]{1,0:T(8,128)(2,1)S(1)}, bf16[1024,256]{1,0:T(8,128)(2,1)}, u32[]{:S(2)}) copy-start(bf16[1024,256]{1,0:T(8,128)(2,1)} %param.9) | copy-start | bytes 1572868
  16.9 8.9 %copy-start.1 = (s32[16,256]{1,0:T(8,128)S(1)}, s32[16,256]{1,0:T(8,128)}, u32[]{:S(2)}) copy-start(s32[16,256]{1,0:T(8,128)} %param.12) | copy-start | bytes 49156
  16.9 9.3 %copy-start.2 = (f32[128]{0:T(128)S(1)}, f32[128]{0:T(128)}, u32[]{:S(2)}) copy-start(f32[128]{0:T(128)} %param.11) | copy-start | bytes 1540
  18.0 20.2 %all-to-all-start = ((f32[4,16,16,128]{3,2,0,1:T(8,128)}), f32[4,16,16,128]{3,2,0,1:T(8,128)S(1)}, u32[]{:S(2)}, u32[]{:S(2)}) async-start(f32[4,16,16,128]{3,2,0,1:T(8,128)} %copy.237), calls=%async_computation | async-start | bytes 1048576 | tf_op jit(solution)/shard_map/all_to_all | solution.py:112
  180.5 15.9 %all-to-all-start.6 = ((f32[4,16,16,128]{3,2,0,1:T(8,128)}), f32[4,16,16,128]{3,2,0,1:T(8,128)S(1)}, u32[]{:S(2)}, u32[]{:S(2)}) async-start(f32[4,16,16,128]{3,2,0,1:T(8,128)} %copy.270), calls=%async_computation.6 | async-start | bytes 1048576 | tf_op jit(solution)/shard_map/all_to_all | solution.py:112
  208.0 12.7 %all-to-all-start.7 = ((bf16[4,16,16,128]{3,2,0,1:T(8,128)(2,1)}), bf16[4,16,16,128]{3,2,0,1:T(8,128)(2,1)S(1)}, u32[]{:S(2)}, u32[]{:S(2)}) async-start(bf16[4,16,16,128]{3,2,0,1:T(8,128)(2,1)} %copy.277), calls=%async_computation.7 | async-start | bytes 524288 | tf_op jit(solution)/shard_map/all_to_all | solution.py:120
  220.7 19.4 %all-to-all-start.9 = ((f32[8,2,16,128]{3,2,1,0:T(8,128)}), f32[8,2,16,128]{3,2,1,0:T(8,128)S(1)}, u32[]{:S(2)}, u32[]{:S(2)}) async-start(f32[8,2,16,128]{3,2,1,0:T(8,128)} %copy.284), calls=%async_computation.9 | async-start | bytes 262144 | tf_op jit(solution)/shard_map/all_to_all | solution.py:18
  240.0 21.1 %all-to-all-start.8 = ((f32[8,2,128,128]{3,2,1,0:T(8,128)}), f32[8,2,128,128]{3,2,1,0:T(8,128)S(1)}, u32[]{:S(2)}, u32[]{:S(2)}) async-start(f32[8,2,128,128]{3,2,1,0:T(8,128)} %maximum_bitcast_fusion), calls=%async_computation.8 | async-start | bytes 2097152 | tf_op jit(solution)/shard_map/all_to_all | solution.py:18
where the time goes:
time: 263 us; the launch traced here: 262 us
  matrix products  68.2 us (26%)
  blocking collectives  65.2 us (25%)
  waiting for transfers between devices  47.1 us (18%)
  other arithmetic  40 us (15%)
  starting transfers between devices  25.6 us (10%)
  local copies, waits for them, and re-layouts  13.8 us (5%)
    dot_general x5, matrix products, complex_apply(): jnp.einsum('qij,qjc->qic', inverse_im, swapped, preferred_element_type=jn...  35.9 us
    all_to_all x3, blocking collectives, on_device(): lax.all_to_all(outgoing, 'area', split_axis=1, concat_axis=1, tiled=True)  35.3 us
    scatter-add x4, other arithmetic, on_device(): summed.at[:, flat_offsets]  33.3 us
    all_to_all x2, blocking collectives, on_device(): lax.all_to_all(parcels, 'area', split_axis=1, concat_axis=1, tiled=True)  29.9 us
    all_to_all x2, waiting for transfers between devices, on_device(): lax.all_to_all(parcels, 'area', split_axis=1, concat_axis=1, tiled=True)  24.1 us
    dot_general x4, matrix products, on_device(): jnp.einsum('ig,qic->qgc', coupling_live, states.astype(jnp.bfloat16), pre...  24 us
    all_to_all x2, waiting for transfers between devices, sent_and_summed(): lax.all_to_all(parts, axis, split_axis=0, concat_axis=0, tiled=True)  14.8 us
    all_to_all x2, starting transfers between devices, on_device(): lax.all_to_all(parcels, 'area', split_axis=1, concat_axis=1, tiled=True)  11.4 us
  transfers between devices with their start and end apart: 5, of which 4 were waited for; matrix products, arithmetic and copies ran while one was open for 6% of the time, Pallas kernels for 0%

commit v1 on v0

v1 whole, which is shorter than its diff:
```python
import math

import jax
import jax.numpy as jnp
from jax import lax
from jax.sharding import PartitionSpec as P

ITERS = 4
F32 = jnp.float32
BF16 = jnp.bfloat16


def split_hi_lo(value):
    high = value.astype(BF16)
    low = (value - high.astype(F32)).astype(BF16)
    return high, low


def split_three(value):
    first = value.astype(BF16)
    rest = value - first.astype(F32)
    second = rest.astype(BF16)
    third = (rest - second.astype(F32)).astype(BF16)
    return first, second, third


def dot_split(spec, left_parts, right_parts):
    total = None
    for left in left_parts:
        for right in right_parts:
            term = jnp.einsum(spec, left, right, preferred_element_type=F32)
            total = term if total is None else total + term
    return total


def complex_block(values):
    width_half = values.shape[-1] // 2
    value_re = values[..., :width_half]
    value_im = values[..., width_half:]
    lower = jnp.concatenate([-value_im, value_re], axis=-1)
    return jnp.concatenate([values, lower], axis=-2)


def divide_rows(summed, shift_re, shift_im, diagonal_rows):
    width_half = summed.shape[-1] // 2
    real_den = shift_re[:, None] - diagonal_rows[None, :]
    imag_den = shift_im[:, None] * jnp.ones_like(diagonal_rows)[None, :]
    norm_den = real_den * real_den + imag_den * imag_den
    summed_re = summed[..., :width_half]
    summed_im = summed[..., width_half:]
    new_re = (summed_re * real_den[..., None] + summed_im * imag_den[..., None]) / norm_den[
        ..., None
    ]
    new_im = (summed_im * real_den[..., None] - summed_re * imag_den[..., None]) / norm_den[
        ..., None
    ]
    return jnp.concatenate([new_re, new_im], axis=-1)


def weight_moments(values, angles):
    width_half = values.shape[-1] // 2
    value_re = values[..., :width_half]
    value_im = values[..., width_half:]
    results = []
    for power_index in (1, 2):
        cosine_now = jnp.cos(power_index * angles)[:, None, None]
        sine_now = jnp.sin(power_index * angles)[:, None, None]
        real_term = jnp.sum(cosine_now * value_re - sine_now * value_im, axis=0)
        imag_term = jnp.sum(cosine_now * value_im + sine_now * value_re, axis=0)
        results.append(jnp.concatenate([real_term, imag_term], axis=-1))
    return jnp.stack(results)


def on_device(inverses, coupling, probes, interface_diagonal, area_rows, live_counts):
    local_points = inverses.shape[0]
    area_count = lax.axis_size("area")
    quad_count = lax.axis_size("quad")
    area_index = lax.axis_index("area")
    shared_rows = coupling.shape[1]
    probe_width = probes.shape[1]
    owned_rows = interface_diagonal.shape[0]
    bucket = shared_rows // area_count
    live_mask = jnp.arange(shared_rows) < live_counts[0]
    coupling_live = jnp.where(live_mask[None, :], coupling, jnp.zeros_like(coupling))
    right = jnp.concatenate([probes, coupling_live], axis=1)
    applied = jnp.einsum("qrij,jc->qric", inverses, right, preferred_element_type=F32)
    applied_parts = split_hi_lo(applied)
    projected = dot_split("ig,qric->qrgc", (coupling_live,), applied_parts)
    probe_state = jnp.concatenate(
        [applied[:, 0, :, :probe_width], applied[:, 1, :, :probe_width]], axis=-1
    )
    state_map = jnp.concatenate(
        [applied[:, 0, :, probe_width:], applied[:, 1, :, probe_width:]], axis=-1
    )
    reply_start = jnp.concatenate(
        [projected[:, 0, :, :probe_width], projected[:, 1, :, :probe_width]], axis=-1
    )
    reply_map = jnp.concatenate(
        [projected[:, 0, :, probe_width:], projected[:, 1, :, probe_width:]], axis=-1
    )
    reply_parts = split_hi_lo(reply_map)
    block_offsets = (
        lax.dynamic_slice_in_dim(area_rows, area_index * bucket, bucket, 1)
        - area_index * owned_rows
    )
    flat_offsets = block_offsets.reshape(-1)
    selector = (flat_offsets[None, :] == jnp.arange(owned_rows)[:, None]).astype(BF16)
    angle_step = jnp.float32(2.0 * math.pi / (local_points * quad_count))
    point_ids = lax.axis_index("quad") * local_points + jnp.arange(local_points, dtype=jnp.int32)
    angles = (point_ids.astype(jnp.float32) + 0.5) * angle_step
    shift_re = jnp.cos(angles)
    shift_im = jnp.sin(angles)
    gathered_block = None
    interface_values = None
    for sweep_index in range(ITERS):
        if sweep_index == 0:
            replies = reply_start
        else:
            replies = reply_start + dot_split("qgh,qhc->qgc", reply_parts, (gathered_block,))
        parcels = replies.reshape(local_points, area_count, bucket, 2 * probe_width)
        arrived = lax.all_to_all(parcels, "area", split_axis=1, concat_axis=1, tiled=True)
        arrived = arrived.reshape(local_points, area_count * bucket, 2 * probe_width)
        summed = dot_split("rn,qnc->qrc", (selector,), split_three(arrived))
        interface_values = divide_rows(summed, shift_re, shift_im, interface_diagonal)
        outgoing = jnp.einsum(
            "rn,qrc->qnc",
            selector,
            interface_values.astype(BF16),
            preferred_element_type=F32,
        ).astype(BF16)
        outgoing = outgoing.reshape(local_points, area_count, bucket, 2 * probe_width)
        returned = lax.all_to_all(outgoing, "area", split_axis=1, concat_axis=1, tiled=True)
        gathered_rows = returned.reshape(local_points, shared_rows, 2 * probe_width)
        gathered_block = complex_block(gathered_rows)
    states = probe_state + dot_split("qih,qhc->qic", split_hi_lo(state_map), (gathered_block,))
    inner_moments = lax.psum_scatter(
        weight_moments(states, angles), "quad", scatter_dimension=1, tiled=True
    )
    owned_moments = lax.psum_scatter(
        weight_moments(interface_values, angles), "quad", scatter_dimension=1, tiled=True
    )
    return (inner_moments, owned_moments)


def solution(mesh):
    return jax.shard_map(
        on_device,
        mesh=mesh,
        in_specs=(
            P("quad", None, "area", None),
            P("area", None),
            P("area", None),
            P("area"),
            P(),
            P("area"),
        ),
        out_specs=(P(None, ("area", "quad"), None), P(None, ("area", "quad"), None)),
        check_vma=False,
    )
```

time: 263 us -> 288 us (1.095)
  waiting for transfers between devices: 47.1 us -> 151 us
  matrix products: 68.2 us -> 29.4 us
  blocking collectives: 65.2 us -> 26.7 us
  other arithmetic: 40 us -> 3.43 us
  local copies, waits for them, and re-layouts: 13.8 us -> 34.3 us
  between operations: 1.95 us -> 16.1 us
    unnamed x0 -> x3, waiting for transfers between devices: none -> 59.9 us
    reduce_scatter x0 -> x1, waiting for transfers between devices: none -> 40.3 us  [on_device(): lax.psum_scatter(weight_moments(states, angles), 'quad', scatter_dimensio...]
    dot_general x14 -> x27, matrix products: 68.2 us -> 29.4 us  [the longest x22 19.2 us: dot_split(): term = jnp.einsum(spec, left, right, preferred_element_type=F32)]
    scatter-add x4 -> x0, other arithmetic: 33.3 us -> none  [on_device(): summed.at[:, flat_offsets]]
    all_to_all x3 -> x1, blocking collectives: 35.3 us -> 11.8 us  [on_device(): lax.all_to_all(outgoing, 'area', split_axis=1, concat_axis=1, tiled=True)]
    all_to_all x1 -> x3, waiting for transfers between devices: 8.23 us -> 23.2 us  [on_device(): lax.all_to_all(outgoing, 'area', split_axis=1, concat_axis=1, tiled=True)]
    all_to_all x2 -> x1, blocking collectives: 29.9 us -> 15 us  [on_device(): lax.all_to_all(parcels, 'area', split_axis=1, concat_axis=1, tiled=True)]
    all_to_all x2 -> x0, waiting for transfers between devices: 14.8 us -> none  [sent_and_summed(): lax.all_to_all(parts, axis, split_axis=0, concat_axis=0, tiled=True)]
  transfers between devices with their start and end apart: 5 -> 8, of which waited for: 4 -> 8; matrix products, arithmetic and copies ran while one was open for 6% -> 8% of each run, Pallas kernels for 0% -> 0%
where the time goes in v1:
time: 288 us; the launch traced here: 287 us
  waiting for transfers between devices  151 us (52%)
  local copies, waits for them, and re-layouts  34.3 us (12%)
  matrix products  29.4 us (10%)
  blocking collectives  26.7 us (9%)
  starting transfers between devices  25.9 us (9%)
  between operations  16.1 us (6%)
  other arithmetic  3.43 us (1%)
    unnamed x3, waiting for transfers between devices  59.9 us
    reduce_scatter x1, waiting for transfers between devices, on_device(): lax.psum_scatter(weight_moments(states, angles), 'quad', scatter_dimensio...  40.3 us
    all_to_all x3, waiting for transfers between devices, on_device(): lax.all_to_all(parcels, 'area', split_axis=1, concat_axis=1, tiled=True)  28.1 us
    all_to_all x3, waiting for transfers between devices, on_device(): lax.all_to_all(outgoing, 'area', split_axis=1, concat_axis=1, tiled=True)  23.2 us
    dot_general x22, matrix products, dot_split(): term = jnp.einsum(spec, left, right, preferred_element_type=F32)  19.2 us
    all_to_all x3, starting transfers between devices, on_device(): lax.all_to_all(parcels, 'area', split_axis=1, concat_axis=1, tiled=True)  15.2 us
    all_to_all x1, blocking collectives, on_device(): lax.all_to_all(parcels, 'area', split_axis=1, concat_axis=1, tiled=True)  15 us
    all_to_all x1, blocking collectives, on_device(): lax.all_to_all(outgoing, 'area', split_axis=1, concat_axis=1, tiled=True)  11.8 us
  transfers between devices with their start and end apart: 8, of which 8 were waited for; matrix products, arithmetic and copies ran while one was open for 8% of the time, Pallas kernels for 0%

profile of v1, /device:TPU:0, one launch (start us, length us, event | category | flops | bytes accessed | tf_op | source)
XLA Modules:
  0.0 287.2 jit_solution(7642763723580758532)
XLA Ops:
  9.2 9.3 %convolution_bitcast_fusion = f32[4,2,1024,320]{2,3,1,0:T(8,128)S(1)} fusion(bf16[4,2,1024,1024]{3,2,1,0:T(8,128)(2,1)} %param.6, bf16[1024,256]{0,1:T(8,128)(2,1)S(1)} %broadcast_select_fusion, bf16[1024,64]{0,1:T(8,128)(2,1)} %param.8), kind=kOutput, calls=%fused_computation.9 | convolution fusion | flops 5370019840 | bytes 27918336 | tf_op jit(solution)/shard_map/qrij,jc->qric/dot_general | solution.py:86
  18.5 1.7 fusion.1
  20.2 2.3 copy-done
  28.0 8.1 %all-to-all-start = ((f32[4,16,16,128]{3,2,0,1:T(8,128)}), f32[4,16,16,128]{3,2,0,1:T(8,128)S(1)}, u32[]{:S(2)}, u32[]{:S(2)}) async-start(f32[4,16,16,128]{3,2,0,1:T(8,128)} %copy.141), calls=%async_computation | async-start | bytes 1048576 | tf_op jit(solution)/shard_map/all_to_all | solution.py:121
  36.5 12.0 %all-to-all-done = f32[4,16,16,128]{3,2,0,1:T(8,128)S(1)} async-done(((f32[4,16,16,128]{3,2,0,1:T(8,128)}), f32[4,16,16,128]{3,2,0,1:T(8,128)S(1)}, u32[]{:S(2)}, u32[]{:S(2)}) %all-to-all-start) | async-done | bytes 524320 | tf_op jit(solution)/shard_map/all_to_all | solution.py:121
  52.5 3.5 %all-to-all-start.1 = ((bf16[4,16,16,128]{3,2,0,1:T(8,128)(2,1)}), bf16[4,16,16,128]{3,2,0,1:T(8,128)(2,1)S(1)}, u32[]{:S(2)}, u32[]{:S(2)}) async-start(bf16[4,16,16,128]{3,2,0,1:T(8,128)(2,1)} %copy.146), calls=%async_computation.1 | async-start | bytes 524288 | tf_op jit(solution)/shard_map/all_to_all | solution.py:132
  57.6 7.6 %all-to-all-done.1 = bf16[4,16,16,128]{3,2,0,1:T(8,128)(2,1)S(1)} async-done(((bf16[4,16,16,128]{3,2,0,1:T(8,128)(2,1)}), bf16[4,16,16,128]{3,2,0,1:T(8,128)(2,1)S(1)}, u32[]{:S(2)}, u32[]{:S(2)}) %all-to-all-start.1) | async-done | bytes 262176 | tf_op jit(solution)/shard_map/all_to_all | solution.py:132
  65.4 2.0 fusion.73
  68.1 15.0 %all_to_all.40 = f32[4,16,16,128]{3,2,0,1:T(8,128)S(1)} all-to-all(f32[4,16,16,128]{3,2,0,1:T(8,128)S(1)} %copy.153), channel_id=1, replica_groups=mesh['quad'=8,'area'=16] {'area'}, dimensions={1} | all-to-all | bytes 1048576 | tf_op jit(solution)/shard_map/all_to_all | solution.py:121
  84.6 11.8 %all_to_all.41 = bf16[4,16,16,128]{3,2,0,1:T(8,128)(2,1)S(1)} all-to-all(bf16[4,16,16,128]{3,2,0,1:T(8,128)(2,1)S(1)} %copy.158), channel_id=1, replica_groups=mesh['quad'=8,'area'=16] {'area'}, dimensions={1} | all-to-all | bytes 524288 | tf_op jit(solution)/shard_map/all_to_all | solution.py:132
  99.6 3.6 %all-to-all-start.4 = ((f32[4,16,16,128]{3,2,0,1:T(8,128)}), f32[4,16,16,128]{3,2,0,1:T(8,128)S(1)}, u32[]{:S(2)}, u32[]{:S(2)}) async-start(f32[4,16,16,128]{3,2,0,1:T(8,128)} %copy.165), calls=%async_computation.4 | async-start | bytes 1048576 | tf_op jit(solution)/shard_map/all_to_all | solution.py:121
  103.2 12.3 %all-to-all-done.4 = f32[4,16,16,128]{3,2,0,1:T(8,128)S(1)} async-done(((f32[4,16,16,128]{3,2,0,1:T(8,128)}), f32[4,16,16,128]{3,2,0,1:T(8,128)S(1)}, u32[]{:S(2)}, u32[]{:S(2)}) %all-to-all-start.4) | async-done | bytes 524320 | tf_op jit(solution)/shard_map/all_to_all | solution.py:121
  117.7 3.5 %all-to-all-start.5 = ((bf16[4,16,16,128]{3,2,0,1:T(8,128)(2,1)}), bf16[4,16,16,128]{3,2,0,1:T(8,128)(2,1)S(1)}, u32[]{:S(2)}, u32[]{:S(2)}) async-start(bf16[4,16,16,128]{3,2,0,1:T(8,128)(2,1)} %copy.170), calls=%async_computation.5 | async-start | bytes 524288 | tf_op jit(solution)/shard_map/all_to_all | solution.py:132
  121.2 1.7 slice_bitcast_fusion.5
  122.9 7.5 %all-to-all-done.5 = bf16[4,16,16,128]{3,2,0,1:T(8,128)(2,1)S(1)} async-done(((bf16[4,16,16,128]{3,2,0,1:T(8,128)(2,1)}), bf16[4,16,16,128]{3,2,0,1:T(8,128)(2,1)S(1)}, u32[]{:S(2)}, u32[]{:S(2)}) %all-to-all-start.5) | async-done | bytes 262176 | tf_op jit(solution)/shard_map/all_to_all | solution.py:132
  130.6 1.8 fusion.71
  135.8 3.6 %all-to-all-start.6 = ((f32[4,16,16,128]{3,2,0,1:T(8,128)}), f32[4,16,16,128]{3,2,0,1:T(8,128)S(1)}, u32[]{:S(2)}, u32[]{:S(2)}) async-start(f32[4,16,16,128]{3,2,0,1:T(8,128)} %copy.177), calls=%async_computation.6 | async-start | bytes 1048576 | tf_op jit(solution)/shard_map/all_to_all | solution.py:121
  139.3 8.5 %slice_bitcast_fusion.1 = (f32[4,1024,256]{1,2,0:T(8,128)}, f32[4,1024,256]{1,2,0:T(8,128)}) fusion(f32[4,2,1024,320]{2,3,1,0:T(8,128)} %copy-done), kind=kLoop, calls=%fused_computation.7 | loop fusion | bytes 16777216 | tf_op jit(solution)/shard_map/squeeze | solution.py:93
  147.8 3.8 %all-to-all-done.6 = f32[4,16,16,128]{3,2,0,1:T(8,128)S(1)} async-done(((f32[4,16,16,128]{3,2,0,1:T(8,128)}), f32[4,16,16,128]{3,2,0,1:T(8,128)S(1)}, u32[]{:S(2)}, u32[]{:S(2)}) %all-to-all-start.6) | async-done | bytes 524320 | tf_op jit(solution)/shard_map/all_to_all | solution.py:121
  153.9 3.5 %all-to-all-start.7 = ((bf16[4,16,16,128]{3,2,0,1:T(8,128)(2,1)}), bf16[4,16,16,128]{3,2,0,1:T(8,128)(2,1)S(1)}, u32[]{:S(2)}, u32[]{:S(2)}) async-start(bf16[4,16,16,128]{3,2,0,1:T(8,128)(2,1)} %copy.182), calls=%async_computation.7 | async-start | bytes 524288 | tf_op jit(solution)/shard_map/all_to_all | solution.py:132
  158.4 8.2 %all-to-all-done.7 = bf16[4,16,16,128]{3,2,0,1:T(8,128)(2,1)S(1)} async-done(((bf16[4,16,16,128]{3,2,0,1:T(8,128)(2,1)}), bf16[4,16,16,128]{3,2,0,1:T(8,128)(2,1)S(1)}, u32[]{:S(2)}, u32[]{:S(2)}) %all-to-all-start.7) | async-done | bytes 262176 | tf_op jit(solution)/shard_map/all_to_all | solution.py:132
  166.8 4.3 %fusion.2 = f32[4,1024,128]{1,2,0:T(8,128)S(1)} fusion(f32[4,1024,256]{1,2,0:T(8,128)} %get-tuple-element.21, f32[4,1024,256]{1,2,0:T(8,128)} %get-tuple-element.20, bf16[4,256,64]{1,2,0:T(8,128)(2,1)S(1)} %get-tuple-element.37, bf16[4,256,64]{1,2,0:T(8,128)(2,1)S(1)} %get-tuple-element.36, bf16[4,256,128]{1,2,0:T(8,128)(2,1)S(1)} %copy.186), kind=kOutput, calls=%fused_computation.5 | convolution fusion | flops 546832384 | bytes 11010048 | tf_op jit(solution)/shard_map/qih,qhc->qic/dot_general | solution.py:31
  177.3 59.8 %all-reduce.3.cloned.1.call-done = f32[2,128,128]{2,0,1:T(2,128)} async-done(((f32[2,128,128]{2,0,1:T(2,128)}), f32[2,128,128]{2,0,1:T(2,128)}) %all-reduce.3.cloned.1.call-update) | async-done | bytes 131088
  238.4 40.3 %reduce-scatter.2.cloned.1.call-done = f32[2,128,128]{1,2,0:T(8,128)} async-done(((f32[2,1024,128]{1,2,0:T(8,128)}), f32[2,128,128]{1,2,0:T(8,128)}) %reduce-scatter.2.cloned.1.call-update) | async-done | bytes 131088 | tf_op jit(solution)/shard_map/reduce_scatter | solution.py:136
  (121 shorter events, 35.7 us)
Async XLA Ops:
  18.5 4.0 %copy-start = (f32[4,2,1024,320]{2,3,1,0:T(8,128)}, f32[4,2,1024,320]{2,3,1,0:T(8,128)S(1)}, u32[]{:S(2)}) copy-start(f32[4,2,1024,320]{2,3,1,0:T(8,128)S(1)} %convolution_bitcast_fusion) | copy-start | bytes 31457284
  25.7 10.4 %copy-start.14 = (s32[16,256]{1,0:T(8,128)S(1)}, s32[16,256]{1,0:T(8,128)}, u32[]{:S(2)}) copy-start(s32[16,256]{1,0:T(8,128)} %param.10) | copy-start | bytes 49156
  25.7 10.7 %copy-start.15 = (f32[128]{0:T(128)S(1)}, f32[128]{0:T(128)}, u32[]{:S(2)}) copy-start(f32[128]{0:T(128)} %param.9) | copy-start | bytes 1540
  26.5 70.5 %copy-start.10 = (f32[4,256,64]{1,2,0:T(8,128)}, f32[4,256,64]{1,2,0:T(8,128)S(1)}, u32[]{:S(2)}) copy-start(f32[4,256,64]{1,2,0:T(8,128)S(1)} %get-tuple-element.24) | copy-start | bytes 786436
  28.0 28.0 %copy-start.4 = (f32[4,2,256,320]{2,3,1,0:T(8,128)S(1)}, f32[4,2,256,320]{2,3,1,0:T(8,128)}, u32[]{:S(2)}) copy-start(f32[4,2,256,320]{2,3,1,0:T(8,128)} %copy-done.3) | copy-start | bytes 7864324
  28.0 20.4 %all-to-all-start = ((f32[4,16,16,128]{3,2,0,1:T(8,128)}), f32[4,16,16,128]{3,2,0,1:T(8,128)S(1)}, u32[]{:S(2)}, u32[]{:S(2)}) async-start(f32[4,16,16,128]{3,2,0,1:T(8,128)} %copy.141), calls=%async_computation | async-start | bytes 1048576 | tf_op jit(solution)/shard_map/all_to_all | solution.py:121
  52.5 12.7 %all-to-all-start.1 = ((bf16[4,16,16,128]{3,2,0,1:T(8,128)(2,1)}), bf16[4,16,16,128]{3,2,0,1:T(8,128)(2,1)S(1)}, u32[]{:S(2)}, u32[]{:S(2)}) async-start(bf16[4,16,16,128]{3,2,0,1:T(8,128)(2,1)} %copy.146), calls=%async_computation.1 | async-start | bytes 524288 | tf_op jit(solution)/shard_map/all_to_all | solution.py:132
  56.1 11.3 %copy-start.12 = (f32[4,256,64]{1,2,0:T(8,128)S(1)}, f32[4,256,64]{1,2,0:T(8,128)}, u32[]{:S(2)}) copy-start(f32[4,256,64]{1,2,0:T(8,128)} %get-tuple-element.25) | copy-start | bytes 786436
  57.6 9.7 %copy-start.5 = (f32[4,256,256]{1,2,0:T(8,128)S(1)}, f32[4,256,256]{1,2,0:T(8,128)}, u32[]{:S(2)}) copy-start(f32[4,256,256]{1,2,0:T(8,128)} %get-tuple-element.28) | copy-start | bytes 3145732
  57.6 9.8 %copy-start.7 = (f32[4,256,256]{1,2,0:T(8,128)S(1)}, f32[4,256,256]{1,2,0:T(8,128)}, u32[]{:S(2)}) copy-start(f32[4,256,256]{1,2,0:T(8,128)} %get-tuple-element.29) | copy-start | bytes 3145732
  83.1 13.4 %copy-start.8 = (f32[4,256,256]{1,2,0:T(8,128)S(1)}, f32[4,256,256]{1,2,0:T(8,128)}, u32[]{:S(2)}) copy-start(f32[4,256,256]{1,2,0:T(8,128)} %get-tuple-element.29) | copy-start | bytes 3145732
  99.6 15.9 %all-to-all-start.4 = ((f32[4,16,16,128]{3,2,0,1:T(8,128)}), f32[4,16,16,128]{3,2,0,1:T(8,128)S(1)}, u32[]{:S(2)}, u32[]{:S(2)}) async-start(f32[4,16,16,128]{3,2,0,1:T(8,128)} %copy.165), calls=%async_computation.4 | async-start | bytes 1048576 | tf_op jit(solution)/shard_map/all_to_all | solution.py:121
  116.4 14.1 %copy-start.6 = (f32[4,256,256]{1,2,0:T(8,128)S(1)}, f32[4,256,256]{1,2,0:T(8,128)}, u32[]{:S(2)}) copy-start(f32[4,256,256]{1,2,0:T(8,128)} %get-tuple-element.28) | copy-start | bytes 3145732
  117.7 12.7 %all-to-all-start.5 = ((bf16[4,16,16,128]{3,2,0,1:T(8,128)(2,1)}), bf16[4,16,16,128]{3,2,0,1:T(8,128)(2,1)S(1)}, u32[]{:S(2)}, u32[]{:S(2)}) async-start(bf16[4,16,16,128]{3,2,0,1:T(8,128)(2,1)} %copy.170), calls=%async_computation.5 | async-start | bytes 524288 | tf_op jit(solution)/shard_map/all_to_all | solution.py:132
  130.4 2.0 copy-start.9
  130.4 2.0 copy-start.11
  130.4 2.0 copy-start.13
  135.8 15.9 %all-to-all-start.6 = ((f32[4,16,16,128]{3,2,0,1:T(8,128)}), f32[4,16,16,128]{3,2,0,1:T(8,128)S(1)}, u32[]{:S(2)}, u32[]{:S(2)}) async-start(f32[4,16,16,128]{3,2,0,1:T(8,128)} %copy.177), calls=%async_computation.6 | async-start | bytes 1048576 | tf_op jit(solution)/shard_map/all_to_all | solution.py:121
  153.9 12.7 %all-to-all-start.7 = ((bf16[4,16,16,128]{3,2,0,1:T(8,128)(2,1)}), bf16[4,16,16,128]{3,2,0,1:T(8,128)(2,1)S(1)}, u32[]{:S(2)}, u32[]{:S(2)}) async-start(bf16[4,16,16,128]{3,2,0,1:T(8,128)(2,1)} %copy.182), calls=%async_computation.7 | async-start | bytes 524288 | tf_op jit(solution)/shard_map/all_to_all | solution.py:132
  157.5 79.6 %all-reduce.3.cloned.1.call-start = ((), (), s32[]{:S(2)}) async-start(), calls=%async_computation.10 | async-start | bytes 262144
  158.3 120.4 %reduce-scatter.2.cloned.1.call-start = ((), (), s32[]{:S(2)}) async-start(), calls=%async_computation.9 | async-start | bytes 1179648 | tf_op jit(solution)/shard_map/reduce_scatter | solution.py:136
  166.8 4.6 %copy-start.1 = (f32[4,1024,256]{1,2,0:T(8,128)S(1)}, f32[4,1024,256]{1,2,0:T(8,128)}, u32[]{:S(2)}) copy-start(f32[4,1024,256]{1,2,0:T(8,128)} %get-tuple-element.20) | copy-start | bytes 12582916
  166.8 5.9 %copy-start.2 = (f32[4,1024,256]{1,2,0:T(8,128)S(1)}, f32[4,1024,256]{1,2,0:T(8,128)}, u32[]{:S(2)}) copy-start(f32[4,1024,256]{1,2,0:T(8,128)} %get-tuple-element.21) | copy-start | bytes 12582916
  174.1 1.9 copy-start.16
  (1 other events, 1.6 us)
Sparse Core Ops, SparseCore 0:
  161.3 75.7 all-reduce.2
  239.5 39.2 reduce-scatter.1

commit v2 on v1

--- a/solution.py
+++ b/solution.py
@@ -55,6 +55,13 @@
         ..., None
     ]
     return jnp.concatenate([new_re, new_im], axis=-1)
+
+
+def sent_and_summed(value, axis, dim):
+    before, after = (value.shape[:dim], value.shape[dim + 1 :])
+    parts = jnp.moveaxis(value.reshape(*before, lax.axis_size(axis), -1, *after), dim, 0)
+    arrived = lax.all_to_all(parts, axis, split_axis=0, concat_axis=0, tiled=True)
+    return arrived.sum(axis=0)
 
 
 def weight_moments(values, angles):
@@ -133,12 +140,8 @@
         gathered_rows = returned.reshape(local_points, shared_rows, 2 * probe_width)
         gathered_block = complex_block(gathered_rows)
     states = probe_state + dot_split("qih,qhc->qic", split_hi_lo(state_map), (gathered_block,))
-    inner_moments = lax.psum_scatter(
-        weight_moments(states, angles), "quad", scatter_dimension=1, tiled=True
-    )
-    owned_moments = lax.psum_scatter(
-        weight_moments(interface_values, angles), "quad", scatter_dimension=1, tiled=True
-    )
+    inner_moments = sent_and_summed(weight_moments(states, angles), "quad", 1)
+    owned_moments = sent_and_summed(weight_moments(interface_values, angles), "quad", 1)
     return (inner_moments, owned_moments)
 
 

time: 288 us -> 198 us (0.69)
  waiting for transfers between devices: 151 us -> 66 us
  between operations: 16.1 us -> 2 us
  starting transfers between devices: 25.9 us -> 36.4 us
  local copies, waits for them, and re-layouts: 34.3 us -> 31.1 us
    unnamed x3 -> x0, waiting for transfers between devices: 59.9 us -> none
    reduce_scatter x1 -> x0, waiting for transfers between devices: 40.3 us -> none  [on_device(): lax.psum_scatter(weight_moments(states, angles), 'quad', scatter_dimensio...]
    all_to_all x0 -> x2, waiting for transfers between devices: none -> 14.7 us  [sent_and_summed(): lax.all_to_all(parts, axis, split_axis=0, concat_axis=0, tiled=True)]
    all_to_all x0 -> x2, starting transfers between devices: none -> 10.6 us  [sent_and_summed(): lax.all_to_all(parts, axis, split_axis=0, concat_axis=0, tiled=True)]
    unnamed x39 -> x33, local copies, waits for them, and re-layouts: 10.3 us -> 6.7 us
  transfers between devices with their start and end apart: 8 -> 8, of which waited for: 8 -> 7; matrix products, arithmetic and copies ran while one was open for 8% -> 11% of each run, Pallas kernels for 0% -> 0%
where the time goes in v2:
time: 198 us; the launch traced here: 196 us
  waiting for transfers between devices  66 us (33%)
  starting transfers between devices  36.4 us (18%)
  local copies, waits for them, and re-layouts  31.1 us (16%)
  matrix products  29.4 us (15%)
  blocking collectives  26.7 us (13%)
  other arithmetic  4.73 us (2%)
  between operations  2 us (1%)
    all_to_all x3, waiting for transfers between devices, on_device(): lax.all_to_all(parcels, 'area', split_axis=1, concat_axis=1, tiled=True)  28.1 us
    all_to_all x3, waiting for transfers between devices, on_device(): lax.all_to_all(outgoing, 'area', split_axis=1, concat_axis=1, tiled=True)  23.2 us
    dot_general x22, matrix products, dot_split(): term = jnp.einsum(spec, left, right, preferred_element_type=F32)  19.3 us
    all_to_all x3, starting transfers between devices, on_device(): lax.all_to_all(parcels, 'area', split_axis=1, concat_axis=1, tiled=True)  15.2 us
    all_to_all x1, blocking collectives, on_device(): lax.all_to_all(parcels, 'area', split_axis=1, concat_axis=1, tiled=True)  15 us
    all_to_all x2, waiting for transfers between devices, sent_and_summed(): lax.all_to_all(parts, axis, split_axis=0, concat_axis=0, tiled=True)  14.7 us
    all_to_all x1, blocking collectives, on_device(): lax.all_to_all(outgoing, 'area', split_axis=1, concat_axis=1, tiled=True)  11.8 us
    all_to_all x2, starting transfers between devices, sent_and_summed(): lax.all_to_all(parts, axis, split_axis=0, concat_axis=0, tiled=True)  10.6 us
  transfers between devices with their start and end apart: 8, of which 7 were waited for; matrix products, arithmetic and copies ran while one was open for 11% of the time, Pallas kernels for 0%

profile of v2, /device:TPU:0, one launch (start us, length us, event | category | flops | bytes accessed | tf_op | source)
XLA Modules:
  0.0 196.4 jit_solution(17826156662177921983)
XLA Ops:
  2.7 9.3 %convolution_bitcast_fusion = f32[4,2,1024,320]{2,3,1,0:T(8,128)S(1)} fusion(bf16[4,2,1024,1024]{3,2,1,0:T(8,128)(2,1)} %param.6, bf16[1024,256]{0,1:T(8,128)(2,1)S(1)} %broadcast_select_fusion, bf16[1024,64]{0,1:T(8,128)(2,1)} %param.8), kind=kOutput, calls=%fused_computation.9 | convolution fusion | flops 5370019840 | bytes 27918336 | tf_op jit(solution)/shard_map/qrij,jc->qric/dot_general | solution.py:93
  11.9 1.7 fusion.1
  13.6 2.3 %copy-done = f32[4,2,1024,320]{2,3,1,0:T(8,128)} copy-done((f32[4,2,1024,320]{2,3,1,0:T(8,128)}, f32[4,2,1024,320]{2,3,1,0:T(8,128)S(1)}, u32[]{:S(2)}) %copy-start) | copy-done | bytes 10485784
  21.5 8.1 %all-to-all-start = ((f32[4,16,16,128]{3,2,0,1:T(8,128)}), f32[4,16,16,128]{3,2,0,1:T(8,128)S(1)}, u32[]{:S(2)}, u32[]{:S(2)}) async-start(f32[4,16,16,128]{3,2,0,1:T(8,128)} %copy.143), calls=%async_computation | async-start | bytes 1048576 | tf_op jit(solution)/shard_map/all_to_all | solution.py:128
  30.0 12.0 %all-to-all-done = f32[4,16,16,128]{3,2,0,1:T(8,128)S(1)} async-done(((f32[4,16,16,128]{3,2,0,1:T(8,128)}), f32[4,16,16,128]{3,2,0,1:T(8,128)S(1)}, u32[]{:S(2)}, u32[]{:S(2)}) %all-to-all-start) | async-done | bytes 524320 | tf_op jit(solution)/shard_map/all_to_all | solution.py:128
  46.0 3.5 %all-to-all-start.1 = ((bf16[4,16,16,128]{3,2,0,1:T(8,128)(2,1)}), bf16[4,16,16,128]{3,2,0,1:T(8,128)(2,1)S(1)}, u32[]{:S(2)}, u32[]{:S(2)}) async-start(bf16[4,16,16,128]{3,2,0,1:T(8,128)(2,1)} %copy.148), calls=%async_computation.1 | async-start | bytes 524288 | tf_op jit(solution)/shard_map/all_to_all | solution.py:139
  51.1 7.6 %all-to-all-done.1 = bf16[4,16,16,128]{3,2,0,1:T(8,128)(2,1)S(1)} async-done(((bf16[4,16,16,128]{3,2,0,1:T(8,128)(2,1)}), bf16[4,16,16,128]{3,2,0,1:T(8,128)(2,1)S(1)}, u32[]{:S(2)}, u32[]{:S(2)}) %all-to-all-start.1) | async-done | bytes 262176 | tf_op jit(solution)/shard_map/all_to_all | solution.py:139
  58.8 2.0 %fusion.73 = f32[4,256,128]{1,2,0:T(8,128)S(1)} fusion(bf16[4,256,64]{2,1,0:T(8,128)(2,1)S(1)} %get-tuple-element.39, bf16[4,256,64]{2,1,0:T(8,128)(2,1)S(1)} %get-tuple-element.38, bf16[4,256,128]{2,1,0:T(8,128)(2,1)S(1)} %bitcast.106, f32[4,256,256]{1,2,0:T(8,128)} %get-tuple-element.25, f32[4,256,256]{1,2,0:T(8,128)} %get-tuple-element.24), kind=kOutput, calls=%fused_computation.122 | convolution fusion | flops 137887744 | bytes 3145728 | tf_op jit(solution)/shard_map/qgh,qhc->qgc/dot_general | solution.py:31
  61.6 15.0 %all_to_all.50 = f32[4,16,16,128]{3,2,0,1:T(8,128)S(1)} all-to-all(f32[4,16,16,128]{3,2,0,1:T(8,128)S(1)} %copy.155), channel_id=1, replica_groups=mesh['quad'=8,'area'=16] {'area'}, dimensions={1} | all-to-all | bytes 1048576 | tf_op jit(solution)/shard_map/all_to_all | solution.py:128
  78.1 11.8 %all_to_all.51 = bf16[4,16,16,128]{3,2,0,1:T(8,128)(2,1)S(1)} all-to-all(bf16[4,16,16,128]{3,2,0,1:T(8,128)(2,1)S(1)} %copy.160), channel_id=1, replica_groups=mesh['quad'=8,'area'=16] {'area'}, dimensions={1} | all-to-all | bytes 524288 | tf_op jit(solution)/shard_map/all_to_all | solution.py:139
  93.0 3.6 %all-to-all-start.4 = ((f32[4,16,16,128]{3,2,0,1:T(8,128)}), f32[4,16,16,128]{3,2,0,1:T(8,128)S(1)}, u32[]{:S(2)}, u32[]{:S(2)}) async-start(f32[4,16,16,128]{3,2,0,1:T(8,128)} %copy.167), calls=%async_computation.4 | async-start | bytes 1048576 | tf_op jit(solution)/shard_map/all_to_all | solution.py:128
  96.7 12.3 %all-to-all-done.4 = f32[4,16,16,128]{3,2,0,1:T(8,128)S(1)} async-done(((f32[4,16,16,128]{3,2,0,1:T(8,128)}), f32[4,16,16,128]{3,2,0,1:T(8,128)S(1)}, u32[]{:S(2)}, u32[]{:S(2)}) %all-to-all-start.4) | async-done | bytes 524320 | tf_op jit(solution)/shard_map/all_to_all | solution.py:128
  111.1 3.5 %all-to-all-start.5 = ((bf16[4,16,16,128]{3,2,0,1:T(8,128)(2,1)}), bf16[4,16,16,128]{3,2,0,1:T(8,128)(2,1)S(1)}, u32[]{:S(2)}, u32[]{:S(2)}) async-start(bf16[4,16,16,128]{3,2,0,1:T(8,128)(2,1)} %copy.172), calls=%async_computation.5 | async-start | bytes 524288 | tf_op jit(solution)/shard_map/all_to_all | solution.py:139
  116.4 7.5 %all-to-all-done.5 = bf16[4,16,16,128]{3,2,0,1:T(8,128)(2,1)S(1)} async-done(((bf16[4,16,16,128]{3,2,0,1:T(8,128)(2,1)}), bf16[4,16,16,128]{3,2,0,1:T(8,128)(2,1)S(1)}, u32[]{:S(2)}, u32[]{:S(2)}) %all-to-all-start.5) | async-done | bytes 262176 | tf_op jit(solution)/shard_map/all_to_all | solution.py:139
  124.0 1.8 fusion.71
  129.2 3.6 %all-to-all-start.6 = ((f32[4,16,16,128]{3,2,0,1:T(8,128)}), f32[4,16,16,128]{3,2,0,1:T(8,128)S(1)}, u32[]{:S(2)}, u32[]{:S(2)}) async-start(f32[4,16,16,128]{3,2,0,1:T(8,128)} %copy.179), calls=%async_computation.6 | async-start | bytes 1048576 | tf_op jit(solution)/shard_map/all_to_all | solution.py:128
  132.8 8.5 %slice_bitcast_fusion.1 = (f32[4,1024,256]{1,2,0:T(8,128)}, f32[4,1024,256]{1,2,0:T(8,128)}) fusion(f32[4,2,1024,320]{2,3,1,0:T(8,128)} %copy-done), kind=kLoop, calls=%fused_computation.7 | loop fusion | bytes 16777216 | tf_op jit(solution)/shard_map/squeeze | solution.py:100
  141.3 3.8 %all-to-all-done.6 = f32[4,16,16,128]{3,2,0,1:T(8,128)S(1)} async-done(((f32[4,16,16,128]{3,2,0,1:T(8,128)}), f32[4,16,16,128]{3,2,0,1:T(8,128)S(1)}, u32[]{:S(2)}, u32[]{:S(2)}) %all-to-all-start.6) | async-done | bytes 524320 | tf_op jit(solution)/shard_map/all_to_all | solution.py:128
  147.4 3.5 %all-to-all-start.7 = ((bf16[4,16,16,128]{3,2,0,1:T(8,128)(2,1)}), bf16[4,16,16,128]{3,2,0,1:T(8,128)(2,1)S(1)}, u32[]{:S(2)}, u32[]{:S(2)}) async-start(bf16[4,16,16,128]{3,2,0,1:T(8,128)(2,1)} %copy.184), calls=%async_computation.7 | async-start | bytes 524288 | tf_op jit(solution)/shard_map/all_to_all | solution.py:139
  151.8 8.2 %all-to-all-done.7 = bf16[4,16,16,128]{3,2,0,1:T(8,128)(2,1)S(1)} async-done(((bf16[4,16,16,128]{3,2,0,1:T(8,128)(2,1)}), bf16[4,16,16,128]{3,2,0,1:T(8,128)(2,1)S(1)}, u32[]{:S(2)}, u32[]{:S(2)}) %all-to-all-start.7) | async-done | bytes 262176 | tf_op jit(solution)/shard_map/all_to_all | solution.py:139
  160.1 4.9 %all-to-all-start.9 = ((f32[8,2,16,128]{3,2,1,0:T(8,128)}), f32[8,2,16,128]{3,2,1,0:T(8,128)S(1)}, u32[]{:S(2)}, u32[]{:S(2)}) async-start(f32[8,2,16,128]{3,2,1,0:T(8,128)} %copy.195), calls=%async_computation.9 | async-start | bytes 262144 | tf_op jit(solution)/shard_map/all_to_all | solution.py:63
  165.2 4.4 %fusion.2 = f32[4,1024,128]{1,2,0:T(8,128)S(1)} fusion(f32[4,1024,256]{1,2,0:T(8,128)} %get-tuple-element.17, f32[4,1024,256]{1,2,0:T(8,128)} %get-tuple-element.16, bf16[4,256,64]{1,2,0:T(8,128)(2,1)S(1)} %get-tuple-element.33, bf16[4,256,64]{1,2,0:T(8,128)(2,1)S(1)} %get-tuple-element.32, bf16[4,256,128]{1,2,0:T(8,128)(2,1)S(1)} %copy.188), kind=kOutput, calls=%fused_computation.5 | convolution fusion | flops 546832384 | bytes 11010048 | tf_op jit(solution)/shard_map/qih,qhc->qic/dot_general | solution.py:31
  174.7 5.7 %all-to-all-start.8 = ((f32[8,2,128,128]{3,2,1,0:T(8,128)}), f32[8,2,128,128]{3,2,1,0:T(8,128)S(1)}, u32[]{:S(2)}, u32[]{:S(2)}) async-start(f32[8,2,128,128]{3,2,1,0:T(8,128)} %maximum_bitcast_fusion), calls=%async_computation.8 | async-start | bytes 2097152 | tf_op jit(solution)/shard_map/all_to_all | solution.py:63
  181.0 14.7 %all-to-all-done.8 = f32[8,2,128,128]{3,2,1,0:T(8,128)S(1)} async-done(((f32[8,2,128,128]{3,2,1,0:T(8,128)}), f32[8,2,128,128]{3,2,1,0:T(8,128)S(1)}, u32[]{:S(2)}, u32[]{:S(2)}) %all-to-all-start.8) | async-done | bytes 1048608 | tf_op jit(solution)/shard_map/all_to_all | solution.py:63
  (119 shorter events, 35.4 us)
Async XLA Ops:
  11.9 4.0 %copy-start = (f32[4,2,1024,320]{2,3,1,0:T(8,128)}, f32[4,2,1024,320]{2,3,1,0:T(8,128)S(1)}, u32[]{:S(2)}) copy-start(f32[4,2,1024,320]{2,3,1,0:T(8,128)S(1)} %convolution_bitcast_fusion) | copy-start | bytes 31457284
  17.6 1.6 copy-start.3
  19.2 10.4 %copy-start.14 = (s32[16,256]{1,0:T(8,128)S(1)}, s32[16,256]{1,0:T(8,128)}, u32[]{:S(2)}) copy-start(s32[16,256]{1,0:T(8,128)} %param.10) | copy-start | bytes 49156
  19.2 10.7 %copy-start.15 = (f32[128]{0:T(128)S(1)}, f32[128]{0:T(128)}, u32[]{:S(2)}) copy-start(f32[128]{0:T(128)} %param.9) | copy-start | bytes 1540
  20.0 70.5 %copy-start.10 = (f32[4,256,64]{1,2,0:T(8,128)}, f32[4,256,64]{1,2,0:T(8,128)S(1)}, u32[]{:S(2)}) copy-start(f32[4,256,64]{1,2,0:T(8,128)S(1)} %get-tuple-element.20) | copy-start | bytes 786436
  21.5 28.0 %copy-start.4 = (f32[4,2,256,320]{2,3,1,0:T(8,128)S(1)}, f32[4,2,256,320]{2,3,1,0:T(8,128)}, u32[]{:S(2)}) copy-start(f32[4,2,256,320]{2,3,1,0:T(8,128)} %copy-done.3) | copy-start | bytes 7864324
  21.5 20.4 %all-to-all-start = ((f32[4,16,16,128]{3,2,0,1:T(8,128)}), f32[4,16,16,128]{3,2,0,1:T(8,128)S(1)}, u32[]{:S(2)}, u32[]{:S(2)}) async-start(f32[4,16,16,128]{3,2,0,1:T(8,128)} %copy.143), calls=%async_computation | async-start | bytes 1048576 | tf_op jit(solution)/shard_map/all_to_all | solution.py:128
  46.0 12.7 %all-to-all-start.1 = ((bf16[4,16,16,128]{3,2,0,1:T(8,128)(2,1)}), bf16[4,16,16,128]{3,2,0,1:T(8,128)(2,1)S(1)}, u32[]{:S(2)}, u32[]{:S(2)}) async-start(bf16[4,16,16,128]{3,2,0,1:T(8,128)(2,1)} %copy.148), calls=%async_computation.1 | async-start | bytes 524288 | tf_op jit(solution)/shard_map/all_to_all | solution.py:139
  49.5 11.3 %copy-start.12 = (f32[4,256,64]{1,2,0:T(8,128)S(1)}, f32[4,256,64]{1,2,0:T(8,128)}, u32[]{:S(2)}) copy-start(f32[4,256,64]{1,2,0:T(8,128)} %get-tuple-element.21) | copy-start | bytes 786436
  51.1 9.8 %copy-start.5 = (f32[4,256,256]{1,2,0:T(8,128)S(1)}, f32[4,256,256]{1,2,0:T(8,128)}, u32[]{:S(2)}) copy-start(f32[4,256,256]{1,2,0:T(8,128)} %get-tuple-element.24) | copy-start | bytes 3145732
  51.1 9.8 %copy-start.7 = (f32[4,256,256]{1,2,0:T(8,128)S(1)}, f32[4,256,256]{1,2,0:T(8,128)}, u32[]{:S(2)}) copy-start(f32[4,256,256]{1,2,0:T(8,128)} %get-tuple-element.25) | copy-start | bytes 3145732
  76.6 13.4 %copy-start.8 = (f32[4,256,256]{1,2,0:T(8,128)S(1)}, f32[4,256,256]{1,2,0:T(8,128)}, u32[]{:S(2)}) copy-start(f32[4,256,256]{1,2,0:T(8,128)} %get-tuple-element.25) | copy-start | bytes 3145732
  93.0 15.9 %all-to-all-start.4 = ((f32[4,16,16,128]{3,2,0,1:T(8,128)}), f32[4,16,16,128]{3,2,0,1:T(8,128)S(1)}, u32[]{:S(2)}, u32[]{:S(2)}) async-start(f32[4,16,16,128]{3,2,0,1:T(8,128)} %copy.167), calls=%async_computation.4 | async-start | bytes 1048576 | tf_op jit(solution)/shard_map/all_to_all | solution.py:128
  109.9 14.1 %copy-start.6 = (f32[4,256,256]{1,2,0:T(8,128)S(1)}, f32[4,256,256]{1,2,0:T(8,128)}, u32[]{:S(2)}) copy-start(f32[4,256,256]{1,2,0:T(8,128)} %get-tuple-element.24) | copy-start | bytes 3145732
  111.1 12.7 %all-to-all-start.5 = ((bf16[4,16,16,128]{3,2,0,1:T(8,128)(2,1)}), bf16[4,16,16,128]{3,2,0,1:T(8,128)(2,1)S(1)}, u32[]{:S(2)}, u32[]{:S(2)}) async-start(bf16[4,16,16,128]{3,2,0,1:T(8,128)(2,1)} %copy.172), calls=%async_computation.5 | async-start | bytes 524288 | tf_op jit(solution)/shard_map/all_to_all | solution.py:139
  123.8 2.0 %copy-start.9 = (f32[4,256,256]{1,2,0:T(8,128)S(1)}, f32[4,256,256]{1,2,0:T(8,128)}, u32[]{:S(2)}) copy-start(f32[4,256,256]{1,2,0:T(8,128)} %get-tuple-element.25) | copy-start | bytes 3145732
  123.8 2.0 %copy-start.11 = (f32[4,256,64]{1,2,0:T(8,128)S(1)}, f32[4,256,64]{1,2,0:T(8,128)}, u32[]{:S(2)}) copy-start(f32[4,256,64]{1,2,0:T(8,128)} %copy-done.10) | copy-start | bytes 786436
  123.8 2.0 %copy-start.13 = (f32[4,256,64]{1,2,0:T(8,128)S(1)}, f32[4,256,64]{1,2,0:T(8,128)}, u32[]{:S(2)}) copy-start(f32[4,256,64]{1,2,0:T(8,128)} %get-tuple-element.21) | copy-start | bytes 786436
  129.2 15.9 %all-to-all-start.6 = ((f32[4,16,16,128]{3,2,0,1:T(8,128)}), f32[4,16,16,128]{3,2,0,1:T(8,128)S(1)}, u32[]{:S(2)}, u32[]{:S(2)}) async-start(f32[4,16,16,128]{3,2,0,1:T(8,128)} %copy.179), calls=%async_computation.6 | async-start | bytes 1048576 | tf_op jit(solution)/shard_map/all_to_all | solution.py:128
  147.4 12.7 %all-to-all-start.7 = ((bf16[4,16,16,128]{3,2,0,1:T(8,128)(2,1)}), bf16[4,16,16,128]{3,2,0,1:T(8,128)(2,1)S(1)}, u32[]{:S(2)}, u32[]{:S(2)}) async-start(bf16[4,16,16,128]{3,2,0,1:T(8,128)(2,1)} %copy.184), calls=%async_computation.7 | async-start | bytes 524288 | tf_op jit(solution)/shard_map/all_to_all | solution.py:139
  160.1 14.6 %all-to-all-start.9 = ((f32[8,2,16,128]{3,2,1,0:T(8,128)}), f32[8,2,16,128]{3,2,1,0:T(8,128)S(1)}, u32[]{:S(2)}, u32[]{:S(2)}) async-start(f32[8,2,16,128]{3,2,1,0:T(8,128)} %copy.195), calls=%async_computation.9 | async-start | bytes 262144 | tf_op jit(solution)/shard_map/all_to_all | solution.py:63
  165.2 4.6 %copy-start.1 = (f32[4,1024,256]{1,2,0:T(8,128)S(1)}, f32[4,1024,256]{1,2,0:T(8,128)}, u32[]{:S(2)}) copy-start(f32[4,1024,256]{1,2,0:T(8,128)} %get-tuple-element.16) | copy-start | bytes 12582916
  165.2 5.9 %copy-start.2 = (f32[4,1024,256]{1,2,0:T(8,128)S(1)}, f32[4,1024,256]{1,2,0:T(8,128)}, u32[]{:S(2)}) copy-start(f32[4,1024,256]{1,2,0:T(8,128)} %get-tuple-element.17) | copy-start | bytes 12582916
  174.7 21.1 %all-to-all-start.8 = ((f32[8,2,128,128]{3,2,1,0:T(8,128)}), f32[8,2,128,128]{3,2,1,0:T(8,128)S(1)}, u32[]{:S(2)}, u32[]{:S(2)}) async-start(f32[8,2,128,128]{3,2,1,0:T(8,128)} %maximum_bitcast_fusion), calls=%async_computation.8 | async-start | bytes 2097152 | tf_op jit(solution)/shard_map/all_to_all | solution.py:63

commit v3 on v2

--- a/solution.py
+++ b/solution.py
@@ -89,22 +89,14 @@
     bucket = shared_rows // area_count
     live_mask = jnp.arange(shared_rows) < live_counts[0]
     coupling_live = jnp.where(live_mask[None, :], coupling, jnp.zeros_like(coupling))
-    right = jnp.concatenate([probes, coupling_live], axis=1)
-    applied = jnp.einsum("qrij,jc->qric", inverses, right, preferred_element_type=F32)
-    applied_parts = split_hi_lo(applied)
-    projected = dot_split("ig,qric->qrgc", (coupling_live,), applied_parts)
-    probe_state = jnp.concatenate(
-        [applied[:, 0, :, :probe_width], applied[:, 1, :, :probe_width]], axis=-1
-    )
-    state_map = jnp.concatenate(
-        [applied[:, 0, :, probe_width:], applied[:, 1, :, probe_width:]], axis=-1
-    )
-    reply_start = jnp.concatenate(
-        [projected[:, 0, :, :probe_width], projected[:, 1, :, :probe_width]], axis=-1
-    )
-    reply_map = jnp.concatenate(
-        [projected[:, 0, :, probe_width:], projected[:, 1, :, probe_width:]], axis=-1
-    )
+    applied_probe = jnp.einsum("qrij,jc->qric", inverses, probes, preferred_element_type=F32)
+    applied_map = jnp.einsum("qrij,jc->qric", inverses, coupling_live, preferred_element_type=F32)
+    projected_probe = dot_split("ig,qric->qrgc", (coupling_live,), split_hi_lo(applied_probe))
+    projected_map = dot_split("ig,qric->qrgc", (coupling_live,), split_hi_lo(applied_map))
+    probe_state = jnp.concatenate([applied_probe[:, 0], applied_probe[:, 1]], axis=-1)
+    state_map = jnp.concatenate([applied_map[:, 0], applied_map[:, 1]], axis=-1)
+    reply_start = jnp.concatenate([projected_probe[:, 0], projected_probe[:, 1]], axis=-1)
+    reply_map = jnp.concatenate([projected_map[:, 0], projected_map[:, 1]], axis=-1)
     reply_parts = split_hi_lo(reply_map)
     block_offsets = (
         lax.dynamic_slice_in_dim(area_rows, area_index * bucket, bucket, 1)
@@ -124,10 +116,10 @@
             replies = reply_start
         else:
             replies = reply_start + dot_split("qgh,qhc->qgc", reply_parts, (gathered_block,))
-        parcels = replies.reshape(local_points, area_count, bucket, 2 * probe_width)
+        parcels = replies.reshape(local_points, area_count, bucket, 2 * probe_width).astype(BF16)
         arrived = lax.all_to_all(parcels, "area", split_axis=1, concat_axis=1, tiled=True)
         arrived = arrived.reshape(local_points, area_count * bucket, 2 * probe_width)
-        summed = dot_split("rn,qnc->qrc", (selector,), split_three(arrived))
+        summed = jnp.einsum("rn,qnc->qrc", selector, arrived, preferred_element_type=F32)
         interface_values = divide_rows(summed, shift_re, shift_im, interface_diagonal)
         outgoing = jnp.einsum(
             "rn,qrc->qnc",

time: 198 us -> 203 us (1.025)
  waiting for transfers between devices: 66 us -> 35.5 us
  matrix products: 29.4 us -> 55.2 us
  blocking collectives: 26.7 us -> 35.5 us
  local copies, waits for them, and re-layouts: 31.1 us -> 26.3 us
  starting transfers between devices: 36.4 us -> 40 us
  other arithmetic: 4.73 us -> 7.71 us
    dot_general x1 -> x6, matrix products: 9.26 us -> 31.2 us  [the longest x1 19.1 us: on_device(): jnp.einsum('qrij,jc->qric', inverses, coupling_live, preferred_element_ty...]
    all_to_all x3 -> x2, waiting for transfers between devices: 28.1 us -> 7.99 us  [on_device(): lax.all_to_all(parcels, 'area', split_axis=1, concat_axis=1, tiled=True)]
    all_to_all x3, waiting for transfers between devices: 23.2 us -> 13.7 us  [on_device(): lax.all_to_all(outgoing, 'area', split_axis=1, concat_axis=1, tiled=True)]
    all_to_all x1 -> x2, blocking collectives: 15 us -> 23.6 us  [on_device(): lax.all_to_all(parcels, 'area', split_axis=1, concat_axis=1, tiled=True)]
    all_to_all x3, starting transfers between devices: 10.6 us -> 14.5 us  [on_device(): lax.all_to_all(outgoing, 'area', split_axis=1, concat_axis=1, tiled=True)]
    dot_general x22 -> x12, matrix products: 19.3 us -> 23.1 us  [dot_split(): term = jnp.einsum(spec, left, right, preferred_element_type=F32)]
    unnamed x33 -> x46, local copies, waits for them, and re-layouts: 6.7 us -> 2.88 us
    reshape x7 -> x0, local copies, waits for them, and re-layouts: 3.64 us -> none  [the longest x4 1.83 us: on_device(): arrived.reshape(local_points, area_count * bucket, 2 * probe_width)]
  transfers between devices with their start and end apart: 8 -> 7, of which waited for: 7 -> 5; matrix products, arithmetic and copies ran while one was open for 11% -> 27% of each run, Pallas kernels for 0% -> 0%
where the time goes in v3:
time: 203 us; the launch traced here: 202 us
  matrix products  55.2 us (27%)
  starting transfers between devices  40 us (20%)
  waiting for transfers between devices  35.5 us (17%)
  blocking collectives  35.5 us (17%)
  local copies, waits for them, and re-layouts  26.3 us (13%)
  other arithmetic  7.71 us (4%)
    all_to_all x2, blocking collectives, on_device(): lax.all_to_all(parcels, 'area', split_axis=1, concat_axis=1, tiled=True)  23.6 us
    dot_general x12, matrix products, dot_split(): term = jnp.einsum(spec, left, right, preferred_element_type=F32)  23.1 us
    dot_general x1, matrix products, on_device(): jnp.einsum('qrij,jc->qric', inverses, coupling_live, preferred_element_ty...  19.1 us
    all_to_all x2, starting transfers between devices, on_device(): lax.all_to_all(parcels, 'area', split_axis=1, concat_axis=1, tiled=True)  14.9 us
    all_to_all x3, starting transfers between devices, on_device(): lax.all_to_all(outgoing, 'area', split_axis=1, concat_axis=1, tiled=True)  14.5 us
    all_to_all x2, waiting for transfers between devices, sent_and_summed(): lax.all_to_all(parts, axis, split_axis=0, concat_axis=0, tiled=True)  13.8 us
    all_to_all x3, waiting for transfers between devices, on_device(): lax.all_to_all(outgoing, 'area', split_axis=1, concat_axis=1, tiled=True)  13.7 us
    all_to_all x1, blocking collectives, on_device(): lax.all_to_all(outgoing, 'area', split_axis=1, concat_axis=1, tiled=True)  11.9 us
  transfers between devices with their start and end apart: 7, of which 5 were waited for; matrix products, arithmetic and copies ran while one was open for 27% of the time, Pallas kernels for 0%

profile of v3, /device:TPU:0, one launch (start us, length us, event | category | flops | bytes accessed | tf_op | source)
XLA Modules:
  0.0 202.3 jit_solution(3826316599325434169)
XLA Ops:
  1.6 11.0 %fusion.47 = f32[4,2,1024,64]{2,3,1,0:T(8,128)S(1)} fusion(bf16[4,2,1024,1024]{3,2,1,0:T(8,128)(2,1)} %param.6, bf16[1024,64]{0,1:T(8,128)(2,1)S(1)} %copy-done), kind=kOutput, calls=%fused_computation.94 | convolution fusion | flops 1073741824 | bytes 19005440 | tf_op jit(solution)/shard_map/qrij,jc->qric/dot_general | solution.py:92
  17.9 7.8 %all-to-all-start = ((bf16[4,16,16,128]{3,2,0,1:T(8,128)(2,1)}), bf16[4,16,16,128]{3,2,0,1:T(8,128)(2,1)S(1)}, u32[]{:S(2)}, u32[]{:S(2)}) async-start(bf16[4,16,16,128]{3,2,0,1:T(8,128)(2,1)} %copy.127), calls=%async_computation | async-start | bytes 524288 | tf_op jit(solution)/shard_map/all_to_all | solution.py:120
  25.8 19.1 %convolution_bitcast_fusion = f32[4,2,1024,256]{2,3,1,0:T(8,128)} fusion(bf16[4,2,1024,1024]{3,2,1,0:T(8,128)(2,1)} %param.6, bf16[1024,256]{1,0:T(8,128)(2,1)S(1)} %copy-done.5, pred[256]{0:T(512)(128)(4,1)S(1)} %iota_compare_fusion.1), kind=kOutput, calls=%fused_computation.9 | convolution fusion | flops 4295229440 | bytes 25690368 | tf_op jit(solution)/shard_map/qrij,jc->qric/dot_general | solution.py:93
  45.0 7.3 %fusion.3 = f32[4,2,256,256]{3,2,1,0:T(8,128)S(1)} fusion(f32[4,2,1024,256]{2,3,1,0:T(8,128)} %convolution_bitcast_fusion, bf16[1024,256]{1,0:T(8,128)(2,1)S(1)} %copy-done.5, pred[256]{0:T(512)(128)(4,1)S(1)} %iota_compare_fusion.1), kind=kOutput, calls=%fused_computation.5 | convolution fusion | flops 1082392576 | bytes 11010304 | tf_op jit(solution)/shard_map/ig,qric->qrgc/dot_general | solution.py:31
  53.1 2.6 %add_bitcast_fusion = f32[4,2,256,256]{2,3,1,0:T(8,128)} fusion(f32[4,2,256,256]{3,2,1,0:T(8,128)S(1)} %fusion.3, f32[4,2,1024,256]{2,3,1,0:T(8,128)S(1)} %copy-done.2, bf16[1024,256]{1,0:T(8,128)(2,1)S(1)} %copy-done.5, pred[256]{0:T(512)(128)(4,1)S(1)} %iota_compare_fusion.1), kind=kOutput, calls=%fused_computation.13 | convolution fusion | flops 1076625408 | bytes 13107456 | tf_op jit(solution)/shard_map/ig,qric->qrgc/dot_general | solution.py:31
  57.6 7.2 %all-to-all-start.1 = ((bf16[4,16,16,128]{3,2,0,1:T(8,128)(2,1)}), bf16[4,16,16,128]{3,2,0,1:T(8,128)(2,1)S(1)}, u32[]{:S(2)}, u32[]{:S(2)}) async-start(bf16[4,16,16,128]{3,2,0,1:T(8,128)(2,1)} %copy.131), calls=%async_computation.1 | async-start | bytes 524288 | tf_op jit(solution)/shard_map/all_to_all | solution.py:131
  64.8 3.0 %slice_bitcast_fusion.3 = (f32[4,256,256]{1,2,0:T(8,128)}, f32[4,256,256]{1,2,0:T(8,128)}) fusion(f32[4,2,256,256]{2,3,1,0:T(8,128)} %add_bitcast_fusion), kind=kLoop, calls=%fused_computation.43 | loop fusion | bytes 4194304 | tf_op jit(solution)/shard_map/squeeze | solution.py:99
  68.6 5.4 %all-to-all-done.1 = bf16[4,16,16,128]{3,2,0,1:T(8,128)(2,1)S(1)} async-done(((bf16[4,16,16,128]{3,2,0,1:T(8,128)(2,1)}), bf16[4,16,16,128]{3,2,0,1:T(8,128)(2,1)S(1)}, u32[]{:S(2)}, u32[]{:S(2)}) %all-to-all-start.1) | async-done | bytes 262176 | tf_op jit(solution)/shard_map/all_to_all | solution.py:131
  74.2 2.1 %fusion.60 = f32[4,256,128]{1,2,0:T(8,128)S(1)} fusion(bf16[4,256,64]{2,1,0:T(8,128)(2,1)S(1)} %get-tuple-element.39, bf16[4,256,64]{2,1,0:T(8,128)(2,1)S(1)} %get-tuple-element.38, bf16[4,256,128]{2,1,0:T(8,128)(2,1)S(1)} %bitcast.113, f32[4,256,256]{1,2,0:T(8,128)} %get-tuple-element.19, f32[4,256,256]{1,2,0:T(8,128)} %get-tuple-element.18), kind=kOutput, calls=%fused_computation.112 | convolution fusion | flops 137887744 | bytes 3145728 | tf_op jit(solution)/shard_map/qgh,qhc->qgc/dot_general | solution.py:31
  77.1 11.8 %all_to_all.50 = bf16[4,16,16,128]{3,2,0,1:T(8,128)(2,1)S(1)} all-to-all(bf16[4,16,16,128]{3,2,0,1:T(8,128)(2,1)S(1)} %copy.138), channel_id=1, replica_groups=mesh['quad'=8,'area'=16] {'area'}, dimensions={1} | all-to-all | bytes 524288 | tf_op jit(solution)/shard_map/all_to_all | solution.py:120
  89.7 11.9 %all_to_all.51 = bf16[4,16,16,128]{3,2,0,1:T(8,128)(2,1)S(1)} all-to-all(bf16[4,16,16,128]{3,2,0,1:T(8,128)(2,1)S(1)} %copy.142), channel_id=1, replica_groups=mesh['quad'=8,'area'=16] {'area'}, dimensions={1} | all-to-all | bytes 524288 | tf_op jit(solution)/shard_map/all_to_all | solution.py:131
  103.0 11.8 %all_to_all.52 = bf16[4,16,16,128]{3,2,0,1:T(8,128)(2,1)S(1)} all-to-all(bf16[4,16,16,128]{3,2,0,1:T(8,128)(2,1)S(1)} %copy.149), channel_id=1, replica_groups=mesh['quad'=8,'area'=16] {'area'}, dimensions={1} | all-to-all | bytes 524288 | tf_op jit(solution)/shard_map/all_to_all | solution.py:120
  116.4 3.8 %all-to-all-start.5 = ((bf16[4,16,16,128]{3,2,0,1:T(8,128)(2,1)}), bf16[4,16,16,128]{3,2,0,1:T(8,128)(2,1)S(1)}, u32[]{:S(2)}, u32[]{:S(2)}) async-start(bf16[4,16,16,128]{3,2,0,1:T(8,128)(2,1)} %copy.153), calls=%async_computation.5 | async-start | bytes 524288 | tf_op jit(solution)/shard_map/all_to_all | solution.py:131
  120.1 8.4 %slice_bitcast_fusion.1 = (f32[4,1024,256]{1,2,0:T(8,128)}, f32[4,1024,256]{1,2,0:T(8,128)}) fusion(f32[4,2,1024,256]{2,3,1,0:T(8,128)} %convolution_bitcast_fusion), kind=kLoop, calls=%fused_computation.7 | loop fusion | bytes 16777216 | tf_op jit(solution)/shard_map/squeeze | solution.py:97
  129.5 1.8 fusion.58
  134.3 7.1 %all-to-all-start.6 = ((bf16[4,16,16,128]{3,2,0,1:T(8,128)(2,1)}), bf16[4,16,16,128]{3,2,0,1:T(8,128)(2,1)S(1)}, u32[]{:S(2)}, u32[]{:S(2)}) async-start(bf16[4,16,16,128]{3,2,0,1:T(8,128)(2,1)} %copy.160), calls=%async_computation.6 | async-start | bytes 524288 | tf_op jit(solution)/shard_map/all_to_all | solution.py:120
  142.6 8.0 %all-to-all-done.6 = bf16[4,16,16,128]{3,2,0,1:T(8,128)(2,1)S(1)} async-done(((bf16[4,16,16,128]{3,2,0,1:T(8,128)(2,1)}), bf16[4,16,16,128]{3,2,0,1:T(8,128)(2,1)S(1)}, u32[]{:S(2)}, u32[]{:S(2)}) %all-to-all-start.6) | async-done | bytes 262176 | tf_op jit(solution)/shard_map/all_to_all | solution.py:120
  152.9 3.5 %all-to-all-start.7 = ((bf16[4,16,16,128]{3,2,0,1:T(8,128)(2,1)}), bf16[4,16,16,128]{3,2,0,1:T(8,128)(2,1)S(1)}, u32[]{:S(2)}, u32[]{:S(2)}) async-start(bf16[4,16,16,128]{3,2,0,1:T(8,128)(2,1)} %copy.164), calls=%async_computation.7 | async-start | bytes 524288 | tf_op jit(solution)/shard_map/all_to_all | solution.py:131
  157.4 8.2 %all-to-all-done.7 = bf16[4,16,16,128]{3,2,0,1:T(8,128)(2,1)S(1)} async-done(((bf16[4,16,16,128]{3,2,0,1:T(8,128)(2,1)}), bf16[4,16,16,128]{3,2,0,1:T(8,128)(2,1)S(1)}, u32[]{:S(2)}, u32[]{:S(2)}) %all-to-all-start.7) | async-done | bytes 262176 | tf_op jit(solution)/shard_map/all_to_all | solution.py:131
  165.6 4.9 %all-to-all-start.9 = ((f32[8,2,16,128]{3,2,1,0:T(8,128)}), f32[8,2,16,128]{3,2,1,0:T(8,128)}, u32[]{:S(2)}, u32[]{:S(2)}) async-start(f32[8,2,16,128]{3,2,1,0:T(8,128)} %copy.175), calls=%async_computation.9 | async-start | bytes 262144 | tf_op jit(solution)/shard_map/all_to_all | solution.py:63
  170.7 4.3 %fusion.1 = f32[4,1024,128]{1,2,0:T(8,128)S(1)} fusion(f32[4,1024,256]{1,2,0:T(8,128)} %get-tuple-element.17, f32[4,1024,256]{1,2,0:T(8,128)} %get-tuple-element.16, bf16[4,256,64]{1,2,0:T(8,128)(2,1)S(1)} %get-tuple-element.33, bf16[4,256,64]{1,2,0:T(8,128)(2,1)S(1)} %get-tuple-element.32, bf16[4,256,128]{1,2,0:T(8,128)(2,1)S(1)} %copy.168), kind=kOutput, calls=%fused_computation.4 | convolution fusion | flops 546832384 | bytes 11010048 | tf_op jit(solution)/shard_map/qih,qhc->qic/dot_general | solution.py:31
  180.5 5.7 %all-to-all-start.8 = ((f32[8,2,128,128]{3,2,1,0:T(8,128)}), f32[8,2,128,128]{3,2,1,0:T(8,128)S(1)}, u32[]{:S(2)}, u32[]{:S(2)}) async-start(f32[8,2,128,128]{3,2,1,0:T(8,128)} %maximum_bitcast_fusion), calls=%async_computation.8 | async-start | bytes 2097152 | tf_op jit(solution)/shard_map/all_to_all | solution.py:63
  186.2 1.5 reduce_sum.99
  187.7 13.8 %all-to-all-done.8 = f32[8,2,128,128]{3,2,1,0:T(8,128)S(1)} async-done(((f32[8,2,128,128]{3,2,1,0:T(8,128)}), f32[8,2,128,128]{3,2,1,0:T(8,128)S(1)}, u32[]{:S(2)}, u32[]{:S(2)}) %all-to-all-start.8) | async-done | bytes 1048608 | tf_op jit(solution)/shard_map/all_to_all | solution.py:63
  (122 shorter events, 27.9 us)
Async XLA Ops:
  1.6 11.0 %copy-start.5 = (bf16[1024,256]{1,0:T(8,128)(2,1)S(1)}, bf16[1024,256]{1,0:T(8,128)(2,1)}, u32[]{:S(2)}) copy-start(bf16[1024,256]{1,0:T(8,128)(2,1)} %param.7) | copy-start | bytes 1572868
  17.9 38.1 %all-to-all-start = ((bf16[4,16,16,128]{3,2,0,1:T(8,128)(2,1)}), bf16[4,16,16,128]{3,2,0,1:T(8,128)(2,1)S(1)}, u32[]{:S(2)}, u32[]{:S(2)}) async-start(bf16[4,16,16,128]{3,2,0,1:T(8,128)(2,1)} %copy.127), calls=%async_computation | async-start | bytes 524288 | tf_op jit(solution)/shard_map/all_to_all | solution.py:120
  45.0 11.0 %copy-start.17 = (f32[4]{0:T(128)}, f32[4]{0:T(128)S(1)}, u32[]{:S(2)}) copy-start(f32[4]{0:T(128)S(1)} %get-tuple-element.43) | copy-start | bytes 52
  45.0 8.2 %copy-start.2 = (f32[4,2,1024,256]{2,3,1,0:T(8,128)S(1)}, f32[4,2,1024,256]{2,3,1,0:T(8,128)}, u32[]{:S(2)}) copy-start(f32[4,2,1024,256]{2,3,1,0:T(8,128)} %convolution_bitcast_fusion) | copy-start | bytes 25165828
  53.1 2.7 %copy-start.19 = (s32[16,256]{1,0:T(8,128)S(1)}, s32[16,256]{1,0:T(8,128)}, u32[]{:S(2)}) copy-start(s32[16,256]{1,0:T(8,128)} %param.10) | copy-start | bytes 49156
  53.1 2.9 %copy-start.22 = (f32[128]{0:T(128)S(1)}, f32[128]{0:T(128)}, u32[]{:S(2)}) copy-start(f32[128]{0:T(128)} %param.9) | copy-start | bytes 1540
  57.6 16.4 %all-to-all-start.1 = ((bf16[4,16,16,128]{3,2,0,1:T(8,128)(2,1)}), bf16[4,16,16,128]{3,2,0,1:T(8,128)(2,1)S(1)}, u32[]{:S(2)}, u32[]{:S(2)}) async-start(bf16[4,16,16,128]{3,2,0,1:T(8,128)(2,1)} %copy.131), calls=%async_computation.1 | async-start | bytes 524288 | tf_op jit(solution)/shard_map/all_to_all | solution.py:131
  68.6 33.7 %copy-start.13 = (f32[4,256,64]{1,2,0:T(8,128)}, f32[4,256,64]{1,2,0:T(8,128)S(1)}, u32[]{:S(2)}) copy-start(f32[4,256,64]{1,2,0:T(8,128)S(1)} %get-tuple-element.22) | copy-start | bytes 786436
  74.0 2.3 %copy-start.7 = (f32[4,256,256]{1,2,0:T(8,128)S(1)}, f32[4,256,256]{1,2,0:T(8,128)}, u32[]{:S(2)}) copy-start(f32[4,256,256]{1,2,0:T(8,128)} %get-tuple-element.18) | copy-start | bytes 3145732
  74.0 2.3 %copy-start.10 = (f32[4,256,256]{1,2,0:T(8,128)S(1)}, f32[4,256,256]{1,2,0:T(8,128)}, u32[]{:S(2)}) copy-start(f32[4,256,256]{1,2,0:T(8,128)} %get-tuple-element.19) | copy-start | bytes 3145732
  74.0 2.3 %copy-start.15 = (f32[4,256,64]{1,2,0:T(8,128)S(1)}, f32[4,256,64]{1,2,0:T(8,128)}, u32[]{:S(2)}) copy-start(f32[4,256,64]{1,2,0:T(8,128)} %get-tuple-element.23) | copy-start | bytes 786436
  89.7 12.1 %copy-start.8 = (f32[4,256,256]{1,2,0:T(8,128)S(1)}, f32[4,256,256]{1,2,0:T(8,128)}, u32[]{:S(2)}) copy-start(f32[4,256,256]{1,2,0:T(8,128)} %get-tuple-element.18) | copy-start | bytes 3145732
  89.7 12.1 %copy-start.11 = (f32[4,256,256]{1,2,0:T(8,128)S(1)}, f32[4,256,256]{1,2,0:T(8,128)}, u32[]{:S(2)}) copy-start(f32[4,256,256]{1,2,0:T(8,128)} %get-tuple-element.19) | copy-start | bytes 3145732
  116.4 12.9 %all-to-all-start.5 = ((bf16[4,16,16,128]{3,2,0,1:T(8,128)(2,1)}), bf16[4,16,16,128]{3,2,0,1:T(8,128)(2,1)S(1)}, u32[]{:S(2)}, u32[]{:S(2)}) async-start(bf16[4,16,16,128]{3,2,0,1:T(8,128)(2,1)} %copy.153), calls=%async_computation.5 | async-start | bytes 524288 | tf_op jit(solution)/shard_map/all_to_all | solution.py:131
  120.1 9.3 %copy-start.9 = (f32[4,256,256]{1,2,0:T(8,128)S(1)}, f32[4,256,256]{1,2,0:T(8,128)}, u32[]{:S(2)}) copy-start(f32[4,256,256]{1,2,0:T(8,128)} %get-tuple-element.18) | copy-start | bytes 3145732
  129.3 2.0 copy-start.12
  134.3 16.3 %all-to-all-start.6 = ((bf16[4,16,16,128]{3,2,0,1:T(8,128)(2,1)}), bf16[4,16,16,128]{3,2,0,1:T(8,128)(2,1)S(1)}, u32[]{:S(2)}, u32[]{:S(2)}) async-start(bf16[4,16,16,128]{3,2,0,1:T(8,128)(2,1)} %copy.160), calls=%async_computation.6 | async-start | bytes 524288 | tf_op jit(solution)/shard_map/all_to_all | solution.py:120
  152.9 12.7 %all-to-all-start.7 = ((bf16[4,16,16,128]{3,2,0,1:T(8,128)(2,1)}), bf16[4,16,16,128]{3,2,0,1:T(8,128)(2,1)S(1)}, u32[]{:S(2)}, u32[]{:S(2)}) async-start(bf16[4,16,16,128]{3,2,0,1:T(8,128)(2,1)} %copy.164), calls=%async_computation.7 | async-start | bytes 524288 | tf_op jit(solution)/shard_map/all_to_all | solution.py:131
  165.6 14.9 %all-to-all-start.9 = ((f32[8,2,16,128]{3,2,1,0:T(8,128)}), f32[8,2,16,128]{3,2,1,0:T(8,128)}, u32[]{:S(2)}, u32[]{:S(2)}) async-start(f32[8,2,16,128]{3,2,1,0:T(8,128)} %copy.175), calls=%async_computation.9 | async-start | bytes 262144 | tf_op jit(solution)/shard_map/all_to_all | solution.py:63
  170.7 4.6 %copy-start.3 = (f32[4,1024,256]{1,2,0:T(8,128)S(1)}, f32[4,1024,256]{1,2,0:T(8,128)}, u32[]{:S(2)}) copy-start(f32[4,1024,256]{1,2,0:T(8,128)} %get-tuple-element.16) | copy-start | bytes 12582916
  170.7 5.9 %copy-start.4 = (f32[4,1024,256]{1,2,0:T(8,128)S(1)}, f32[4,1024,256]{1,2,0:T(8,128)}, u32[]{:S(2)}) copy-start(f32[4,1024,256]{1,2,0:T(8,128)} %get-tuple-element.17) | copy-start | bytes 12582916
  170.7 6.1 %copy-start.6 = (f32[4,1024,64]{1,2,0:T(8,128)S(1)}, f32[4,1024,64]{1,2,0:T(8,128)}, u32[]{:S(2)}) copy-start(f32[4,1024,64]{1,2,0:T(8,128)} %get-tuple-element.21) | copy-start | bytes 3145732
  179.4 22.9 %copy-start.1 = (bf16[1024,64]{0,1:T(8,128)(2,1)S(1)}, bf16[1024,64]{0,1:T(8,128)(2,1)}, u32[]{:S(2)}) copy-start(bf16[1024,64]{0,1:T(8,128)(2,1)} %param.8) | copy-start | bytes 393220
  180.5 21.1 %all-to-all-start.8 = ((f32[8,2,128,128]{3,2,1,0:T(8,128)}), f32[8,2,128,128]{3,2,1,0:T(8,128)S(1)}, u32[]{:S(2)}, u32[]{:S(2)}) async-start(f32[8,2,128,128]{3,2,1,0:T(8,128)} %maximum_bitcast_fusion), calls=%async_computation.8 | async-start | bytes 2097152 | tf_op jit(solution)/shard_map/all_to_all | solution.py:63
  (6 other events, 9.0 us)

commit v4 on v2

--- a/solution.py
+++ b/solution.py
@@ -124,10 +124,10 @@
             replies = reply_start
         else:
             replies = reply_start + dot_split("qgh,qhc->qgc", reply_parts, (gathered_block,))
-        parcels = replies.reshape(local_points, area_count, bucket, 2 * probe_width)
+        parcels = replies.reshape(local_points, area_count, bucket, 2 * probe_width).astype(BF16)
         arrived = lax.all_to_all(parcels, "area", split_axis=1, concat_axis=1, tiled=True)
         arrived = arrived.reshape(local_points, area_count * bucket, 2 * probe_width)
-        summed = dot_split("rn,qnc->qrc", (selector,), split_three(arrived))
+        summed = jnp.einsum("rn,qnc->qrc", selector, arrived, preferred_element_type=F32)
         interface_values = divide_rows(summed, shift_re, shift_im, interface_diagonal)
         outgoing = jnp.einsum(
             "rn,qrc->qnc",
@@ -140,8 +140,20 @@
         gathered_rows = returned.reshape(local_points, shared_rows, 2 * probe_width)
         gathered_block = complex_block(gathered_rows)
     states = probe_state + dot_split("qih,qhc->qic", split_hi_lo(state_map), (gathered_block,))
-    inner_moments = sent_and_summed(weight_moments(states, angles), "quad", 1)
-    owned_moments = sent_and_summed(weight_moments(interface_values, angles), "quad", 1)
+    inner_rows = states.shape[1]
+    inner_terms = weight_moments(states, angles)
+    owned_terms = weight_moments(interface_values, angles)
+    inner_parts = jnp.moveaxis(
+        inner_terms.reshape(2, quad_count, inner_rows // quad_count, 2 * probe_width), 1, 0
+    )
+    owned_parts = jnp.moveaxis(
+        owned_terms.reshape(2, quad_count, owned_rows // quad_count, 2 * probe_width), 1, 0
+    )
+    both = jnp.concatenate([inner_parts, owned_parts], axis=2).astype(BF16)
+    summed_both = lax.all_to_all(both, "quad", split_axis=0, concat_axis=0, tiled=True)
+    summed_both = summed_both.astype(F32).sum(axis=0)
+    inner_moments = summed_both[:, : inner_rows // quad_count]
+    owned_moments = summed_both[:, inner_rows // quad_count :]
     return (inner_moments, owned_moments)
 
 

time: 198 us -> 165 us (0.83)
  waiting for transfers between devices: 66 us -> 33.2 us
  blocking collectives: 26.7 us -> 51.1 us
  starting transfers between devices: 36.4 us -> 25.2 us
  local copies, waits for them, and re-layouts: 31.1 us -> 25.9 us
  matrix products: 29.4 us -> 24.6 us
  other arithmetic: 4.73 us -> 2.46 us
    all_to_all x0 -> x1, blocking collectives: none -> 15.8 us  [on_device(): lax.all_to_all(both, 'quad', split_axis=0, concat_axis=0, tiled=True)]
    all_to_all x2 -> x0, waiting for transfers between devices: 14.7 us -> none  [sent_and_summed(): lax.all_to_all(parts, axis, split_axis=0, concat_axis=0, tiled=True)]
    all_to_all x3 -> x2, waiting for transfers between devices: 28.1 us -> 16.3 us  [on_device(): lax.all_to_all(parcels, 'area', split_axis=1, concat_axis=1, tiled=True)]
    all_to_all x2 -> x0, starting transfers between devices: 10.6 us -> none  [sent_and_summed(): lax.all_to_all(parts, axis, split_axis=0, concat_axis=0, tiled=True)]
    all_to_all x1 -> x2, blocking collectives: 15 us -> 23.6 us  [on_device(): lax.all_to_all(parcels, 'area', split_axis=1, concat_axis=1, tiled=True)]
    all_to_all x3, waiting for transfers between devices: 23.2 us -> 16.8 us  [on_device(): lax.all_to_all(outgoing, 'area', split_axis=1, concat_axis=1, tiled=True)]
    dot_general x22 -> x10, matrix products: 19.3 us -> 13.4 us  [dot_split(): term = jnp.einsum(spec, left, right, preferred_element_type=F32)]
    reshape x7 -> x0, local copies, waits for them, and re-layouts: 3.64 us -> none  [the longest x4 1.83 us: on_device(): arrived.reshape(local_points, area_count * bucket, 2 * probe_width)]
  transfers between devices with their start and end apart: 8 -> 5, of which waited for: 7 -> 5; matrix products, arithmetic and copies ran while one was open for 11% -> 8% of each run, Pallas kernels for 0% -> 0%
where the time goes in v4:
time: 165 us; the launch traced here: 164 us
  blocking collectives  51.1 us (31%)
  waiting for transfers between devices  33.2 us (20%)
  local copies, waits for them, and re-layouts  25.9 us (16%)
  starting transfers between devices  25.2 us (15%)
  matrix products  24.6 us (15%)
  other arithmetic  2.46 us (1%)
  between operations  1.86 us (1%)
    all_to_all x2, blocking collectives, on_device(): lax.all_to_all(parcels, 'area', split_axis=1, concat_axis=1, tiled=True)  23.6 us
    all_to_all x3, waiting for transfers between devices, on_device(): lax.all_to_all(outgoing, 'area', split_axis=1, concat_axis=1, tiled=True)  16.8 us
    all_to_all x2, waiting for transfers between devices, on_device(): lax.all_to_all(parcels, 'area', split_axis=1, concat_axis=1, tiled=True)  16.3 us
    all_to_all x1, blocking collectives, on_device(): lax.all_to_all(both, 'quad', split_axis=0, concat_axis=0, tiled=True)  15.8 us
    all_to_all x2, starting transfers between devices, on_device(): lax.all_to_all(parcels, 'area', split_axis=1, concat_axis=1, tiled=True)  14.4 us
    dot_general x10, matrix products, dot_split(): term = jnp.einsum(spec, left, right, preferred_element_type=F32)  13.4 us
    all_to_all x1, blocking collectives, on_device(): lax.all_to_all(outgoing, 'area', split_axis=1, concat_axis=1, tiled=True)  11.8 us
    all_to_all x3, starting transfers between devices, on_device(): lax.all_to_all(outgoing, 'area', split_axis=1, concat_axis=1, tiled=True)  10.8 us
  transfers between devices with their start and end apart: 5, of which 5 were waited for; matrix products, arithmetic and copies ran while one was open for 8% of the time, Pallas kernels for 0%

profile of v4, /device:TPU:0, one launch (start us, length us, event | category | flops | bytes accessed | tf_op | source)
XLA Modules:
  0.0 164.2 jit_solution(4726595059272706158)
XLA Ops:
  2.7 9.3 %convolution_bitcast_fusion = f32[4,2,1024,320]{2,3,1,0:T(8,128)S(1)} fusion(bf16[4,2,1024,1024]{3,2,1,0:T(8,128)(2,1)} %param.6, bf16[1024,256]{0,1:T(8,128)(2,1)S(1)} %broadcast_select_fusion, bf16[1024,64]{0,1:T(8,128)(2,1)} %param.8), kind=kOutput, calls=%fused_computation.9 | convolution fusion | flops 5370019840 | bytes 27918336 | tf_op jit(solution)/shard_map/qrij,jc->qric/dot_general | solution.py:93
  11.9 1.7 %fusion.1 = f32[4,2,320,256]{3,2,1,0:T(8,128)S(1)} fusion(f32[4,2,1024,320]{2,3,1,0:T(8,128)S(1)} %convolution_bitcast_fusion, bf16[1024,256]{0,1:T(8,128)(2,1)S(1)} %broadcast_select_fusion), kind=kOutput, calls=%fused_computation.4 | convolution fusion | flops 1352663040 | bytes 13631488 | tf_op jit(solution)/shard_map/ig,qric->qrgc/dot_general | solution.py:31
  13.6 2.3 %copy-done = f32[4,2,1024,320]{2,3,1,0:T(8,128)} copy-done((f32[4,2,1024,320]{2,3,1,0:T(8,128)}, f32[4,2,1024,320]{2,3,1,0:T(8,128)S(1)}, u32[]{:S(2)}) %copy-start) | copy-done | bytes 10485784
  15.9 1.7 %add_bitcast_fusion = f32[4,2,256,320]{2,3,1,0:T(8,128)S(1)} fusion(f32[4,2,320,256]{3,2,1,0:T(8,128)S(1)} %fusion.1, f32[4,2,1024,320]{2,3,1,0:T(8,128)S(1)} %convolution_bitcast_fusion, bf16[1024,256]{0,1:T(8,128)(2,1)S(1)} %broadcast_select_fusion), kind=kOutput, calls=%fused_computation.10 | convolution fusion | flops 1345454080 | bytes 16252928 | tf_op jit(solution)/shard_map/ig,qric->qrgc/dot_general | solution.py:31
  17.6 1.5 copy-done.3
  20.4 7.8 %all-to-all-start = ((bf16[4,16,16,128]{3,2,0,1:T(8,128)(2,1)}), bf16[4,16,16,128]{3,2,0,1:T(8,128)(2,1)S(1)}, u32[]{:S(2)}, u32[]{:S(2)}) async-start(bf16[4,16,16,128]{3,2,0,1:T(8,128)(2,1)} %copy.135), calls=%async_computation | async-start | bytes 524288 | tf_op jit(solution)/shard_map/all_to_all | solution.py:128
  28.6 8.8 %all-to-all-done = bf16[4,16,16,128]{3,2,0,1:T(8,128)(2,1)S(1)} async-done(((bf16[4,16,16,128]{3,2,0,1:T(8,128)(2,1)}), bf16[4,16,16,128]{3,2,0,1:T(8,128)(2,1)S(1)}, u32[]{:S(2)}, u32[]{:S(2)}) %all-to-all-start) | async-done | bytes 262176 | tf_op jit(solution)/shard_map/all_to_all | solution.py:128
  39.0 3.5 %all-to-all-start.1 = ((bf16[4,16,16,128]{3,2,0,1:T(8,128)(2,1)}), bf16[4,16,16,128]{3,2,0,1:T(8,128)(2,1)S(1)}, u32[]{:S(2)}, u32[]{:S(2)}) async-start(bf16[4,16,16,128]{3,2,0,1:T(8,128)(2,1)} %copy.139), calls=%async_computation.1 | async-start | bytes 524288 | tf_op jit(solution)/shard_map/all_to_all | solution.py:139
  42.6 1.6 slice_bitcast_fusion.3
  44.2 7.5 %all-to-all-done.1 = bf16[4,16,16,128]{3,2,0,1:T(8,128)(2,1)S(1)} async-done(((bf16[4,16,16,128]{3,2,0,1:T(8,128)(2,1)}), bf16[4,16,16,128]{3,2,0,1:T(8,128)(2,1)S(1)}, u32[]{:S(2)}, u32[]{:S(2)}) %all-to-all-start.1) | async-done | bytes 262176 | tf_op jit(solution)/shard_map/all_to_all | solution.py:139
  51.9 2.0 %fusion.48 = f32[4,256,128]{1,2,0:T(8,128)S(1)} fusion(bf16[4,256,64]{2,1,0:T(8,128)(2,1)S(1)} %get-tuple-element.43, bf16[4,256,64]{2,1,0:T(8,128)(2,1)S(1)} %get-tuple-element.42, bf16[4,256,128]{2,1,0:T(8,128)(2,1)S(1)} %bitcast.104, f32[4,256,256]{1,2,0:T(8,128)} %get-tuple-element.25, f32[4,256,256]{1,2,0:T(8,128)} %get-tuple-element.24), kind=kOutput, calls=%fused_computation.100 | convolution fusion | flops 137887744 | bytes 3145728 | tf_op jit(solution)/shard_map/qgh,qhc->qgc/dot_general | solution.py:31
  54.6 11.8 %all_to_all.45 = bf16[4,16,16,128]{3,2,0,1:T(8,128)(2,1)S(1)} all-to-all(bf16[4,16,16,128]{3,2,0,1:T(8,128)(2,1)S(1)} %copy.146), channel_id=1, replica_groups=mesh['quad'=8,'area'=16] {'area'}, dimensions={1} | all-to-all | bytes 524288 | tf_op jit(solution)/shard_map/all_to_all | solution.py:128
  67.2 11.8 %all_to_all.46 = bf16[4,16,16,128]{3,2,0,1:T(8,128)(2,1)S(1)} all-to-all(bf16[4,16,16,128]{3,2,0,1:T(8,128)(2,1)S(1)} %copy.150), channel_id=1, replica_groups=mesh['quad'=8,'area'=16] {'area'}, dimensions={1} | all-to-all | bytes 524288 | tf_op jit(solution)/shard_map/all_to_all | solution.py:139
  80.3 11.8 %all_to_all.47 = bf16[4,16,16,128]{3,2,0,1:T(8,128)(2,1)S(1)} all-to-all(bf16[4,16,16,128]{3,2,0,1:T(8,128)(2,1)S(1)} %copy.157), channel_id=1, replica_groups=mesh['quad'=8,'area'=16] {'area'}, dimensions={1} | all-to-all | bytes 524288 | tf_op jit(solution)/shard_map/all_to_all | solution.py:128
  93.6 3.7 %all-to-all-start.5 = ((bf16[4,16,16,128]{3,2,0,1:T(8,128)(2,1)}), bf16[4,16,16,128]{3,2,0,1:T(8,128)(2,1)S(1)}, u32[]{:S(2)}, u32[]{:S(2)}) async-start(bf16[4,16,16,128]{3,2,0,1:T(8,128)(2,1)} %copy.161), calls=%async_computation.5 | async-start | bytes 524288 | tf_op jit(solution)/shard_map/all_to_all | solution.py:139
  97.3 8.5 %slice_bitcast_fusion.1 = (f32[4,1024,256]{1,2,0:T(8,128)}, f32[4,1024,256]{1,2,0:T(8,128)}) fusion(f32[4,2,1024,320]{2,3,1,0:T(8,128)} %copy-done), kind=kLoop, calls=%fused_computation.7 | loop fusion | bytes 16777216 | tf_op jit(solution)/shard_map/squeeze | solution.py:100
  108.4 6.5 %all-to-all-start.6 = ((bf16[4,16,16,128]{3,2,0,1:T(8,128)(2,1)}), bf16[4,16,16,128]{3,2,0,1:T(8,128)(2,1)S(1)}, u32[]{:S(2)}, u32[]{:S(2)}) async-start(bf16[4,16,16,128]{3,2,0,1:T(8,128)(2,1)} %copy.168), calls=%async_computation.6 | async-start | bytes 524288 | tf_op jit(solution)/shard_map/all_to_all | solution.py:128
  115.0 1.7 %slice_bitcast_fusion.5 = (f32[4,1024,64]{1,2,0:T(8,128)S(1)}, f32[4,1024,64]{1,2,0:T(8,128)S(1)}) fusion(f32[4,2,1024,320]{2,3,1,0:T(8,128)} %copy-done), kind=kLoop, calls=%fused_computation.43 | loop fusion | bytes 4194304 | tf_op jit(solution)/shard_map/squeeze | solution.py:97
  116.7 7.5 %all-to-all-done.6 = bf16[4,16,16,128]{3,2,0,1:T(8,128)(2,1)S(1)} async-done(((bf16[4,16,16,128]{3,2,0,1:T(8,128)(2,1)}), bf16[4,16,16,128]{3,2,0,1:T(8,128)(2,1)S(1)}, u32[]{:S(2)}, u32[]{:S(2)}) %all-to-all-start.6) | async-done | bytes 262176 | tf_op jit(solution)/shard_map/all_to_all | solution.py:128
  125.7 3.5 %all-to-all-start.7 = ((bf16[4,16,16,128]{3,2,0,1:T(8,128)(2,1)}), bf16[4,16,16,128]{3,2,0,1:T(8,128)(2,1)S(1)}, u32[]{:S(2)}, u32[]{:S(2)}) async-start(bf16[4,16,16,128]{3,2,0,1:T(8,128)(2,1)} %copy.172), calls=%async_computation.7 | async-start | bytes 524288 | tf_op jit(solution)/shard_map/all_to_all | solution.py:139
  129.7 8.7 %all-to-all-done.7 = bf16[4,16,16,128]{3,2,0,1:T(8,128)(2,1)S(1)} async-done(((bf16[4,16,16,128]{3,2,0,1:T(8,128)(2,1)}), bf16[4,16,16,128]{3,2,0,1:T(8,128)(2,1)S(1)}, u32[]{:S(2)}, u32[]{:S(2)}) %all-to-all-start.7) | async-done | bytes 262176 | tf_op jit(solution)/shard_map/all_to_all | solution.py:139
  138.6 4.3 %fusion.2 = f32[4,1024,128]{1,2,0:T(8,128)S(1)} fusion(f32[4,1024,256]{1,2,0:T(8,128)} %get-tuple-element.19, f32[4,1024,256]{1,2,0:T(8,128)} %get-tuple-element.18, bf16[4,256,64]{1,2,0:T(8,128)(2,1)S(1)} %get-tuple-element.37, bf16[4,256,64]{1,2,0:T(8,128)(2,1)S(1)} %get-tuple-element.36, bf16[4,256,128]{1,2,0:T(8,128)(2,1)S(1)} %copy.176), kind=kOutput, calls=%fused_computation.5 | convolution fusion | flops 546832384 | bytes 11010048 | tf_op jit(solution)/shard_map/qih,qhc->qic/dot_general | solution.py:31
  144.5 1.3 maximum_add_fusion
  147.1 15.8 %all_to_all.48 = bf16[8,2,144,128]{3,2,1,0:T(8,128)(2,1)S(1)} all-to-all(bf16[8,2,144,128]{3,2,1,0:T(8,128)(2,1)S(1)} %pad_maximum_fusion.2), channel_id=1, replica_groups=mesh['quad'=8,'area'=16] {'quad'}, dimensions={0} | all-to-all | bytes 1179648 | tf_op jit(solution)/shard_map/all_to_all | solution.py:153
  (91 shorter events, 17.7 us)
Async XLA Ops:
  11.9 4.0 %copy-start = (f32[4,2,1024,320]{2,3,1,0:T(8,128)}, f32[4,2,1024,320]{2,3,1,0:T(8,128)S(1)}, u32[]{:S(2)}) copy-start(f32[4,2,1024,320]{2,3,1,0:T(8,128)S(1)} %convolution_bitcast_fusion) | copy-start | bytes 31457284
  17.6 1.6 copy-start.3
  19.1 9.2 %copy-start.7 = (s32[16,256]{1,0:T(8,128)S(1)}, s32[16,256]{1,0:T(8,128)}, u32[]{:S(2)}) copy-start(s32[16,256]{1,0:T(8,128)} %param.10) | copy-start | bytes 49156
  19.1 9.4 %copy-start.8 = (f32[128]{0:T(128)S(1)}, f32[128]{0:T(128)}, u32[]{:S(2)}) copy-start(f32[128]{0:T(128)} %param.9) | copy-start | bytes 1540
  19.5 23.0 %copy-start.4 = (f32[4,2,256,320]{2,3,1,0:T(8,128)S(1)}, f32[4,2,256,320]{2,3,1,0:T(8,128)}, u32[]{:S(2)}) copy-start(f32[4,2,256,320]{2,3,1,0:T(8,128)} %copy-done.3) | copy-start | bytes 7864324
  20.4 17.0 %all-to-all-start = ((bf16[4,16,16,128]{3,2,0,1:T(8,128)(2,1)}), bf16[4,16,16,128]{3,2,0,1:T(8,128)(2,1)S(1)}, u32[]{:S(2)}, u32[]{:S(2)}) async-start(bf16[4,16,16,128]{3,2,0,1:T(8,128)(2,1)} %copy.135), calls=%async_computation | async-start | bytes 524288 | tf_op jit(solution)/shard_map/all_to_all | solution.py:128
  39.0 12.7 %all-to-all-start.1 = ((bf16[4,16,16,128]{3,2,0,1:T(8,128)(2,1)}), bf16[4,16,16,128]{3,2,0,1:T(8,128)(2,1)S(1)}, u32[]{:S(2)}, u32[]{:S(2)}) async-start(bf16[4,16,16,128]{3,2,0,1:T(8,128)(2,1)} %copy.139), calls=%async_computation.1 | async-start | bytes 524288 | tf_op jit(solution)/shard_map/all_to_all | solution.py:139
  44.2 9.7 %copy-start.5 = (f32[4,256,256]{1,2,0:T(8,128)S(1)}, f32[4,256,256]{1,2,0:T(8,128)}, u32[]{:S(2)}) copy-start(f32[4,256,256]{1,2,0:T(8,128)} %get-tuple-element.24) | copy-start | bytes 3145732
  44.2 9.7 %copy-start.6 = (f32[4,256,256]{1,2,0:T(8,128)S(1)}, f32[4,256,256]{1,2,0:T(8,128)}, u32[]{:S(2)}) copy-start(f32[4,256,256]{1,2,0:T(8,128)} %get-tuple-element.25) | copy-start | bytes 3145732
  93.6 12.9 %all-to-all-start.5 = ((bf16[4,16,16,128]{3,2,0,1:T(8,128)(2,1)}), bf16[4,16,16,128]{3,2,0,1:T(8,128)(2,1)S(1)}, u32[]{:S(2)}, u32[]{:S(2)}) async-start(bf16[4,16,16,128]{3,2,0,1:T(8,128)(2,1)} %copy.161), calls=%async_computation.5 | async-start | bytes 524288 | tf_op jit(solution)/shard_map/all_to_all | solution.py:139
  108.4 15.7 %all-to-all-start.6 = ((bf16[4,16,16,128]{3,2,0,1:T(8,128)(2,1)}), bf16[4,16,16,128]{3,2,0,1:T(8,128)(2,1)S(1)}, u32[]{:S(2)}, u32[]{:S(2)}) async-start(bf16[4,16,16,128]{3,2,0,1:T(8,128)(2,1)} %copy.168), calls=%async_computation.6 | async-start | bytes 524288 | tf_op jit(solution)/shard_map/all_to_all | solution.py:128
  125.7 12.7 %all-to-all-start.7 = ((bf16[4,16,16,128]{3,2,0,1:T(8,128)(2,1)}), bf16[4,16,16,128]{3,2,0,1:T(8,128)(2,1)S(1)}, u32[]{:S(2)}, u32[]{:S(2)}) async-start(bf16[4,16,16,128]{3,2,0,1:T(8,128)(2,1)} %copy.172), calls=%async_computation.7 | async-start | bytes 524288 | tf_op jit(solution)/shard_map/all_to_all | solution.py:139
  138.6 4.6 %copy-start.1 = (f32[4,1024,256]{1,2,0:T(8,128)S(1)}, f32[4,1024,256]{1,2,0:T(8,128)}, u32[]{:S(2)}) copy-start(f32[4,1024,256]{1,2,0:T(8,128)} %get-tuple-element.18) | copy-start | bytes 12582916
  138.6 5.9 %copy-start.2 = (f32[4,1024,256]{1,2,0:T(8,128)S(1)}, f32[4,1024,256]{1,2,0:T(8,128)}, u32[]{:S(2)}) copy-start(f32[4,1024,256]{1,2,0:T(8,128)} %get-tuple-element.19) | copy-start | bytes 12582916

commit v5 on v4

--- a/solution.py
+++ b/solution.py
@@ -91,20 +91,20 @@
     coupling_live = jnp.where(live_mask[None, :], coupling, jnp.zeros_like(coupling))
     right = jnp.concatenate([probes, coupling_live], axis=1)
     applied = jnp.einsum("qrij,jc->qric", inverses, right, preferred_element_type=F32)
-    applied_parts = split_hi_lo(applied)
-    projected = dot_split("ig,qric->qrgc", (coupling_live,), applied_parts)
+    projected_probe = dot_split(
+        "ig,qric->qrgc", (coupling_live,), split_hi_lo(applied[..., :probe_width])
+    )
+    projected_map = dot_split(
+        "ig,qric->qrgc", (coupling_live,), split_hi_lo(applied[..., probe_width:])
+    )
     probe_state = jnp.concatenate(
         [applied[:, 0, :, :probe_width], applied[:, 1, :, :probe_width]], axis=-1
     )
     state_map = jnp.concatenate(
         [applied[:, 0, :, probe_width:], applied[:, 1, :, probe_width:]], axis=-1
     )
-    reply_start = jnp.concatenate(
-        [projected[:, 0, :, :probe_width], projected[:, 1, :, :probe_width]], axis=-1
-    )
-    reply_map = jnp.concatenate(
-        [projected[:, 0, :, probe_width:], projected[:, 1, :, probe_width:]], axis=-1
-    )
+    reply_start = jnp.concatenate([projected_probe[:, 0], projected_probe[:, 1]], axis=-1)
+    reply_map = jnp.concatenate([projected_map[:, 0], projected_map[:, 1]], axis=-1)
     reply_parts = split_hi_lo(reply_map)
     block_offsets = (
         lax.dynamic_slice_in_dim(area_rows, area_index * bucket, bucket, 1)

time: 165 us -> 168 us (1.018)
  waiting for transfers between devices: 33.2 us -> 24.8 us
  matrix products: 24.6 us -> 31.9 us
  starting transfers between devices: 25.2 us -> 28.6 us
    all_to_all x2, waiting for transfers between devices: 16.3 us -> 7.49 us  [on_device(): lax.all_to_all(parcels, 'area', split_axis=1, concat_axis=1, tiled=True)]
    dot_general x10 -> x12, matrix products: 13.4 us -> 20.7 us  [dot_split(): term = jnp.einsum(spec, left, right, preferred_element_type=F32)]
    all_to_all x3, starting transfers between devices: 10.8 us -> 14.3 us  [on_device(): lax.all_to_all(outgoing, 'area', split_axis=1, concat_axis=1, tiled=True)]
  transfers between devices with their start and end apart: 5 -> 5, of which waited for: 5 -> 4; matrix products, arithmetic and copies ran while one was open for 8% -> 14% of each run, Pallas kernels for 0% -> 0%
where the time goes in v5:
time: 168 us; the launch traced here: 167 us
  blocking collectives  51.2 us (30%)
  matrix products  31.9 us (19%)
  starting transfers between devices  28.6 us (17%)
  local copies, waits for them, and re-layouts  26 us (15%)
  waiting for transfers between devices  24.8 us (15%)
  other arithmetic  2.45 us (1%)
  between operations  1.91 us (1%)
    all_to_all x2, blocking collectives, on_device(): lax.all_to_all(parcels, 'area', split_axis=1, concat_axis=1, tiled=True)  23.6 us
    dot_general x12, matrix products, dot_split(): term = jnp.einsum(spec, left, right, preferred_element_type=F32)  20.7 us
    all_to_all x3, waiting for transfers between devices, on_device(): lax.all_to_all(outgoing, 'area', split_axis=1, concat_axis=1, tiled=True)  17.3 us
    all_to_all x1, blocking collectives, on_device(): lax.all_to_all(both, 'quad', split_axis=0, concat_axis=0, tiled=True)  15.8 us
    all_to_all x2, starting transfers between devices, on_device(): lax.all_to_all(parcels, 'area', split_axis=1, concat_axis=1, tiled=True)  14.4 us
    all_to_all x3, starting transfers between devices, on_device(): lax.all_to_all(outgoing, 'area', split_axis=1, concat_axis=1, tiled=True)  14.3 us
    all_to_all x1, blocking collectives, on_device(): lax.all_to_all(outgoing, 'area', split_axis=1, concat_axis=1, tiled=True)  11.8 us
    dot_general x1, matrix products, on_device(): jnp.einsum('qrij,jc->qric', inverses, right, preferred_element_type=F32)  9.26 us
  transfers between devices with their start and end apart: 5, of which 4 were waited for; matrix products, arithmetic and copies ran while one was open for 14% of the time, Pallas kernels for 0%

profile of v5, /device:TPU:0, one launch (start us, length us, event | category | flops | bytes accessed | tf_op | source)
XLA Modules:
  0.0 166.8 jit_solution(13780975575666567708)
XLA Ops:
  1.3 1.2 copy.132
  2.7 9.3 %convolution_bitcast_fusion = f32[4,2,1024,320]{2,3,1,0:T(8,128)S(1)} fusion(bf16[4,2,1024,1024]{3,2,1,0:T(8,128)(2,1)} %param.6, bf16[1024,256]{0,1:T(8,128)(2,1)S(1)} %broadcast_select_fusion, bf16[1024,64]{0,1:T(8,128)(2,1)S(1)} %copy-done.8), kind=kOutput, calls=%fused_computation.10 | convolution fusion | flops 5370019840 | bytes 27918336 | tf_op jit(solution)/shard_map/qrij,jc->qric/dot_general | solution.py:93
  12.5 3.5 %copy-done = f32[4,2,1024,320]{2,3,1,0:T(8,128)} copy-done((f32[4,2,1024,320]{2,3,1,0:T(8,128)}, f32[4,2,1024,320]{2,3,1,0:T(8,128)S(1)}, u32[]{:S(2)}) %copy-start) | copy-done | bytes 10485784
  16.4 0.8 copy-done.3
  18.5 7.8 %all-to-all-start = ((bf16[4,16,16,128]{3,2,0,1:T(8,128)(2,1)}), bf16[4,16,16,128]{3,2,0,1:T(8,128)(2,1)S(1)}, u32[]{:S(2)}, u32[]{:S(2)}) async-start(bf16[4,16,16,128]{3,2,0,1:T(8,128)(2,1)} %copy.143), calls=%async_computation | async-start | bytes 524288 | tf_op jit(solution)/shard_map/all_to_all | solution.py:128
  26.4 6.0 %fusion.3 = f32[4,2,256,256]{3,2,1,0:T(8,128)} fusion(f32[4,2,1024,320]{2,3,1,0:T(8,128)} %copy-done, bf16[1024,256]{0,1:T(8,128)(2,1)S(1)} %broadcast_select_fusion), kind=kOutput, calls=%fused_computation.6 | convolution fusion | flops 1082130432 | bytes 11010048 | tf_op jit(solution)/shard_map/ig,qric->qrgc/dot_general | solution.py:31
  32.5 5.3 %add_bitcast_fusion = f32[4,2,256,256]{2,3,1,0:T(8,128)S(1)} fusion(f32[4,2,256,256]{3,2,1,0:T(8,128)} %fusion.3, f32[4,2,1024,320]{2,3,1,0:T(8,128)} %copy-done, bf16[1024,256]{0,1:T(8,128)(2,1)S(1)} %broadcast_select_fusion), kind=kOutput, calls=%fused_computation.14 | convolution fusion | flops 1074266112 | bytes 8912896 | tf_op jit(solution)/shard_map/ig,qric->qrgc/dot_general | solution.py:31
  39.6 7.2 %all-to-all-start.1 = ((bf16[4,16,16,128]{3,2,0,1:T(8,128)(2,1)}), bf16[4,16,16,128]{3,2,0,1:T(8,128)(2,1)S(1)}, u32[]{:S(2)}, u32[]{:S(2)}) async-start(bf16[4,16,16,128]{3,2,0,1:T(8,128)(2,1)} %copy.147), calls=%async_computation.1 | async-start | bytes 524288 | tf_op jit(solution)/shard_map/all_to_all | solution.py:139
  46.9 1.2 slice_bitcast_fusion.3
  48.1 7.9 %all-to-all-done.1 = bf16[4,16,16,128]{3,2,0,1:T(8,128)(2,1)S(1)} async-done(((bf16[4,16,16,128]{3,2,0,1:T(8,128)(2,1)}), bf16[4,16,16,128]{3,2,0,1:T(8,128)(2,1)S(1)}, u32[]{:S(2)}, u32[]{:S(2)}) %all-to-all-start.1) | async-done | bytes 262176 | tf_op jit(solution)/shard_map/all_to_all | solution.py:139
  57.3 11.8 %all_to_all.45 = bf16[4,16,16,128]{3,2,0,1:T(8,128)(2,1)S(1)} all-to-all(bf16[4,16,16,128]{3,2,0,1:T(8,128)(2,1)S(1)} %copy.154), channel_id=1, replica_groups=mesh['quad'=8,'area'=16] {'area'}, dimensions={1} | all-to-all | bytes 524288 | tf_op jit(solution)/shard_map/all_to_all | solution.py:128
  70.0 11.8 %all_to_all.46 = bf16[4,16,16,128]{3,2,0,1:T(8,128)(2,1)S(1)} all-to-all(bf16[4,16,16,128]{3,2,0,1:T(8,128)(2,1)S(1)} %copy.158), channel_id=1, replica_groups=mesh['quad'=8,'area'=16] {'area'}, dimensions={1} | all-to-all | bytes 524288 | tf_op jit(solution)/shard_map/all_to_all | solution.py:139
  83.1 11.8 %all_to_all.47 = bf16[4,16,16,128]{3,2,0,1:T(8,128)(2,1)S(1)} all-to-all(bf16[4,16,16,128]{3,2,0,1:T(8,128)(2,1)S(1)} %copy.165), channel_id=1, replica_groups=mesh['quad'=8,'area'=16] {'area'}, dimensions={1} | all-to-all | bytes 524288 | tf_op jit(solution)/shard_map/all_to_all | solution.py:128
  96.4 3.5 %all-to-all-start.5 = ((bf16[4,16,16,128]{3,2,0,1:T(8,128)(2,1)}), bf16[4,16,16,128]{3,2,0,1:T(8,128)(2,1)S(1)}, u32[]{:S(2)}, u32[]{:S(2)}) async-start(bf16[4,16,16,128]{3,2,0,1:T(8,128)(2,1)} %copy.169), calls=%async_computation.5 | async-start | bytes 524288 | tf_op jit(solution)/shard_map/all_to_all | solution.py:139
  99.9 8.5 %slice_bitcast_fusion.1 = (f32[4,1024,256]{1,2,0:T(8,128)}, f32[4,1024,256]{1,2,0:T(8,128)}) fusion(f32[4,2,1024,320]{2,3,1,0:T(8,128)} %copy-done), kind=kLoop, calls=%fused_computation.8 | loop fusion | bytes 16777216 | tf_op jit(solution)/shard_map/squeeze | solution.py:104
  111.1 6.5 %all-to-all-start.6 = ((bf16[4,16,16,128]{3,2,0,1:T(8,128)(2,1)}), bf16[4,16,16,128]{3,2,0,1:T(8,128)(2,1)S(1)}, u32[]{:S(2)}, u32[]{:S(2)}) async-start(bf16[4,16,16,128]{3,2,0,1:T(8,128)(2,1)} %copy.176), calls=%async_computation.6 | async-start | bytes 524288 | tf_op jit(solution)/shard_map/all_to_all | solution.py:128
  117.6 1.7 %slice_bitcast_fusion.5 = (f32[4,1024,64]{1,2,0:T(8,128)S(1)}, f32[4,1024,64]{1,2,0:T(8,128)S(1)}) fusion(f32[4,2,1024,320]{2,3,1,0:T(8,128)} %copy-done), kind=kLoop, calls=%fused_computation.46 | loop fusion | bytes 4194304 | tf_op jit(solution)/shard_map/squeeze | solution.py:101
  119.3 7.5 %all-to-all-done.6 = bf16[4,16,16,128]{3,2,0,1:T(8,128)(2,1)S(1)} async-done(((bf16[4,16,16,128]{3,2,0,1:T(8,128)(2,1)}), bf16[4,16,16,128]{3,2,0,1:T(8,128)(2,1)S(1)}, u32[]{:S(2)}, u32[]{:S(2)}) %all-to-all-start.6) | async-done | bytes 262176 | tf_op jit(solution)/shard_map/all_to_all | solution.py:128
  128.4 3.5 %all-to-all-start.7 = ((bf16[4,16,16,128]{3,2,0,1:T(8,128)(2,1)}), bf16[4,16,16,128]{3,2,0,1:T(8,128)(2,1)S(1)}, u32[]{:S(2)}, u32[]{:S(2)}) async-start(bf16[4,16,16,128]{3,2,0,1:T(8,128)(2,1)} %copy.180), calls=%async_computation.7 | async-start | bytes 524288 | tf_op jit(solution)/shard_map/all_to_all | solution.py:139
  132.3 8.7 %all-to-all-done.7 = bf16[4,16,16,128]{3,2,0,1:T(8,128)(2,1)S(1)} async-done(((bf16[4,16,16,128]{3,2,0,1:T(8,128)(2,1)}), bf16[4,16,16,128]{3,2,0,1:T(8,128)(2,1)S(1)}, u32[]{:S(2)}, u32[]{:S(2)}) %all-to-all-start.7) | async-done | bytes 262176 | tf_op jit(solution)/shard_map/all_to_all | solution.py:139
  141.3 4.3 %fusion.1 = f32[4,1024,128]{1,2,0:T(8,128)S(1)} fusion(f32[4,1024,256]{1,2,0:T(8,128)} %get-tuple-element.19, f32[4,1024,256]{1,2,0:T(8,128)} %get-tuple-element.18, bf16[4,256,64]{1,2,0:T(8,128)(2,1)S(1)} %get-tuple-element.37, bf16[4,256,64]{1,2,0:T(8,128)(2,1)S(1)} %get-tuple-element.36, bf16[4,256,128]{1,2,0:T(8,128)(2,1)S(1)} %copy.184), kind=kOutput, calls=%fused_computation.5 | convolution fusion | flops 546832384 | bytes 11010048 | tf_op jit(solution)/shard_map/qih,qhc->qic/dot_general | solution.py:31
  145.9 1.3 copy-done.2
  147.2 1.3 maximum_add_fusion
  149.7 15.8 %all_to_all.48 = bf16[8,2,144,128]{3,2,1,0:T(8,128)(2,1)S(1)} all-to-all(bf16[8,2,144,128]{3,2,1,0:T(8,128)(2,1)S(1)} %pad_maximum_fusion.2), channel_id=1, replica_groups=mesh['quad'=8,'area'=16] {'quad'}, dimensions={0} | all-to-all | bytes 1179648 | tf_op jit(solution)/shard_map/all_to_all | solution.py:153
  (93 shorter events, 16.6 us)
Async XLA Ops:
  0.6 2.1 %copy-start.8 = (bf16[1024,64]{0,1:T(8,128)(2,1)S(1)}, bf16[1024,64]{0,1:T(8,128)(2,1)}, u32[]{:S(2)}) copy-start(bf16[1024,64]{0,1:T(8,128)(2,1)} %param.8) | copy-start | bytes 393220
  12.0 4.0 %copy-start = (f32[4,2,1024,320]{2,3,1,0:T(8,128)}, f32[4,2,1024,320]{2,3,1,0:T(8,128)S(1)}, u32[]{:S(2)}) copy-start(f32[4,2,1024,320]{2,3,1,0:T(8,128)S(1)} %convolution_bitcast_fusion) | copy-start | bytes 31457284
  16.4 0.8 copy-start.3
  18.5 19.5 %all-to-all-start = ((bf16[4,16,16,128]{3,2,0,1:T(8,128)(2,1)}), bf16[4,16,16,128]{3,2,0,1:T(8,128)(2,1)S(1)}, u32[]{:S(2)}, u32[]{:S(2)}) async-start(bf16[4,16,16,128]{3,2,0,1:T(8,128)(2,1)} %copy.143), calls=%async_computation | async-start | bytes 524288 | tf_op jit(solution)/shard_map/all_to_all | solution.py:128
  32.5 5.3 %copy-start.6 = (s32[16,256]{1,0:T(8,128)S(1)}, s32[16,256]{1,0:T(8,128)}, u32[]{:S(2)}) copy-start(s32[16,256]{1,0:T(8,128)} %param.10) | copy-start | bytes 49156
  32.5 5.5 %copy-start.7 = (f32[128]{0:T(128)S(1)}, f32[128]{0:T(128)}, u32[]{:S(2)}) copy-start(f32[128]{0:T(128)} %param.9) | copy-start | bytes 1540
  39.6 16.4 %all-to-all-start.1 = ((bf16[4,16,16,128]{3,2,0,1:T(8,128)(2,1)}), bf16[4,16,16,128]{3,2,0,1:T(8,128)(2,1)S(1)}, u32[]{:S(2)}, u32[]{:S(2)}) async-start(bf16[4,16,16,128]{3,2,0,1:T(8,128)(2,1)} %copy.147), calls=%async_computation.1 | async-start | bytes 524288 | tf_op jit(solution)/shard_map/all_to_all | solution.py:139
  46.9 1.2 copy-start.4
  48.1 8.1 %copy-start.5 = (f32[4,256,256]{1,2,0:T(8,128)S(1)}, f32[4,256,256]{1,2,0:T(8,128)}, u32[]{:S(2)}) copy-start(f32[4,256,256]{1,2,0:T(8,128)} %get-tuple-element.23) | copy-start | bytes 3145732
  96.4 12.7 %all-to-all-start.5 = ((bf16[4,16,16,128]{3,2,0,1:T(8,128)(2,1)}), bf16[4,16,16,128]{3,2,0,1:T(8,128)(2,1)S(1)}, u32[]{:S(2)}, u32[]{:S(2)}) async-start(bf16[4,16,16,128]{3,2,0,1:T(8,128)(2,1)} %copy.169), calls=%async_computation.5 | async-start | bytes 524288 | tf_op jit(solution)/shard_map/all_to_all | solution.py:139
  111.1 15.7 %all-to-all-start.6 = ((bf16[4,16,16,128]{3,2,0,1:T(8,128)(2,1)}), bf16[4,16,16,128]{3,2,0,1:T(8,128)(2,1)S(1)}, u32[]{:S(2)}, u32[]{:S(2)}) async-start(bf16[4,16,16,128]{3,2,0,1:T(8,128)(2,1)} %copy.176), calls=%async_computation.6 | async-start | bytes 524288 | tf_op jit(solution)/shard_map/all_to_all | solution.py:128
  128.4 12.7 %all-to-all-start.7 = ((bf16[4,16,16,128]{3,2,0,1:T(8,128)(2,1)}), bf16[4,16,16,128]{3,2,0,1:T(8,128)(2,1)S(1)}, u32[]{:S(2)}, u32[]{:S(2)}) async-start(bf16[4,16,16,128]{3,2,0,1:T(8,128)(2,1)} %copy.180), calls=%async_computation.7 | async-start | bytes 524288 | tf_op jit(solution)/shard_map/all_to_all | solution.py:139
  141.2 4.6 %copy-start.1 = (f32[4,1024,256]{1,2,0:T(8,128)S(1)}, f32[4,1024,256]{1,2,0:T(8,128)}, u32[]{:S(2)}) copy-start(f32[4,1024,256]{1,2,0:T(8,128)} %get-tuple-element.18) | copy-start | bytes 12582916
  141.2 5.9 %copy-start.2 = (f32[4,1024,256]{1,2,0:T(8,128)S(1)}, f32[4,1024,256]{1,2,0:T(8,128)}, u32[]{:S(2)}) copy-start(f32[4,1024,256]{1,2,0:T(8,128)} %get-tuple-element.19) | copy-start | bytes 12582916

commit v6 on v4

--- a/solution.py
+++ b/solution.py
@@ -91,8 +91,9 @@
     coupling_live = jnp.where(live_mask[None, :], coupling, jnp.zeros_like(coupling))
     right = jnp.concatenate([probes, coupling_live], axis=1)
     applied = jnp.einsum("qrij,jc->qric", inverses, right, preferred_element_type=F32)
-    applied_parts = split_hi_lo(applied)
-    projected = dot_split("ig,qric->qrgc", (coupling_live,), applied_parts)
+    projected = jnp.einsum(
+        "ig,qric->qrgc", coupling_live, applied.astype(BF16), preferred_element_type=F32
+    )
     probe_state = jnp.concatenate(
         [applied[:, 0, :, :probe_width], applied[:, 1, :, :probe_width]], axis=-1
     )
@@ -139,7 +140,9 @@
         returned = lax.all_to_all(outgoing, "area", split_axis=1, concat_axis=1, tiled=True)
         gathered_rows = returned.reshape(local_points, shared_rows, 2 * probe_width)
         gathered_block = complex_block(gathered_rows)
-    states = probe_state + dot_split("qih,qhc->qic", split_hi_lo(state_map), (gathered_block,))
+    states = probe_state + jnp.einsum(
+        "qih,qhc->qic", state_map.astype(BF16), gathered_block, preferred_element_type=F32
+    )
     inner_rows = states.shape[1]
     inner_terms = weight_moments(states, angles)
     owned_terms = weight_moments(interface_values, angles)

time: 165 us -> 158 us (0.958)
  local copies, waits for them, and re-layouts: 25.9 us -> 20 us
  starting transfers between devices: 25.2 us -> 22.4 us
  waiting for transfers between devices: 33.2 us -> 35.8 us
    dot_general x10 -> x6, matrix products: 13.4 us -> 5.75 us  [dot_split(): term = jnp.einsum(spec, left, right, preferred_element_type=F32)]
    dot_general x0 -> x2, matrix products: none -> 4.5 us  [the longest x1 2.9 us: on_device(): jnp.einsum('qih,qhc->qic', state_map.astype(BF16), gathered_block, prefer...]
    squeeze x1, local copies, waits for them, and re-layouts: 8.48 us -> 4.19 us  [on_device(): applied[:, 0, :, probe_width:]]
    all_to_all x3, waiting for transfers between devices: 16.8 us -> 20.9 us  [on_device(): lax.all_to_all(outgoing, 'area', split_axis=1, concat_axis=1, tiled=True)]
    unnamed x19 -> x27, local copies, waits for them, and re-layouts: 6.62 us -> 3.54 us
    all_to_all x2, starting transfers between devices: 14.4 us -> 11.6 us  [on_device(): lax.all_to_all(parcels, 'area', split_axis=1, concat_axis=1, tiled=True)]
    dot_general x1, matrix products: 9.26 us -> 11.7 us  [on_device(): jnp.einsum('qrij,jc->qric', inverses, right, preferred_element_type=F32)]
  transfers between devices with their start and end apart: 5 -> 5, of which waited for: 5 -> 5; matrix products, arithmetic and copies ran while one was open for 8% -> 6% of each run, Pallas kernels for 0% -> 0%
where the time goes in v6:
time: 158 us
  blocking collectives  51.1 us (32%)
  waiting for transfers between devices  35.8 us (23%)
  matrix products  23.9 us (15%)
  starting transfers between devices  22.4 us (14%)
  local copies, waits for them, and re-layouts  20 us (13%)
  other arithmetic  2.45 us (2%)
  between operations  1.9 us (1%)
    all_to_all x2, blocking collectives, on_device(): lax.all_to_all(parcels, 'area', split_axis=1, concat_axis=1, tiled=True)  23.6 us
    all_to_all x3, waiting for transfers between devices, on_device(): lax.all_to_all(outgoing, 'area', split_axis=1, concat_axis=1, tiled=True)  20.9 us
    all_to_all x1, blocking collectives, on_device(): lax.all_to_all(both, 'quad', split_axis=0, concat_axis=0, tiled=True)  15.8 us
    all_to_all x2, waiting for transfers between devices, on_device(): lax.all_to_all(parcels, 'area', split_axis=1, concat_axis=1, tiled=True)  14.8 us
    all_to_all x1, blocking collectives, on_device(): lax.all_to_all(outgoing, 'area', split_axis=1, concat_axis=1, tiled=True)  11.8 us
    dot_general x1, matrix products, on_device(): jnp.einsum('qrij,jc->qric', inverses, right, preferred_element_type=F32)  11.7 us
    all_to_all x2, starting transfers between devices, on_device(): lax.all_to_all(parcels, 'area', split_axis=1, concat_axis=1, tiled=True)  11.6 us
    all_to_all x3, starting transfers between devices, on_device(): lax.all_to_all(outgoing, 'area', split_axis=1, concat_axis=1, tiled=True)  10.8 us
  transfers between devices with their start and end apart: 5, of which 5 were waited for; matrix products, arithmetic and copies ran while one was open for 6% of the time, Pallas kernels for 0%

profile of v6, /device:TPU:0, one launch (start us, length us, event | category | flops | bytes accessed | tf_op | source)
XLA Modules:
  0.0 157.5 jit_solution(3336829494175568295)
XLA Ops:
  0.6 1.3 copy.120
  2.7 11.7 %fusion.81 = (bf16[4,2,1024,320]{2,3,1,0:T(8,128)(2,1)S(1)}, f32[4,2,1024,320]{2,3,1,0:T(8,128)}) fusion(bf16[4,2,1024,1024]{3,2,1,0:T(8,128)(2,1)} %param.6, bf16[1024,256]{0,1:T(8,128)(2,1)S(1)} %broadcast_select_fusion, bf16[1024,64]{0,1:T(8,128)(2,1)S(1)} %copy-done.12), kind=kOutput, calls=%fused_computation.135 | convolution fusion | flops 5372641280 | bytes 33161216 | tf_op jit(solution)/shard_map/qrij,jc->qric/dot_general | solution.py:93
  14.4 1.6 %convolution_bitcast_fusion.1 = f32[4,2,256,320]{2,3,1,0:T(8,128)S(1)} fusion(bf16[4,2,1024,320]{2,3,1,0:T(8,128)(2,1)S(1)} %get-tuple-element.46, bf16[1024,256]{0,1:T(8,128)(2,1)S(1)} %broadcast_select_fusion), kind=kOutput, calls=%fused_computation.10 | convolution fusion | flops 1342177280 | bytes 8388608 | tf_op jit(solution)/shard_map/ig,qric->qrgc/dot_general | solution.py:94
  16.8 1.5 copy-done.1
  19.5 8.1 %all-to-all-start = ((bf16[4,16,16,128]{3,2,0,1:T(8,128)(2,1)}), bf16[4,16,16,128]{3,2,0,1:T(8,128)(2,1)S(1)}, u32[]{:S(2)}, u32[]{:S(2)}) async-start(bf16[4,16,16,128]{3,2,0,1:T(8,128)(2,1)} %copy.128), calls=%async_computation | async-start | bytes 524288 | tf_op jit(solution)/shard_map/all_to_all | solution.py:129
  28.0 8.8 %all-to-all-done = bf16[4,16,16,128]{3,2,0,1:T(8,128)(2,1)S(1)} async-done(((bf16[4,16,16,128]{3,2,0,1:T(8,128)(2,1)}), bf16[4,16,16,128]{3,2,0,1:T(8,128)(2,1)S(1)}, u32[]{:S(2)}, u32[]{:S(2)}) %all-to-all-start) | async-done | bytes 262176 | tf_op jit(solution)/shard_map/all_to_all | solution.py:129
  38.3 3.5 %all-to-all-start.1 = ((bf16[4,16,16,128]{3,2,0,1:T(8,128)(2,1)}), bf16[4,16,16,128]{3,2,0,1:T(8,128)(2,1)S(1)}, u32[]{:S(2)}, u32[]{:S(2)}) async-start(bf16[4,16,16,128]{3,2,0,1:T(8,128)(2,1)} %copy.132), calls=%async_computation.1 | async-start | bytes 524288 | tf_op jit(solution)/shard_map/all_to_all | solution.py:140
  41.9 1.6 %slice_bitcast_fusion.3 = (f32[4,256,256]{1,2,0:T(8,128)}, f32[4,256,256]{1,2,0:T(8,128)}) fusion(f32[4,2,256,320]{2,3,1,0:T(8,128)S(1)} %copy-done.2), kind=kLoop, calls=%fused_computation.35 | loop fusion | bytes 4194304 | tf_op jit(solution)/shard_map/squeeze | solution.py:107
  43.5 7.5 %all-to-all-done.1 = bf16[4,16,16,128]{3,2,0,1:T(8,128)(2,1)S(1)} async-done(((bf16[4,16,16,128]{3,2,0,1:T(8,128)(2,1)}), bf16[4,16,16,128]{3,2,0,1:T(8,128)(2,1)S(1)}, u32[]{:S(2)}, u32[]{:S(2)}) %all-to-all-start.1) | async-done | bytes 262176 | tf_op jit(solution)/shard_map/all_to_all | solution.py:140
  51.2 2.1 %fusion.48 = f32[4,256,128]{1,2,0:T(8,128)S(1)} fusion(bf16[4,256,64]{2,1,0:T(8,128)(2,1)S(1)} %get-tuple-element.43, bf16[4,256,64]{2,1,0:T(8,128)(2,1)S(1)} %get-tuple-element.42, bf16[4,256,128]{2,1,0:T(8,128)(2,1)S(1)} %bitcast.104, f32[4,256,256]{1,2,0:T(8,128)} %get-tuple-element.25, f32[4,256,256]{1,2,0:T(8,128)} %get-tuple-element.24), kind=kOutput, calls=%fused_computation.97 | convolution fusion | flops 137887744 | bytes 3145728 | tf_op jit(solution)/shard_map/qgh,qhc->qgc/dot_general | solution.py:31
  54.0 11.8 %all_to_all.45 = bf16[4,16,16,128]{3,2,0,1:T(8,128)(2,1)S(1)} all-to-all(bf16[4,16,16,128]{3,2,0,1:T(8,128)(2,1)S(1)} %copy.139), channel_id=1, replica_groups=mesh['quad'=8,'area'=16] {'area'}, dimensions={1} | all-to-all | bytes 524288 | tf_op jit(solution)/shard_map/all_to_all | solution.py:129
  66.6 11.8 %all_to_all.46 = bf16[4,16,16,128]{3,2,0,1:T(8,128)(2,1)S(1)} all-to-all(bf16[4,16,16,128]{3,2,0,1:T(8,128)(2,1)S(1)} %copy.143), channel_id=1, replica_groups=mesh['quad'=8,'area'=16] {'area'}, dimensions={1} | all-to-all | bytes 524288 | tf_op jit(solution)/shard_map/all_to_all | solution.py:140
  79.7 11.8 %all_to_all.47 = bf16[4,16,16,128]{3,2,0,1:T(8,128)(2,1)S(1)} all-to-all(bf16[4,16,16,128]{3,2,0,1:T(8,128)(2,1)S(1)} %copy.150), channel_id=1, replica_groups=mesh['quad'=8,'area'=16] {'area'}, dimensions={1} | all-to-all | bytes 524288 | tf_op jit(solution)/shard_map/all_to_all | solution.py:129
  93.1 3.7 %all-to-all-start.5 = ((bf16[4,16,16,128]{3,2,0,1:T(8,128)(2,1)}), bf16[4,16,16,128]{3,2,0,1:T(8,128)(2,1)S(1)}, u32[]{:S(2)}, u32[]{:S(2)}) async-start(bf16[4,16,16,128]{3,2,0,1:T(8,128)(2,1)} %copy.154), calls=%async_computation.5 | async-start | bytes 524288 | tf_op jit(solution)/shard_map/all_to_all | solution.py:140
  96.8 4.2 %slice_bitcast_fusion.1 = (bf16[4,1024,256]{1,2,0:T(8,128)(2,1)S(1)}, bf16[4,1024,256]{1,2,0:T(8,128)(2,1)}) fusion(bf16[4,2,1024,320]{2,3,1,0:T(8,128)(2,1)} %copy-done), kind=kLoop, calls=%fused_computation.6 | loop fusion | bytes 8388608 | tf_op jit(solution)/shard_map/squeeze | solution.py:101
  101.0 4.7 %all-to-all-done.5 = bf16[4,16,16,128]{3,2,0,1:T(8,128)(2,1)S(1)} async-done(((bf16[4,16,16,128]{3,2,0,1:T(8,128)(2,1)}), bf16[4,16,16,128]{3,2,0,1:T(8,128)(2,1)S(1)}, u32[]{:S(2)}, u32[]{:S(2)}) %all-to-all-start.5) | async-done | bytes 262176 | tf_op jit(solution)/shard_map/all_to_all | solution.py:140
  106.0 1.8 %fusion.46 = f32[4,256,128]{1,2,0:T(8,128)S(1)} fusion(bf16[4,256,64]{2,1,0:T(8,128)(2,1)S(1)} %get-tuple-element.39, bf16[4,256,64]{2,1,0:T(8,128)(2,1)S(1)} %get-tuple-element.38, bf16[4,256,128]{2,1,0:T(8,128)(2,1)S(1)} %bitcast.101, f32[4,256,256]{1,2,0:T(8,128)} %get-tuple-element.25, f32[4,256,256]{1,2,0:T(8,128)S(1)} %copy-done.3), kind=kOutput, calls=%fused_computation.95 | convolution fusion | flops 137887744 | bytes 3145728 | tf_op jit(solution)/shard_map/qgh,qhc->qgc/dot_general | solution.py:31
  109.2 3.5 %all-to-all-start.6 = ((bf16[4,16,16,128]{3,2,0,1:T(8,128)(2,1)}), bf16[4,16,16,128]{3,2,0,1:T(8,128)(2,1)S(1)}, u32[]{:S(2)}, u32[]{:S(2)}) async-start(bf16[4,16,16,128]{3,2,0,1:T(8,128)(2,1)} %copy.161), calls=%async_computation.6 | async-start | bytes 524288 | tf_op jit(solution)/shard_map/all_to_all | solution.py:129
  112.7 3.1 %slice_bitcast_fusion.5 = (f32[4,1024,64]{1,2,0:T(8,128)}, f32[4,1024,64]{1,2,0:T(8,128)}) fusion(f32[4,2,1024,320]{2,3,1,0:T(8,128)} %get-tuple-element.47), kind=kLoop, calls=%fused_computation.37 | loop fusion | bytes 4194304 | tf_op jit(solution)/shard_map/squeeze | solution.py:98
  115.8 6.0 %all-to-all-done.6 = bf16[4,16,16,128]{3,2,0,1:T(8,128)(2,1)S(1)} async-done(((bf16[4,16,16,128]{3,2,0,1:T(8,128)(2,1)}), bf16[4,16,16,128]{3,2,0,1:T(8,128)(2,1)S(1)}, u32[]{:S(2)}, u32[]{:S(2)}) %all-to-all-start.6) | async-done | bytes 262176 | tf_op jit(solution)/shard_map/all_to_all | solution.py:129
  123.4 3.5 %all-to-all-start.7 = ((bf16[4,16,16,128]{3,2,0,1:T(8,128)(2,1)}), bf16[4,16,16,128]{3,2,0,1:T(8,128)(2,1)S(1)}, u32[]{:S(2)}, u32[]{:S(2)}) async-start(bf16[4,16,16,128]{3,2,0,1:T(8,128)(2,1)} %copy.165), calls=%async_computation.7 | async-start | bytes 524288 | tf_op jit(solution)/shard_map/all_to_all | solution.py:140
  127.4 8.7 %all-to-all-done.7 = bf16[4,16,16,128]{3,2,0,1:T(8,128)(2,1)S(1)} async-done(((bf16[4,16,16,128]{3,2,0,1:T(8,128)(2,1)}), bf16[4,16,16,128]{3,2,0,1:T(8,128)(2,1)S(1)}, u32[]{:S(2)}, u32[]{:S(2)}) %all-to-all-start.7) | async-done | bytes 262176 | tf_op jit(solution)/shard_map/all_to_all | solution.py:140
  136.3 2.9 %maximum_add_fusion = f32[4,1024,128]{1,2,0:T(8,128)S(1)} fusion(f32[4,1024,64]{1,2,0:T(8,128)} %get-tuple-element.19, f32[4,1024,64]{1,2,0:T(8,128)} %get-tuple-element.18, bf16[4,1024,256]{1,2,0:T(8,128)(2,1)} %get-tuple-element.21, bf16[4,1024,256]{1,2,0:T(8,128)(2,1)S(1)} %get-tuple-element.20, bf16[4,256,64]{1,2,0:T(8,128)(2,1)S(1)} %get-tuple-element.37, ...), kind=kOutput, calls=%fused_computation.7 | convolution fusion | flops 547880960 | bytes 8912896 | tf_op jit(solution)/shard_map/qih,qhc->qic/dot_general | solution.py:143
  140.4 15.8 %all_to_all.48 = bf16[8,2,144,128]{3,2,1,0:T(8,128)(2,1)S(1)} all-to-all(bf16[8,2,144,128]{3,2,1,0:T(8,128)(2,1)S(1)} %pad_maximum_fusion.1), channel_id=1, replica_groups=mesh['quad'=8,'area'=16] {'quad'}, dimensions={0} | all-to-all | bytes 1179648 | tf_op jit(solution)/shard_map/all_to_all | solution.py:156
  (97 shorter events, 14.6 us)
Async XLA Ops:
  0.6 2.1 %copy-start.12 = (bf16[1024,64]{0,1:T(8,128)(2,1)S(1)}, bf16[1024,64]{0,1:T(8,128)(2,1)}, u32[]{:S(2)}) copy-start(bf16[1024,64]{0,1:T(8,128)(2,1)} %param.8) | copy-start | bytes 393220
  14.4 2.4 %copy-start = (bf16[4,2,1024,320]{2,3,1,0:T(8,128)(2,1)}, bf16[4,2,1024,320]{2,3,1,0:T(8,128)(2,1)S(1)}, u32[]{:S(2)}) copy-start(bf16[4,2,1024,320]{2,3,1,0:T(8,128)(2,1)S(1)} %get-tuple-element.46) | copy-start | bytes 15728644
  16.8 1.5 copy-start.1
  16.8 10.9 %copy-start.10 = (s32[16,256]{1,0:T(8,128)S(1)}, s32[16,256]{1,0:T(8,128)}, u32[]{:S(2)}) copy-start(s32[16,256]{1,0:T(8,128)} %param.10) | copy-start | bytes 49156
  16.8 11.1 %copy-start.11 = (f32[128]{0:T(128)S(1)}, f32[128]{0:T(128)}, u32[]{:S(2)}) copy-start(f32[128]{0:T(128)} %param.9) | copy-start | bytes 1540
  19.5 22.4 %copy-start.2 = (f32[4,2,256,320]{2,3,1,0:T(8,128)S(1)}, f32[4,2,256,320]{2,3,1,0:T(8,128)}, u32[]{:S(2)}) copy-start(f32[4,2,256,320]{2,3,1,0:T(8,128)} %copy-done.1) | copy-start | bytes 7864324
  19.5 17.3 %all-to-all-start = ((bf16[4,16,16,128]{3,2,0,1:T(8,128)(2,1)}), bf16[4,16,16,128]{3,2,0,1:T(8,128)(2,1)S(1)}, u32[]{:S(2)}, u32[]{:S(2)}) async-start(bf16[4,16,16,128]{3,2,0,1:T(8,128)(2,1)} %copy.128), calls=%async_computation | async-start | bytes 524288 | tf_op jit(solution)/shard_map/all_to_all | solution.py:129
  38.3 12.7 %all-to-all-start.1 = ((bf16[4,16,16,128]{3,2,0,1:T(8,128)(2,1)}), bf16[4,16,16,128]{3,2,0,1:T(8,128)(2,1)S(1)}, u32[]{:S(2)}, u32[]{:S(2)}) async-start(bf16[4,16,16,128]{3,2,0,1:T(8,128)(2,1)} %copy.132), calls=%async_computation.1 | async-start | bytes 524288 | tf_op jit(solution)/shard_map/all_to_all | solution.py:140
  43.5 35.5 %copy-start.6 = (f32[4,256,64]{1,2,0:T(8,128)}, f32[4,256,64]{1,2,0:T(8,128)S(1)}, u32[]{:S(2)}) copy-start(f32[4,256,64]{1,2,0:T(8,128)S(1)} %get-tuple-element.22) | copy-start | bytes 786436
  43.5 35.5 %copy-start.8 = (f32[4,256,64]{1,2,0:T(8,128)}, f32[4,256,64]{1,2,0:T(8,128)S(1)}, u32[]{:S(2)}) copy-start(f32[4,256,64]{1,2,0:T(8,128)S(1)} %get-tuple-element.23) | copy-start | bytes 786436
  51.0 2.3 %copy-start.3 = (f32[4,256,256]{1,2,0:T(8,128)S(1)}, f32[4,256,256]{1,2,0:T(8,128)}, u32[]{:S(2)}) copy-start(f32[4,256,256]{1,2,0:T(8,128)} %get-tuple-element.24) | copy-start | bytes 3145732
  51.0 2.3 %copy-start.4 = (f32[4,256,256]{1,2,0:T(8,128)S(1)}, f32[4,256,256]{1,2,0:T(8,128)}, u32[]{:S(2)}) copy-start(f32[4,256,256]{1,2,0:T(8,128)} %get-tuple-element.25) | copy-start | bytes 3145732
  93.1 12.7 %all-to-all-start.5 = ((bf16[4,16,16,128]{3,2,0,1:T(8,128)(2,1)}), bf16[4,16,16,128]{3,2,0,1:T(8,128)(2,1)S(1)}, u32[]{:S(2)}, u32[]{:S(2)}) async-start(bf16[4,16,16,128]{3,2,0,1:T(8,128)(2,1)} %copy.154), calls=%async_computation.5 | async-start | bytes 524288 | tf_op jit(solution)/shard_map/all_to_all | solution.py:140
  105.8 2.0 %copy-start.5 = (f32[4,256,256]{1,2,0:T(8,128)S(1)}, f32[4,256,256]{1,2,0:T(8,128)}, u32[]{:S(2)}) copy-start(f32[4,256,256]{1,2,0:T(8,128)} %get-tuple-element.25) | copy-start | bytes 3145732
  105.8 2.0 %copy-start.7 = (f32[4,256,64]{1,2,0:T(8,128)S(1)}, f32[4,256,64]{1,2,0:T(8,128)}, u32[]{:S(2)}) copy-start(f32[4,256,64]{1,2,0:T(8,128)} %copy-done.6) | copy-start | bytes 786436
  105.8 2.0 %copy-start.9 = (f32[4,256,64]{1,2,0:T(8,128)S(1)}, f32[4,256,64]{1,2,0:T(8,128)}, u32[]{:S(2)}) copy-start(f32[4,256,64]{1,2,0:T(8,128)} %copy-done.8) | copy-start | bytes 786436
  109.2 12.7 %all-to-all-start.6 = ((bf16[4,16,16,128]{3,2,0,1:T(8,128)(2,1)}), bf16[4,16,16,128]{3,2,0,1:T(8,128)(2,1)S(1)}, u32[]{:S(2)}, u32[]{:S(2)}) async-start(bf16[4,16,16,128]{3,2,0,1:T(8,128)(2,1)} %copy.161), calls=%async_computation.6 | async-start | bytes 524288 | tf_op jit(solution)/shard_map/all_to_all | solution.py:129
  123.4 12.7 %all-to-all-start.7 = ((bf16[4,16,16,128]{3,2,0,1:T(8,128)(2,1)}), bf16[4,16,16,128]{3,2,0,1:T(8,128)(2,1)S(1)}, u32[]{:S(2)}, u32[]{:S(2)}) async-start(bf16[4,16,16,128]{3,2,0,1:T(8,128)(2,1)} %copy.165), calls=%async_computation.7 | async-start | bytes 524288 | tf_op jit(solution)/shard_map/all_to_all | solution.py:140

commit v7 on v6

--- a/solution.py
+++ b/solution.py
@@ -113,6 +113,7 @@
     )
     flat_offsets = block_offsets.reshape(-1)
     selector = (flat_offsets[None, :] == jnp.arange(owned_rows)[:, None]).astype(BF16)
+    selector = selector.reshape(owned_rows, area_count, bucket)
     angle_step = jnp.float32(2.0 * math.pi / (local_points * quad_count))
     point_ids = lax.axis_index("quad") * local_points + jnp.arange(local_points, dtype=jnp.int32)
     angles = (point_ids.astype(jnp.float32) + 0.5) * angle_step
@@ -125,20 +126,22 @@
             replies = reply_start
         else:
             replies = reply_start + dot_split("qgh,qhc->qgc", reply_parts, (gathered_block,))
-        parcels = replies.reshape(local_points, area_count, bucket, 2 * probe_width).astype(BF16)
-        arrived = lax.all_to_all(parcels, "area", split_axis=1, concat_axis=1, tiled=True)
-        arrived = arrived.reshape(local_points, area_count * bucket, 2 * probe_width)
-        summed = jnp.einsum("rn,qnc->qrc", selector, arrived, preferred_element_type=F32)
+        parcels = jnp.moveaxis(
+            replies.reshape(local_points, area_count, bucket, 2 * probe_width), 1, 0
+        ).astype(BF16)
+        arrived = lax.all_to_all(parcels, "area", split_axis=0, concat_axis=0, tiled=True)
+        summed = jnp.einsum("rbs,bqsc->qrc", selector, arrived, preferred_element_type=F32)
         interface_values = divide_rows(summed, shift_re, shift_im, interface_diagonal)
         outgoing = jnp.einsum(
-            "rn,qrc->qnc",
+            "rbs,qrc->bqsc",
             selector,
             interface_values.astype(BF16),
             preferred_element_type=F32,
         ).astype(BF16)
-        outgoing = outgoing.reshape(local_points, area_count, bucket, 2 * probe_width)
-        returned = lax.all_to_all(outgoing, "area", split_axis=1, concat_axis=1, tiled=True)
-        gathered_rows = returned.reshape(local_points, shared_rows, 2 * probe_width)
+        returned = lax.all_to_all(outgoing, "area", split_axis=0, concat_axis=0, tiled=True)
+        gathered_rows = jnp.moveaxis(returned, 0, 1).reshape(
+            local_points, shared_rows, 2 * probe_width
+        )
         gathered_block = complex_block(gathered_rows)
     states = probe_state + jnp.einsum(
         "qih,qhc->qic", state_map.astype(BF16), gathered_block, preferred_element_type=F32
@@ -154,9 +157,8 @@
     )
     both = jnp.concatenate([inner_parts, owned_parts], axis=2).astype(BF16)
     summed_both = lax.all_to_all(both, "quad", split_axis=0, concat_axis=0, tiled=True)
-    summed_both = summed_both.astype(F32).sum(axis=0)
-    inner_moments = summed_both[:, : inner_rows // quad_count]
-    owned_moments = summed_both[:, inner_rows // quad_count :]
+    inner_moments = summed_both[:, :, : inner_rows // quad_count].astype(F32).sum(axis=0)
+    owned_moments = summed_both[:, :, inner_rows // quad_count :].astype(F32).sum(axis=0)
     return (inner_moments, owned_moments)
 
 

time: 158 us -> 158 us (level)
    convert_element_type x10 -> x11, local copies, waits for them, and re-layouts: 1.97 us -> 4.26 us  [the longest x4 2.23 us: on_device(): outgoing = jnp.einsum('rbs,qrc->bqsc', selector, interface_values.astype(...]
    reshape x5 -> x1, local copies, waits for them, and re-layouts: 2.41 us -> 0.14 us  [on_device(): jnp.moveaxis(returned, 0, 1)]
    unnamed x27 -> x29, local copies, waits for them, and re-layouts: 3.54 us -> 3.85 us
  transfers between devices with their start and end apart: 5 -> 5, of which waited for: 5 -> 5; matrix products, arithmetic and copies ran while one was open for 6% -> 7% of each run, Pallas kernels for 0% -> 0%
where the time goes in v7:
time: 158 us; the launch traced here: 157 us
  blocking collectives  51.1 us (32%)
  waiting for transfers between devices  35.1 us (22%)
  matrix products  24.3 us (15%)
  starting transfers between devices  22.4 us (14%)
  local copies, waits for them, and re-layouts  18.9 us (12%)
  other arithmetic  3.72 us (2%)
  between operations  1.87 us (1%)
    all_to_all x2, blocking collectives, on_device(): lax.all_to_all(parcels, 'area', split_axis=0, concat_axis=0, tiled=True)  23.6 us
    all_to_all x3, waiting for transfers between devices, on_device(): lax.all_to_all(outgoing, 'area', split_axis=0, concat_axis=0, tiled=True)  20.3 us
    all_to_all x1, blocking collectives, on_device(): lax.all_to_all(both, 'quad', split_axis=0, concat_axis=0, tiled=True)  15.8 us
    all_to_all x2, waiting for transfers between devices, on_device(): lax.all_to_all(parcels, 'area', split_axis=0, concat_axis=0, tiled=True)  14.8 us
    all_to_all x1, blocking collectives, on_device(): lax.all_to_all(outgoing, 'area', split_axis=0, concat_axis=0, tiled=True)  11.8 us
    dot_general x1, matrix products, on_device(): jnp.einsum('qrij,jc->qric', inverses, right, preferred_element_type=F32)  11.7 us
    all_to_all x2, starting transfers between devices, on_device(): lax.all_to_all(parcels, 'area', split_axis=0, concat_axis=0, tiled=True)  11.6 us
    all_to_all x3, starting transfers between devices, on_device(): lax.all_to_all(outgoing, 'area', split_axis=0, concat_axis=0, tiled=True)  10.8 us
  transfers between devices with their start and end apart: 5, of which 5 were waited for; matrix products, arithmetic and copies ran while one was open for 7% of the time, Pallas kernels for 0%

profile of v7, /device:TPU:0, one launch (start us, length us, event | category | flops | bytes accessed | tf_op | source)
XLA Modules:
  0.0 157.4 jit_solution(11216160183867006485)
XLA Ops:
  0.6 1.3 copy.118
  2.7 11.7 %fusion.78 = (bf16[4,2,1024,320]{2,3,1,0:T(8,128)(2,1)S(1)}, f32[4,2,1024,320]{2,3,1,0:T(8,128)}) fusion(bf16[4,2,1024,1024]{3,2,1,0:T(8,128)(2,1)} %param.6, bf16[1024,256]{0,1:T(8,128)(2,1)S(1)} %broadcast_select_fusion, bf16[1024,64]{0,1:T(8,128)(2,1)S(1)} %copy-done.13), kind=kOutput, calls=%fused_computation.137 | convolution fusion | flops 5372641280 | bytes 33161216 | tf_op jit(solution)/shard_map/qrij,jc->qric/dot_general | solution.py:93
  14.4 1.6 %convolution_bitcast_fusion.1 = f32[4,2,256,320]{2,3,1,0:T(8,128)S(1)} fusion(bf16[4,2,1024,320]{2,3,1,0:T(8,128)(2,1)S(1)} %get-tuple-element.46, bf16[1024,256]{0,1:T(8,128)(2,1)S(1)} %broadcast_select_fusion), kind=kOutput, calls=%fused_computation.10 | convolution fusion | flops 1342177280 | bytes 8388608 | tf_op jit(solution)/shard_map/ig,qric->qrgc/dot_general | solution.py:94
  16.8 1.5 copy-done.1
  19.5 8.1 %all-to-all-start = ((bf16[16,4,16,128]{3,2,1,0:T(8,128)(2,1)}), bf16[16,4,16,128]{3,2,1,0:T(8,128)(2,1)S(1)}, u32[]{:S(2)}, u32[]{:S(2)}) async-start(bf16[16,4,16,128]{3,2,1,0:T(8,128)(2,1)} %copy.126), calls=%async_computation | async-start | bytes 524288 | tf_op jit(solution)/shard_map/all_to_all | solution.py:132
  27.9 8.8 %all-to-all-done = bf16[16,4,16,128]{3,2,1,0:T(8,128)(2,1)S(1)} async-done(((bf16[16,4,16,128]{3,2,1,0:T(8,128)(2,1)}), bf16[16,4,16,128]{3,2,1,0:T(8,128)(2,1)S(1)}, u32[]{:S(2)}, u32[]{:S(2)}) %all-to-all-start) | async-done | bytes 262176 | tf_op jit(solution)/shard_map/all_to_all | solution.py:132
  38.2 3.5 %all-to-all-start.1 = ((bf16[16,4,16,128]{3,2,1,0:T(8,128)(2,1)}), bf16[16,4,16,128]{3,2,1,0:T(8,128)(2,1)S(1)}, u32[]{:S(2)}, u32[]{:S(2)}) async-start(bf16[16,4,16,128]{3,2,1,0:T(8,128)(2,1)} %copy.128), calls=%async_computation.1 | async-start | bytes 524288 | tf_op jit(solution)/shard_map/all_to_all | solution.py:141
  41.8 1.6 %slice_bitcast_fusion.3 = (f32[4,256,256]{1,2,0:T(8,128)}, f32[4,256,256]{1,2,0:T(8,128)}) fusion(f32[4,2,256,320]{2,3,1,0:T(8,128)S(1)} %copy-done.2), kind=kLoop, calls=%fused_computation.34 | loop fusion | bytes 4194304 | tf_op jit(solution)/shard_map/squeeze | solution.py:107
  44.1 6.8 %all-to-all-done.1 = bf16[16,4,16,128]{3,2,1,0:T(8,128)(2,1)S(1)} async-done(((bf16[16,4,16,128]{3,2,1,0:T(8,128)(2,1)}), bf16[16,4,16,128]{3,2,1,0:T(8,128)(2,1)S(1)}, u32[]{:S(2)}, u32[]{:S(2)}) %all-to-all-start.1) | async-done | bytes 262176 | tf_op jit(solution)/shard_map/all_to_all | solution.py:141
  51.1 2.1 %fusion.45 = f32[4,256,128]{1,2,0:T(8,128)S(1)} fusion(bf16[4,256,64]{2,1,0:T(8,128)(2,1)S(1)} %get-tuple-element.43, bf16[4,256,64]{2,1,0:T(8,128)(2,1)S(1)} %get-tuple-element.42, bf16[4,256,128]{2,1,0:T(8,128)(2,1)S(1)} %bitcast.140, f32[4,256,256]{1,2,0:T(8,128)} %get-tuple-element.25, f32[4,256,256]{1,2,0:T(8,128)} %get-tuple-element.24), kind=kOutput, calls=%fused_computation.99 | convolution fusion | flops 137887744 | bytes 3145728 | tf_op jit(solution)/shard_map/qgh,qhc->qgc/dot_general | solution.py:31
  53.9 11.8 %all_to_all.45 = bf16[16,4,16,128]{3,2,1,0:T(8,128)(2,1)S(1)} all-to-all(bf16[16,4,16,128]{3,2,1,0:T(8,128)(2,1)S(1)} %copy.135), channel_id=1, replica_groups=mesh['quad'=8,'area'=16] {'area'}, dimensions={0} | all-to-all | bytes 524288 | tf_op jit(solution)/shard_map/all_to_all | solution.py:132
  66.4 11.8 %all_to_all.46 = bf16[16,4,16,128]{3,2,1,0:T(8,128)(2,1)S(1)} all-to-all(bf16[16,4,16,128]{3,2,1,0:T(8,128)(2,1)S(1)} %copy.137), channel_id=1, replica_groups=mesh['quad'=8,'area'=16] {'area'}, dimensions={0} | all-to-all | bytes 524288 | tf_op jit(solution)/shard_map/all_to_all | solution.py:141
  79.9 11.8 %all_to_all.47 = bf16[16,4,16,128]{3,2,1,0:T(8,128)(2,1)S(1)} all-to-all(bf16[16,4,16,128]{3,2,1,0:T(8,128)(2,1)S(1)} %copy.144), channel_id=1, replica_groups=mesh['quad'=8,'area'=16] {'area'}, dimensions={0} | all-to-all | bytes 524288 | tf_op jit(solution)/shard_map/all_to_all | solution.py:132
  93.1 3.7 %all-to-all-start.5 = ((bf16[16,4,16,128]{3,2,1,0:T(8,128)(2,1)}), bf16[16,4,16,128]{3,2,1,0:T(8,128)(2,1)S(1)}, u32[]{:S(2)}, u32[]{:S(2)}) async-start(bf16[16,4,16,128]{3,2,1,0:T(8,128)(2,1)} %copy.146), calls=%async_computation.5 | async-start | bytes 524288 | tf_op jit(solution)/shard_map/all_to_all | solution.py:141
  96.8 4.2 %slice_bitcast_fusion.1 = (bf16[4,1024,256]{1,2,0:T(8,128)(2,1)S(1)}, bf16[4,1024,256]{1,2,0:T(8,128)(2,1)}) fusion(bf16[4,2,1024,320]{2,3,1,0:T(8,128)(2,1)} %copy-done), kind=kLoop, calls=%fused_computation.6 | loop fusion | bytes 8388608 | tf_op jit(solution)/shard_map/squeeze | solution.py:101
  101.0 4.8 %all-to-all-done.5 = bf16[16,4,16,128]{3,2,1,0:T(8,128)(2,1)S(1)} async-done(((bf16[16,4,16,128]{3,2,1,0:T(8,128)(2,1)}), bf16[16,4,16,128]{3,2,1,0:T(8,128)(2,1)S(1)}, u32[]{:S(2)}, u32[]{:S(2)}) %all-to-all-start.5) | async-done | bytes 262176 | tf_op jit(solution)/shard_map/all_to_all | solution.py:141
  106.0 1.8 %fusion.43 = f32[4,256,128]{1,2,0:T(8,128)S(1)} fusion(bf16[4,256,64]{2,1,0:T(8,128)(2,1)S(1)} %get-tuple-element.39, bf16[4,256,64]{2,1,0:T(8,128)(2,1)S(1)} %get-tuple-element.38, bf16[4,256,128]{2,1,0:T(8,128)(2,1)S(1)} %bitcast.137, f32[4,256,256]{1,2,0:T(8,128)} %get-tuple-element.25, f32[4,256,256]{1,2,0:T(8,128)S(1)} %copy-done.3), kind=kOutput, calls=%fused_computation.97 | convolution fusion | flops 137887744 | bytes 3145728 | tf_op jit(solution)/shard_map/qgh,qhc->qgc/dot_general | solution.py:31
  109.2 3.5 %all-to-all-start.6 = ((bf16[16,4,16,128]{3,2,1,0:T(8,128)(2,1)}), bf16[16,4,16,128]{3,2,1,0:T(8,128)(2,1)S(1)}, u32[]{:S(2)}, u32[]{:S(2)}) async-start(bf16[16,4,16,128]{3,2,1,0:T(8,128)(2,1)} %copy.153), calls=%async_computation.6 | async-start | bytes 524288 | tf_op jit(solution)/shard_map/all_to_all | solution.py:132
  112.7 3.1 %slice_bitcast_fusion.5 = (f32[4,1024,64]{1,2,0:T(8,128)}, f32[4,1024,64]{1,2,0:T(8,128)}) fusion(f32[4,2,1024,320]{2,3,1,0:T(8,128)} %get-tuple-element.47), kind=kLoop, calls=%fused_computation.36 | loop fusion | bytes 4194304 | tf_op jit(solution)/shard_map/squeeze | solution.py:98
  115.9 6.0 %all-to-all-done.6 = bf16[16,4,16,128]{3,2,1,0:T(8,128)(2,1)S(1)} async-done(((bf16[16,4,16,128]{3,2,1,0:T(8,128)(2,1)}), bf16[16,4,16,128]{3,2,1,0:T(8,128)(2,1)S(1)}, u32[]{:S(2)}, u32[]{:S(2)}) %all-to-all-start.6) | async-done | bytes 262176 | tf_op jit(solution)/shard_map/all_to_all | solution.py:132
  123.3 3.5 %all-to-all-start.7 = ((bf16[16,4,16,128]{3,2,1,0:T(8,128)(2,1)}), bf16[16,4,16,128]{3,2,1,0:T(8,128)(2,1)S(1)}, u32[]{:S(2)}, u32[]{:S(2)}) async-start(bf16[16,4,16,128]{3,2,1,0:T(8,128)(2,1)} %copy.155), calls=%async_computation.7 | async-start | bytes 524288 | tf_op jit(solution)/shard_map/all_to_all | solution.py:141
  127.3 8.7 %all-to-all-done.7 = bf16[16,4,16,128]{3,2,1,0:T(8,128)(2,1)S(1)} async-done(((bf16[16,4,16,128]{3,2,1,0:T(8,128)(2,1)}), bf16[16,4,16,128]{3,2,1,0:T(8,128)(2,1)S(1)}, u32[]{:S(2)}, u32[]{:S(2)}) %all-to-all-start.7) | async-done | bytes 262176 | tf_op jit(solution)/shard_map/all_to_all | solution.py:141
  136.2 2.9 %maximum_add_fusion = f32[4,1024,128]{1,2,0:T(8,128)S(1)} fusion(f32[4,1024,64]{1,2,0:T(8,128)} %get-tuple-element.19, f32[4,1024,64]{1,2,0:T(8,128)} %get-tuple-element.18, bf16[4,1024,256]{1,2,0:T(8,128)(2,1)} %get-tuple-element.21, bf16[4,1024,256]{1,2,0:T(8,128)(2,1)S(1)} %get-tuple-element.20, bf16[4,256,64]{1,2,0:T(8,128)(2,1)S(1)} %get-tuple-element.37, ...), kind=kOutput, calls=%fused_computation.7 | convolution fusion | flops 547880960 | bytes 8912896 | tf_op jit(solution)/shard_map/qih,qhc->qic/dot_general | solution.py:146
  140.3 15.8 %all_to_all.48 = bf16[8,2,144,128]{3,2,1,0:T(8,128)(2,1)S(1)} all-to-all(bf16[8,2,144,128]{3,2,1,0:T(8,128)(2,1)S(1)} %pad_maximum_fusion.1), channel_id=1, replica_groups=mesh['quad'=8,'area'=16] {'quad'}, dimensions={0} | all-to-all | bytes 1179648 | tf_op jit(solution)/shard_map/all_to_all | solution.py:159
  (89 shorter events, 15.2 us)
Async XLA Ops:
  0.6 2.1 %copy-start.13 = (bf16[1024,64]{0,1:T(8,128)(2,1)S(1)}, bf16[1024,64]{0,1:T(8,128)(2,1)}, u32[]{:S(2)}) copy-start(bf16[1024,64]{0,1:T(8,128)(2,1)} %param.8) | copy-start | bytes 393220
  14.4 2.4 %copy-start = (bf16[4,2,1024,320]{2,3,1,0:T(8,128)(2,1)}, bf16[4,2,1024,320]{2,3,1,0:T(8,128)(2,1)S(1)}, u32[]{:S(2)}) copy-start(bf16[4,2,1024,320]{2,3,1,0:T(8,128)(2,1)S(1)} %get-tuple-element.46) | copy-start | bytes 15728644
  16.8 1.5 copy-start.1
  16.8 11.0 %copy-start.11 = (s32[16,256]{1,0:T(8,128)S(1)}, s32[16,256]{1,0:T(8,128)}, u32[]{:S(2)}) copy-start(s32[16,256]{1,0:T(8,128)} %param.10) | copy-start | bytes 49156
  16.8 11.1 %copy-start.12 = (f32[128]{0:T(128)S(1)}, f32[128]{0:T(128)}, u32[]{:S(2)}) copy-start(f32[128]{0:T(128)} %param.9) | copy-start | bytes 1540
  19.5 22.3 %copy-start.2 = (f32[4,2,256,320]{2,3,1,0:T(8,128)S(1)}, f32[4,2,256,320]{2,3,1,0:T(8,128)}, u32[]{:S(2)}) copy-start(f32[4,2,256,320]{2,3,1,0:T(8,128)} %copy-done.1) | copy-start | bytes 7864324
  19.5 17.3 %all-to-all-start = ((bf16[16,4,16,128]{3,2,1,0:T(8,128)(2,1)}), bf16[16,4,16,128]{3,2,1,0:T(8,128)(2,1)S(1)}, u32[]{:S(2)}, u32[]{:S(2)}) async-start(bf16[16,4,16,128]{3,2,1,0:T(8,128)(2,1)} %copy.126), calls=%async_computation | async-start | bytes 524288 | tf_op jit(solution)/shard_map/all_to_all | solution.py:132
  38.2 12.7 %all-to-all-start.1 = ((bf16[16,4,16,128]{3,2,1,0:T(8,128)(2,1)}), bf16[16,4,16,128]{3,2,1,0:T(8,128)(2,1)S(1)}, u32[]{:S(2)}, u32[]{:S(2)}) async-start(bf16[16,4,16,128]{3,2,1,0:T(8,128)(2,1)} %copy.128), calls=%async_computation.1 | async-start | bytes 524288 | tf_op jit(solution)/shard_map/all_to_all | solution.py:141
  44.1 34.8 %copy-start.6 = (f32[4,256,64]{1,2,0:T(8,128)}, f32[4,256,64]{1,2,0:T(8,128)S(1)}, u32[]{:S(2)}) copy-start(f32[4,256,64]{1,2,0:T(8,128)S(1)} %get-tuple-element.22) | copy-start | bytes 786436
  50.9 2.3 %copy-start.3 = (f32[4,256,256]{1,2,0:T(8,128)S(1)}, f32[4,256,256]{1,2,0:T(8,128)}, u32[]{:S(2)}) copy-start(f32[4,256,256]{1,2,0:T(8,128)} %get-tuple-element.24) | copy-start | bytes 3145732
  50.9 2.3 %copy-start.4 = (f32[4,256,256]{1,2,0:T(8,128)S(1)}, f32[4,256,256]{1,2,0:T(8,128)}, u32[]{:S(2)}) copy-start(f32[4,256,256]{1,2,0:T(8,128)} %get-tuple-element.25) | copy-start | bytes 3145732
  50.9 2.3 %copy-start.8 = (f32[4,256,64]{1,2,0:T(8,128)S(1)}, f32[4,256,64]{1,2,0:T(8,128)}, u32[]{:S(2)}) copy-start(f32[4,256,64]{1,2,0:T(8,128)} %get-tuple-element.23) | copy-start | bytes 786436
  78.2 1.0 copy-start.9
  93.1 12.7 %all-to-all-start.5 = ((bf16[16,4,16,128]{3,2,1,0:T(8,128)(2,1)}), bf16[16,4,16,128]{3,2,1,0:T(8,128)(2,1)S(1)}, u32[]{:S(2)}, u32[]{:S(2)}) async-start(bf16[16,4,16,128]{3,2,1,0:T(8,128)(2,1)} %copy.146), calls=%async_computation.5 | async-start | bytes 524288 | tf_op jit(solution)/shard_map/all_to_all | solution.py:141
  105.8 2.0 %copy-start.5 = (f32[4,256,256]{1,2,0:T(8,128)S(1)}, f32[4,256,256]{1,2,0:T(8,128)}, u32[]{:S(2)}) copy-start(f32[4,256,256]{1,2,0:T(8,128)} %get-tuple-element.25) | copy-start | bytes 3145732
  105.8 2.0 %copy-start.7 = (f32[4,256,64]{1,2,0:T(8,128)S(1)}, f32[4,256,64]{1,2,0:T(8,128)}, u32[]{:S(2)}) copy-start(f32[4,256,64]{1,2,0:T(8,128)} %copy-done.6) | copy-start | bytes 786436
  105.8 2.0 %copy-start.10 = (f32[4,256,64]{1,2,0:T(8,128)S(1)}, f32[4,256,64]{1,2,0:T(8,128)}, u32[]{:S(2)}) copy-start(f32[4,256,64]{1,2,0:T(8,128)} %get-tuple-element.23) | copy-start | bytes 786436
  109.2 12.7 %all-to-all-start.6 = ((bf16[16,4,16,128]{3,2,1,0:T(8,128)(2,1)}), bf16[16,4,16,128]{3,2,1,0:T(8,128)(2,1)S(1)}, u32[]{:S(2)}, u32[]{:S(2)}) async-start(bf16[16,4,16,128]{3,2,1,0:T(8,128)(2,1)} %copy.153), calls=%async_computation.6 | async-start | bytes 524288 | tf_op jit(solution)/shard_map/all_to_all | solution.py:132
  123.3 12.7 %all-to-all-start.7 = ((bf16[16,4,16,128]{3,2,1,0:T(8,128)(2,1)}), bf16[16,4,16,128]{3,2,1,0:T(8,128)(2,1)S(1)}, u32[]{:S(2)}, u32[]{:S(2)}) async-start(bf16[16,4,16,128]{3,2,1,0:T(8,128)(2,1)} %copy.155), calls=%async_computation.7 | async-start | bytes 524288 | tf_op jit(solution)/shard_map/all_to_all | solution.py:141

commit v8 on v7

--- a/solution.py
+++ b/solution.py
@@ -8,20 +8,6 @@
 ITERS = 4
 F32 = jnp.float32
 BF16 = jnp.bfloat16
-
-
-def split_hi_lo(value):
-    high = value.astype(BF16)
-    low = (value - high.astype(F32)).astype(BF16)
-    return high, low
-
-
-def split_three(value):
-    first = value.astype(BF16)
-    rest = value - first.astype(F32)
-    second = rest.astype(BF16)
-    third = (rest - second.astype(F32)).astype(BF16)
-    return first, second, third
 
 
 def dot_split(spec, left_parts, right_parts):
@@ -91,9 +77,8 @@
     coupling_live = jnp.where(live_mask[None, :], coupling, jnp.zeros_like(coupling))
     right = jnp.concatenate([probes, coupling_live], axis=1)
     applied = jnp.einsum("qrij,jc->qric", inverses, right, preferred_element_type=F32)
-    projected = jnp.einsum(
-        "ig,qric->qrgc", coupling_live, applied.astype(BF16), preferred_element_type=F32
-    )
+    applied = applied.astype(BF16)
+    projected = jnp.einsum("ig,qric->qrgc", coupling_live, applied, preferred_element_type=F32)
     probe_state = jnp.concatenate(
         [applied[:, 0, :, :probe_width], applied[:, 1, :, :probe_width]], axis=-1
     )
@@ -106,7 +91,7 @@
     reply_map = jnp.concatenate(
         [projected[:, 0, :, probe_width:], projected[:, 1, :, probe_width:]], axis=-1
     )
-    reply_parts = split_hi_lo(reply_map)
+    reply_parts = (reply_map.astype(BF16),)
     block_offsets = (
         lax.dynamic_slice_in_dim(area_rows, area_index * bucket, bucket, 1)
         - area_index * owned_rows
@@ -143,8 +128,8 @@
             local_points, shared_rows, 2 * probe_width
         )
         gathered_block = complex_block(gathered_rows)
-    states = probe_state + jnp.einsum(
-        "qih,qhc->qic", state_map.astype(BF16), gathered_block, preferred_element_type=F32
+    states = probe_state.astype(F32) + jnp.einsum(
+        "qih,qhc->qic", state_map, gathered_block, preferred_element_type=F32
     )
     inner_rows = states.shape[1]
     inner_terms = weight_moments(states, angles)

time: 158 us -> 151 us (0.956)
  matrix products: 24.3 us -> 20.4 us
  local copies, waits for them, and re-layouts: 18.9 us -> 16 us
    unnamed x29 -> x15, local copies, waits for them, and re-layouts: 3.85 us -> 1.31 us
    dot_general x1, matrix products: 11.7 us -> 9.26 us  [on_device(): jnp.einsum('qrij,jc->qric', inverses, right, preferred_element_type=F32)]
    dot_general x6 -> x3, matrix products: 5.76 us -> 3.59 us  [dot_split(): term = jnp.einsum(spec, left, right, preferred_element_type=F32)]
where the time goes in v8:
time: 151 us
  blocking collectives  51.1 us (34%)
  waiting for transfers between devices  35.7 us (24%)
  starting transfers between devices  22 us (15%)
  matrix products  20.4 us (14%)
  local copies, waits for them, and re-layouts  16 us (11%)
  other arithmetic  3.72 us (2%)
  between operations  1.78 us (1%)
    all_to_all x2, blocking collectives, on_device(): lax.all_to_all(parcels, 'area', split_axis=0, concat_axis=0, tiled=True)  23.6 us
    all_to_all x3, waiting for transfers between devices, on_device(): lax.all_to_all(outgoing, 'area', split_axis=0, concat_axis=0, tiled=True)  19.9 us
    all_to_all x2, waiting for transfers between devices, on_device(): lax.all_to_all(parcels, 'area', split_axis=0, concat_axis=0, tiled=True)  15.9 us
    all_to_all x1, blocking collectives, on_device(): lax.all_to_all(both, 'quad', split_axis=0, concat_axis=0, tiled=True)  15.8 us
    all_to_all x1, blocking collectives, on_device(): lax.all_to_all(outgoing, 'area', split_axis=0, concat_axis=0, tiled=True)  11.8 us
    all_to_all x2, starting transfers between devices, on_device(): lax.all_to_all(parcels, 'area', split_axis=0, concat_axis=0, tiled=True)  11.4 us
    all_to_all x3, starting transfers between devices, on_device(): lax.all_to_all(outgoing, 'area', split_axis=0, concat_axis=0, tiled=True)  10.6 us
    dot_general x1, matrix products, on_device(): jnp.einsum('qrij,jc->qric', inverses, right, preferred_element_type=F32)  9.26 us
  transfers between devices with their start and end apart: 5, of which 5 were waited for; matrix products, arithmetic and copies ran while one was open for 7% of the time, Pallas kernels for 0%

profile of v8, /device:TPU:0, one launch (start us, length us, event | category | flops | bytes accessed | tf_op | source)
XLA Modules:
  0.0 150.6 jit_solution(4287201174157173002)
XLA Ops:
  0.6 1.3 copy.100
  2.7 9.3 %convert_bitcast_fusion = bf16[4,2,1024,320]{2,3,1,0:T(8,128)(2,1)S(1)} fusion(bf16[4,2,1024,1024]{3,2,1,0:T(8,128)(2,1)} %param.6, bf16[1024,256]{0,1:T(8,128)(2,1)S(1)} %broadcast_select_fusion, bf16[1024,64]{0,1:T(8,128)(2,1)S(1)} %copy-done.6), kind=kOutput, calls=%fused_computation | convolution fusion | flops 5372641280 | bytes 22675456 | tf_op jit(solution)/shard_map/qrij,jc->qric/dot_general | solution.py:79
  12.0 2.8 %fusion.80 = (bf16[4,2,256,320]{2,3,1,0:T(8,128)(2,1)}, f32[4,2,256,320]{2,3,1,0:T(8,128)S(1)}) fusion(bf16[4,2,1024,320]{2,3,1,0:T(8,128)(2,1)S(1)} %convert_bitcast_fusion, bf16[1024,256]{0,1:T(8,128)(2,1)S(1)} %broadcast_select_fusion), kind=kOutput, calls=%fused_computation.138 | convolution fusion | flops 1342832640 | bytes 9699328 | tf_op jit(solution)/shard_map/ig,qric->qrgc/dot_general | solution.py:81
  16.1 7.8 %all-to-all-start = ((bf16[16,4,16,128]{3,2,1,0:T(8,128)(2,1)}), bf16[16,4,16,128]{3,2,1,0:T(8,128)(2,1)S(1)}, u32[]{:S(2)}, u32[]{:S(2)}) async-start(bf16[16,4,16,128]{3,2,1,0:T(8,128)(2,1)} %copy.108), calls=%async_computation | async-start | bytes 524288 | tf_op jit(solution)/shard_map/all_to_all | solution.py:117
  24.2 8.8 %all-to-all-done = bf16[16,4,16,128]{3,2,1,0:T(8,128)(2,1)S(1)} async-done(((bf16[16,4,16,128]{3,2,1,0:T(8,128)(2,1)}), bf16[16,4,16,128]{3,2,1,0:T(8,128)(2,1)S(1)}, u32[]{:S(2)}, u32[]{:S(2)}) %all-to-all-start) | async-done | bytes 262176 | tf_op jit(solution)/shard_map/all_to_all | solution.py:117
  34.5 3.5 %all-to-all-start.1 = ((bf16[16,4,16,128]{3,2,1,0:T(8,128)(2,1)}), bf16[16,4,16,128]{3,2,1,0:T(8,128)(2,1)S(1)}, u32[]{:S(2)}, u32[]{:S(2)}) async-start(bf16[16,4,16,128]{3,2,1,0:T(8,128)(2,1)} %copy.110), calls=%async_computation.1 | async-start | bytes 524288 | tf_op jit(solution)/shard_map/all_to_all | solution.py:126
  38.1 2.1 %slice_bitcast_fusion.3 = (bf16[4,256,256]{1,2,0:T(8,128)(2,1)S(1)}, bf16[4,256,256]{1,2,0:T(8,128)(2,1)}) fusion(bf16[4,2,256,320]{2,3,1,0:T(8,128)(2,1)} %get-tuple-element.46), kind=kLoop, calls=%fused_computation.38 | loop fusion | bytes 2097152 | tf_op jit(solution)/shard_map/squeeze | solution.py:92
  40.1 0.8 slice_bitcast_fusion.7
  41.0 6.2 %all-to-all-done.1 = bf16[16,4,16,128]{3,2,1,0:T(8,128)(2,1)S(1)} async-done(((bf16[16,4,16,128]{3,2,1,0:T(8,128)(2,1)}), bf16[16,4,16,128]{3,2,1,0:T(8,128)(2,1)S(1)}, u32[]{:S(2)}, u32[]{:S(2)}) %all-to-all-start.1) | async-done | bytes 262176 | tf_op jit(solution)/shard_map/all_to_all | solution.py:126
  47.4 1.6 %fusion.6 = bf16[4,256,128]{1,2,0:T(8,128)(2,1)S(1)} fusion(bf16[4,256,64]{2,1,0:T(8,128)(2,1)S(1)} %get-tuple-element.43, bf16[4,256,64]{2,1,0:T(8,128)(2,1)S(1)} %get-tuple-element.42, bf16[4,256,128]{2,1,0:T(8,128)(2,1)S(1)} %bitcast.139, f32[4,256,64]{1,2,0:T(8,128)} %get-tuple-element.23, f32[4,256,64]{1,2,0:T(8,128)} %get-tuple-element.22, ...), kind=kOutput, calls=%fused_computation.12 | convolution fusion | flops 138280960 | bytes 2359296 | tf_op jit(solution)/shard_map/qgh,qhc->qgc/dot_general | solution.py:17
  49.2 11.8 %all_to_all.45 = bf16[16,4,16,128]{3,2,1,0:T(8,128)(2,1)S(1)} all-to-all(bf16[16,4,16,128]{3,2,1,0:T(8,128)(2,1)S(1)} %copy.115), channel_id=1, replica_groups=mesh['quad'=8,'area'=16] {'area'}, dimensions={0} | all-to-all | bytes 524288 | tf_op jit(solution)/shard_map/all_to_all | solution.py:117
  61.8 11.8 %all_to_all.46 = bf16[16,4,16,128]{3,2,1,0:T(8,128)(2,1)S(1)} all-to-all(bf16[16,4,16,128]{3,2,1,0:T(8,128)(2,1)S(1)} %copy.117), channel_id=1, replica_groups=mesh['quad'=8,'area'=16] {'area'}, dimensions={0} | all-to-all | bytes 524288 | tf_op jit(solution)/shard_map/all_to_all | solution.py:126
  74.4 11.8 %all_to_all.47 = bf16[16,4,16,128]{3,2,1,0:T(8,128)(2,1)S(1)} all-to-all(bf16[16,4,16,128]{3,2,1,0:T(8,128)(2,1)S(1)} %copy.122), channel_id=1, replica_groups=mesh['quad'=8,'area'=16] {'area'}, dimensions={0} | all-to-all | bytes 524288 | tf_op jit(solution)/shard_map/all_to_all | solution.py:117
  87.7 3.5 %all-to-all-start.5 = ((bf16[16,4,16,128]{3,2,1,0:T(8,128)(2,1)}), bf16[16,4,16,128]{3,2,1,0:T(8,128)(2,1)S(1)}, u32[]{:S(2)}, u32[]{:S(2)}) async-start(bf16[16,4,16,128]{3,2,1,0:T(8,128)(2,1)} %copy.124), calls=%async_computation.5 | async-start | bytes 524288 | tf_op jit(solution)/shard_map/all_to_all | solution.py:126
  91.2 4.2 %slice_bitcast_fusion.1 = (bf16[4,1024,256]{1,2,0:T(8,128)(2,1)S(1)}, bf16[4,1024,256]{1,2,0:T(8,128)(2,1)}) fusion(bf16[4,2,1024,320]{2,3,1,0:T(8,128)(2,1)} %copy-done), kind=kLoop, calls=%fused_computation.6 | loop fusion | bytes 8388608 | tf_op jit(solution)/shard_map/squeeze | solution.py:86
  95.4 4.9 %all-to-all-done.5 = bf16[16,4,16,128]{3,2,1,0:T(8,128)(2,1)S(1)} async-done(((bf16[16,4,16,128]{3,2,1,0:T(8,128)(2,1)}), bf16[16,4,16,128]{3,2,1,0:T(8,128)(2,1)S(1)}, u32[]{:S(2)}, u32[]{:S(2)}) %all-to-all-start.5) | async-done | bytes 262176 | tf_op jit(solution)/shard_map/all_to_all | solution.py:126
  100.5 1.5 fusion.8
  102.9 3.5 %all-to-all-start.6 = ((bf16[16,4,16,128]{3,2,1,0:T(8,128)(2,1)}), bf16[16,4,16,128]{3,2,1,0:T(8,128)(2,1)S(1)}, u32[]{:S(2)}, u32[]{:S(2)}) async-start(bf16[16,4,16,128]{3,2,1,0:T(8,128)(2,1)} %copy.129), calls=%async_computation.6 | async-start | bytes 524288 | tf_op jit(solution)/shard_map/all_to_all | solution.py:117
  106.5 2.1 %slice_bitcast_fusion.5 = (bf16[4,1024,64]{1,2,0:T(8,128)(2,1)S(1)}, bf16[4,1024,64]{1,2,0:T(8,128)(2,1)}) fusion(bf16[4,2,1024,320]{2,3,1,0:T(8,128)(2,1)} %copy-done), kind=kLoop, calls=%fused_computation.40 | loop fusion | bytes 2097152 | tf_op jit(solution)/shard_map/squeeze | solution.py:83
  108.5 7.1 %all-to-all-done.6 = bf16[16,4,16,128]{3,2,1,0:T(8,128)(2,1)S(1)} async-done(((bf16[16,4,16,128]{3,2,1,0:T(8,128)(2,1)}), bf16[16,4,16,128]{3,2,1,0:T(8,128)(2,1)S(1)}, u32[]{:S(2)}, u32[]{:S(2)}) %all-to-all-start.6) | async-done | bytes 262176 | tf_op jit(solution)/shard_map/all_to_all | solution.py:117
  117.0 3.5 %all-to-all-start.7 = ((bf16[16,4,16,128]{3,2,1,0:T(8,128)(2,1)}), bf16[16,4,16,128]{3,2,1,0:T(8,128)(2,1)S(1)}, u32[]{:S(2)}, u32[]{:S(2)}) async-start(bf16[16,4,16,128]{3,2,1,0:T(8,128)(2,1)} %copy.131), calls=%async_computation.7 | async-start | bytes 524288 | tf_op jit(solution)/shard_map/all_to_all | solution.py:126
  121.0 8.7 %all-to-all-done.7 = bf16[16,4,16,128]{3,2,1,0:T(8,128)(2,1)S(1)} async-done(((bf16[16,4,16,128]{3,2,1,0:T(8,128)(2,1)}), bf16[16,4,16,128]{3,2,1,0:T(8,128)(2,1)S(1)}, u32[]{:S(2)}, u32[]{:S(2)}) %all-to-all-start.7) | async-done | bytes 262176 | tf_op jit(solution)/shard_map/all_to_all | solution.py:126
  129.9 2.4 %convert_add_fusion = f32[4,1024,128]{1,2,0:T(8,128)S(1)} fusion(bf16[4,1024,256]{1,2,0:T(8,128)(2,1)} %get-tuple-element.21, bf16[4,1024,256]{1,2,0:T(8,128)(2,1)S(1)} %get-tuple-element.20, bf16[4,1024,64]{1,2,0:T(8,128)(2,1)} %get-tuple-element.19, bf16[4,1024,64]{1,2,0:T(8,128)(2,1)S(1)} %get-tuple-element.18, ...), kind=kOutput, calls=%fused_computation.7 | convolution fusion | flops 549453824 | bytes 7864320 | tf_op jit(solution)/shard_map/qih,qhc->qic/dot_general | solution.py:131
  133.5 15.8 %all_to_all.48 = bf16[8,2,144,128]{3,2,1,0:T(8,128)(2,1)S(1)} all-to-all(bf16[8,2,144,128]{3,2,1,0:T(8,128)(2,1)S(1)} %pad_maximum_fusion.1), channel_id=1, replica_groups=mesh['quad'=8,'area'=16] {'quad'}, dimensions={0} | all-to-all | bytes 1179648 | tf_op jit(solution)/shard_map/all_to_all | solution.py:144
  (72 shorter events, 12.0 us)
Async XLA Ops:
  0.6 2.1 %copy-start.6 = (bf16[1024,64]{0,1:T(8,128)(2,1)S(1)}, bf16[1024,64]{0,1:T(8,128)(2,1)}, u32[]{:S(2)}) copy-start(bf16[1024,64]{0,1:T(8,128)(2,1)} %param.8) | copy-start | bytes 393220
  12.0 2.8 %copy-start = (bf16[4,2,1024,320]{2,3,1,0:T(8,128)(2,1)}, bf16[4,2,1024,320]{2,3,1,0:T(8,128)(2,1)S(1)}, u32[]{:S(2)}) copy-start(bf16[4,2,1024,320]{2,3,1,0:T(8,128)(2,1)S(1)} %convert_bitcast_fusion) | copy-start | bytes 15728644
  14.8 9.3 %copy-start.4 = (s32[16,256]{1,0:T(8,128)S(1)}, s32[16,256]{1,0:T(8,128)}, u32[]{:S(2)}) copy-start(s32[16,256]{1,0:T(8,128)} %param.10) | copy-start | bytes 49156
  14.8 9.4 %copy-start.5 = (f32[128]{0:T(128)S(1)}, f32[128]{0:T(128)}, u32[]{:S(2)}) copy-start(f32[128]{0:T(128)} %param.9) | copy-start | bytes 1540
  16.1 17.0 %all-to-all-start = ((bf16[16,4,16,128]{3,2,1,0:T(8,128)(2,1)}), bf16[16,4,16,128]{3,2,1,0:T(8,128)(2,1)S(1)}, u32[]{:S(2)}, u32[]{:S(2)}) async-start(bf16[16,4,16,128]{3,2,1,0:T(8,128)(2,1)} %copy.108), calls=%async_computation | async-start | bytes 524288 | tf_op jit(solution)/shard_map/all_to_all | solution.py:117
  34.5 12.7 %all-to-all-start.1 = ((bf16[16,4,16,128]{3,2,1,0:T(8,128)(2,1)}), bf16[16,4,16,128]{3,2,1,0:T(8,128)(2,1)S(1)}, u32[]{:S(2)}, u32[]{:S(2)}) async-start(bf16[16,4,16,128]{3,2,1,0:T(8,128)(2,1)} %copy.110), calls=%async_computation.1 | async-start | bytes 524288 | tf_op jit(solution)/shard_map/all_to_all | solution.py:126
  61.3 12.4 %copy-start.1 = (bf16[4,256,256]{1,2,0:T(8,128)(2,1)S(1)}, bf16[4,256,256]{1,2,0:T(8,128)(2,1)}, u32[]{:S(2)}) copy-start(bf16[4,256,256]{1,2,0:T(8,128)(2,1)} %get-tuple-element.27) | copy-start | bytes 1572868
  61.3 12.4 %copy-start.2 = (f32[4,256,64]{1,2,0:T(8,128)S(1)}, f32[4,256,64]{1,2,0:T(8,128)}, u32[]{:S(2)}) copy-start(f32[4,256,64]{1,2,0:T(8,128)} %get-tuple-element.22) | copy-start | bytes 786436
  61.4 12.4 %copy-start.3 = (f32[4,256,64]{1,2,0:T(8,128)S(1)}, f32[4,256,64]{1,2,0:T(8,128)}, u32[]{:S(2)}) copy-start(f32[4,256,64]{1,2,0:T(8,128)} %get-tuple-element.23) | copy-start | bytes 786436
  87.7 12.7 %all-to-all-start.5 = ((bf16[16,4,16,128]{3,2,1,0:T(8,128)(2,1)}), bf16[16,4,16,128]{3,2,1,0:T(8,128)(2,1)S(1)}, u32[]{:S(2)}, u32[]{:S(2)}) async-start(bf16[16,4,16,128]{3,2,1,0:T(8,128)(2,1)} %copy.124), calls=%async_computation.5 | async-start | bytes 524288 | tf_op jit(solution)/shard_map/all_to_all | solution.py:126
  102.9 12.7 %all-to-all-start.6 = ((bf16[16,4,16,128]{3,2,1,0:T(8,128)(2,1)}), bf16[16,4,16,128]{3,2,1,0:T(8,128)(2,1)S(1)}, u32[]{:S(2)}, u32[]{:S(2)}) async-start(bf16[16,4,16,128]{3,2,1,0:T(8,128)(2,1)} %copy.129), calls=%async_computation.6 | async-start | bytes 524288 | tf_op jit(solution)/shard_map/all_to_all | solution.py:117
  117.0 12.7 %all-to-all-start.7 = ((bf16[16,4,16,128]{3,2,1,0:T(8,128)(2,1)}), bf16[16,4,16,128]{3,2,1,0:T(8,128)(2,1)S(1)}, u32[]{:S(2)}, u32[]{:S(2)}) async-start(bf16[16,4,16,128]{3,2,1,0:T(8,128)(2,1)} %copy.131), calls=%async_computation.7 | async-start | bytes 524288 | tf_op jit(solution)/shard_map/all_to_all | solution.py:126

commit v9 on v8

--- a/solution.py
+++ b/solution.py
@@ -82,9 +82,6 @@
     probe_state = jnp.concatenate(
         [applied[:, 0, :, :probe_width], applied[:, 1, :, :probe_width]], axis=-1
     )
-    state_map = jnp.concatenate(
-        [applied[:, 0, :, probe_width:], applied[:, 1, :, probe_width:]], axis=-1
-    )
     reply_start = jnp.concatenate(
         [projected[:, 0, :, :probe_width], projected[:, 1, :, :probe_width]], axis=-1
     )
@@ -128,8 +125,9 @@
             local_points, shared_rows, 2 * probe_width
         )
         gathered_block = complex_block(gathered_rows)
+    part_block = gathered_block.reshape(local_points, 2, shared_rows, 2 * probe_width)
     states = probe_state.astype(F32) + jnp.einsum(
-        "qih,qhc->qic", state_map, gathered_block, preferred_element_type=F32
+        "qris,qrsc->qic", applied[..., probe_width:], part_block, preferred_element_type=F32
     )
     inner_rows = states.shape[1]
     inner_terms = weight_moments(states, angles)

time: 151 us -> 150 us (level)
  blocking collectives: 51.1 us -> 62.9 us
  local copies, waits for them, and re-layouts: 16 us -> 10.1 us
  waiting for transfers between devices: 35.7 us -> 31.4 us
  starting transfers between devices: 22 us -> 18.6 us
    all_to_all x1 -> x2, blocking collectives: 11.8 us -> 23.6 us  [on_device(): lax.all_to_all(outgoing, 'area', split_axis=0, concat_axis=0, tiled=True)]
    all_to_all x3 -> x2, waiting for transfers between devices: 19.9 us -> 14.7 us  [on_device(): lax.all_to_all(outgoing, 'area', split_axis=0, concat_axis=0, tiled=True)]
    squeeze x1 -> x0, local copies, waits for them, and re-layouts: 4.25 us -> none  [on_device(): applied[:, 0, :, probe_width:]]
    all_to_all x3 -> x2, starting transfers between devices: 10.6 us -> 7.24 us  [on_device(): lax.all_to_all(outgoing, 'area', split_axis=0, concat_axis=0, tiled=True)]
  transfers between devices with their start and end apart: 5 -> 4, of which waited for: 5 -> 4; matrix products, arithmetic and copies ran while one was open for 7% -> 3% of each run, Pallas kernels for 0% -> 0%
where the time goes in v9:
time: 150 us; the launch traced here: 149 us
  blocking collectives  62.9 us (42%)
  waiting for transfers between devices  31.4 us (21%)
  matrix products  20 us (13%)
  starting transfers between devices  18.6 us (12%)
  local copies, waits for them, and re-layouts  10.1 us (7%)
  other arithmetic  4 us (3%)
  between operations  1.78 us (1%)
    all_to_all x2, blocking collectives, on_device(): lax.all_to_all(outgoing, 'area', split_axis=0, concat_axis=0, tiled=True)  23.6 us
    all_to_all x2, blocking collectives, on_device(): lax.all_to_all(parcels, 'area', split_axis=0, concat_axis=0, tiled=True)  23.6 us
    all_to_all x2, waiting for transfers between devices, on_device(): lax.all_to_all(parcels, 'area', split_axis=0, concat_axis=0, tiled=True)  16.6 us
    all_to_all x1, blocking collectives, on_device(): lax.all_to_all(both, 'quad', split_axis=0, concat_axis=0, tiled=True)  15.8 us
    all_to_all x2, waiting for transfers between devices, on_device(): lax.all_to_all(outgoing, 'area', split_axis=0, concat_axis=0, tiled=True)  14.7 us
    all_to_all x2, starting transfers between devices, on_device(): lax.all_to_all(parcels, 'area', split_axis=0, concat_axis=0, tiled=True)  11.3 us
    dot_general x1, matrix products, on_device(): jnp.einsum('qrij,jc->qric', inverses, right, preferred_element_type=F32)  9.26 us
    all_to_all x2, starting transfers between devices, on_device(): lax.all_to_all(outgoing, 'area', split_axis=0, concat_axis=0, tiled=True)  7.24 us
  transfers between devices with their start and end apart: 4, of which 4 were waited for; matrix products, arithmetic and copies ran while one was open for 3% of the time, Pallas kernels for 0%

profile of v9, /device:TPU:0, one launch (start us, length us, event | category | flops | bytes accessed | tf_op | source)
XLA Modules:
  0.0 148.7 jit_solution(15217901766013704669)
XLA Ops:
  0.6 1.3 copy.93
  2.7 9.3 %convert_bitcast_fusion = bf16[4,2,1024,320]{2,3,1,0:T(8,128)(2,1)S(1)} fusion(bf16[4,2,1024,1024]{3,2,1,0:T(8,128)(2,1)} %param.6, bf16[1024,256]{0,1:T(8,128)(2,1)S(1)} %broadcast_select_fusion, bf16[1024,64]{0,1:T(8,128)(2,1)S(1)} %copy-done.6), kind=kOutput, calls=%fused_computation | convolution fusion | flops 5372641280 | bytes 22675456 | tf_op jit(solution)/shard_map/qrij,jc->qric/dot_general | solution.py:79
  12.0 2.8 %fusion.72 = (bf16[4,2,256,320]{2,3,1,0:T(8,128)(2,1)}, f32[4,2,256,320]{2,3,1,0:T(8,128)S(1)}) fusion(bf16[4,2,1024,320]{2,3,1,0:T(8,128)(2,1)S(1)} %convert_bitcast_fusion, bf16[1024,256]{0,1:T(8,128)(2,1)S(1)} %broadcast_select_fusion), kind=kOutput, calls=%fused_computation.129 | convolution fusion | flops 1342832640 | bytes 9699328 | tf_op jit(solution)/shard_map/ig,qric->qrgc/dot_general | solution.py:81
  15.3 0.7 copy.100
  16.0 7.8 %all-to-all-start = ((bf16[16,4,16,128]{3,2,1,0:T(8,128)(2,1)}), bf16[16,4,16,128]{3,2,1,0:T(8,128)(2,1)S(1)}, u32[]{:S(2)}, u32[]{:S(2)}) async-start(bf16[16,4,16,128]{3,2,1,0:T(8,128)(2,1)} %copy.100), calls=%async_computation | async-start | bytes 524288 | tf_op jit(solution)/shard_map/all_to_all | solution.py:114
  24.2 8.8 %all-to-all-done = bf16[16,4,16,128]{3,2,1,0:T(8,128)(2,1)S(1)} async-done(((bf16[16,4,16,128]{3,2,1,0:T(8,128)(2,1)}), bf16[16,4,16,128]{3,2,1,0:T(8,128)(2,1)S(1)}, u32[]{:S(2)}, u32[]{:S(2)}) %all-to-all-start) | async-done | bytes 262176 | tf_op jit(solution)/shard_map/all_to_all | solution.py:114
  33.8 0.7 copy.102
  34.5 3.5 %all-to-all-start.1 = ((bf16[16,4,16,128]{3,2,1,0:T(8,128)(2,1)}), bf16[16,4,16,128]{3,2,1,0:T(8,128)(2,1)S(1)}, u32[]{:S(2)}, u32[]{:S(2)}) async-start(bf16[16,4,16,128]{3,2,1,0:T(8,128)(2,1)} %copy.102), calls=%async_computation.1 | async-start | bytes 524288 | tf_op jit(solution)/shard_map/all_to_all | solution.py:123
  38.0 2.1 %slice_bitcast_fusion.1 = (bf16[4,256,256]{1,2,0:T(8,128)(2,1)S(1)}, bf16[4,256,256]{1,2,0:T(8,128)(2,1)}) fusion(bf16[4,2,256,320]{2,3,1,0:T(8,128)(2,1)} %get-tuple-element.44), kind=kLoop, calls=%fused_computation.34 | loop fusion | bytes 2097152 | tf_op jit(solution)/shard_map/squeeze | solution.py:89
  40.1 0.9 slice_bitcast_fusion.5
  41.0 6.2 %all-to-all-done.1 = bf16[16,4,16,128]{3,2,1,0:T(8,128)(2,1)S(1)} async-done(((bf16[16,4,16,128]{3,2,1,0:T(8,128)(2,1)}), bf16[16,4,16,128]{3,2,1,0:T(8,128)(2,1)S(1)}, u32[]{:S(2)}, u32[]{:S(2)}) %all-to-all-start.1) | async-done | bytes 262176 | tf_op jit(solution)/shard_map/all_to_all | solution.py:123
  47.4 1.6 %fusion.4 = bf16[4,256,128]{1,2,0:T(8,128)(2,1)S(1)} fusion(bf16[4,256,64]{2,1,0:T(8,128)(2,1)S(1)} %get-tuple-element.41, bf16[4,256,64]{2,1,0:T(8,128)(2,1)S(1)} %get-tuple-element.40, bf16[4,256,128]{2,1,0:T(8,128)(2,1)S(1)} %bitcast.139, f32[4,256,64]{1,2,0:T(8,128)} %get-tuple-element.21, f32[4,256,64]{1,2,0:T(8,128)} %get-tuple-element.20, ...), kind=kOutput, calls=%fused_computation.8 | convolution fusion | flops 138280960 | bytes 2359296 | tf_op jit(solution)/shard_map/qgh,qhc->qgc/dot_general | solution.py:17
  49.2 11.8 %all_to_all.45 = bf16[16,4,16,128]{3,2,1,0:T(8,128)(2,1)S(1)} all-to-all(bf16[16,4,16,128]{3,2,1,0:T(8,128)(2,1)S(1)} %copy.107), channel_id=1, replica_groups=mesh['quad'=8,'area'=16] {'area'}, dimensions={0} | all-to-all | bytes 524288 | tf_op jit(solution)/shard_map/all_to_all | solution.py:114
  61.8 11.8 %all_to_all.46 = bf16[16,4,16,128]{3,2,1,0:T(8,128)(2,1)S(1)} all-to-all(bf16[16,4,16,128]{3,2,1,0:T(8,128)(2,1)S(1)} %copy.109), channel_id=1, replica_groups=mesh['quad'=8,'area'=16] {'area'}, dimensions={0} | all-to-all | bytes 524288 | tf_op jit(solution)/shard_map/all_to_all | solution.py:123
  74.4 11.8 %all_to_all.47 = bf16[16,4,16,128]{3,2,1,0:T(8,128)(2,1)S(1)} all-to-all(bf16[16,4,16,128]{3,2,1,0:T(8,128)(2,1)S(1)} %copy.114), channel_id=1, replica_groups=mesh['quad'=8,'area'=16] {'area'}, dimensions={0} | all-to-all | bytes 524288 | tf_op jit(solution)/shard_map/all_to_all | solution.py:114
  86.9 11.8 %all_to_all.48 = bf16[16,4,16,128]{3,2,1,0:T(8,128)(2,1)S(1)} all-to-all(bf16[16,4,16,128]{3,2,1,0:T(8,128)(2,1)S(1)} %copy.116), channel_id=1, replica_groups=mesh['quad'=8,'area'=16] {'area'}, dimensions={0} | all-to-all | bytes 524288 | tf_op jit(solution)/shard_map/all_to_all | solution.py:123
  100.3 3.5 %all-to-all-start.6 = ((bf16[16,4,16,128]{3,2,1,0:T(8,128)(2,1)}), bf16[16,4,16,128]{3,2,1,0:T(8,128)(2,1)S(1)}, u32[]{:S(2)}, u32[]{:S(2)}) async-start(bf16[16,4,16,128]{3,2,1,0:T(8,128)(2,1)} %copy.121), calls=%async_computation.6 | async-start | bytes 524288 | tf_op jit(solution)/shard_map/all_to_all | solution.py:114
  103.8 1.3 slice_bitcast_fusion.3
  105.1 7.8 %all-to-all-done.6 = bf16[16,4,16,128]{3,2,1,0:T(8,128)(2,1)S(1)} async-done(((bf16[16,4,16,128]{3,2,1,0:T(8,128)(2,1)}), bf16[16,4,16,128]{3,2,1,0:T(8,128)(2,1)S(1)}, u32[]{:S(2)}, u32[]{:S(2)}) %all-to-all-start.6) | async-done | bytes 262176 | tf_op jit(solution)/shard_map/all_to_all | solution.py:114
  114.4 3.7 %all-to-all-start.7 = ((bf16[16,4,16,128]{3,2,1,0:T(8,128)(2,1)}), bf16[16,4,16,128]{3,2,1,0:T(8,128)(2,1)S(1)}, u32[]{:S(2)}, u32[]{:S(2)}) async-start(bf16[16,4,16,128]{3,2,1,0:T(8,128)(2,1)} %copy.123), calls=%async_computation.7 | async-start | bytes 524288 | tf_op jit(solution)/shard_map/all_to_all | solution.py:123
  118.5 8.5 %all-to-all-done.7 = bf16[16,4,16,128]{3,2,1,0:T(8,128)(2,1)S(1)} async-done(((bf16[16,4,16,128]{3,2,1,0:T(8,128)(2,1)}), bf16[16,4,16,128]{3,2,1,0:T(8,128)(2,1)S(1)}, u32[]{:S(2)}, u32[]{:S(2)}) %all-to-all-start.7) | async-done | bytes 262176 | tf_op jit(solution)/shard_map/all_to_all | solution.py:123
  127.4 3.0 %bitcast_add_fusion = f32[4,1024,128]{1,2,0:T(8,128)S(1)} fusion(bf16[4,2,256,128]{3,2,1,0:T(8,128)(2,1)S(1)} %bitcast.153, bf16[4,2,1024,320]{2,3,1,0:T(8,128)(2,1)} %copy-done, bf16[4,1024,64]{1,2,0:T(8,128)(2,1)S(1)} %get-tuple-element.19, bf16[4,1024,64]{1,2,0:T(8,128)(2,1)S(1)} %get-tuple-element.18), kind=kOutput, calls=%fused_computation.3 | convolution fusion | flops 539492352 | bytes 7864320 | tf_op jit(solution)/shard_map/qris,qrsc->qic/dot_general | solution.py:129
  131.6 15.8 %all_to_all.49 = bf16[8,2,144,128]{3,2,1,0:T(8,128)(2,1)S(1)} all-to-all(bf16[8,2,144,128]{3,2,1,0:T(8,128)(2,1)S(1)} %pad_maximum_fusion.1), channel_id=1, replica_groups=mesh['quad'=8,'area'=16] {'quad'}, dimensions={0} | all-to-all | bytes 1179648 | tf_op jit(solution)/shard_map/all_to_all | solution.py:142
  147.4 0.7 convert_reduce_fusion
  (70 shorter events, 9.6 us)
Async XLA Ops:
  0.6 2.1 %copy-start.6 = (bf16[1024,64]{0,1:T(8,128)(2,1)S(1)}, bf16[1024,64]{0,1:T(8,128)(2,1)}, u32[]{:S(2)}) copy-start(bf16[1024,64]{0,1:T(8,128)(2,1)} %param.8) | copy-start | bytes 393220
  12.0 2.8 %copy-start = (bf16[4,2,1024,320]{2,3,1,0:T(8,128)(2,1)}, bf16[4,2,1024,320]{2,3,1,0:T(8,128)(2,1)S(1)}, u32[]{:S(2)}) copy-start(bf16[4,2,1024,320]{2,3,1,0:T(8,128)(2,1)S(1)} %convert_bitcast_fusion) | copy-start | bytes 15728644
  14.8 9.2 %copy-start.4 = (s32[16,256]{1,0:T(8,128)S(1)}, s32[16,256]{1,0:T(8,128)}, u32[]{:S(2)}) copy-start(s32[16,256]{1,0:T(8,128)} %param.10) | copy-start | bytes 49156
  14.8 9.4 %copy-start.5 = (f32[128]{0:T(128)S(1)}, f32[128]{0:T(128)}, u32[]{:S(2)}) copy-start(f32[128]{0:T(128)} %param.9) | copy-start | bytes 1540
  16.0 17.0 %all-to-all-start = ((bf16[16,4,16,128]{3,2,1,0:T(8,128)(2,1)}), bf16[16,4,16,128]{3,2,1,0:T(8,128)(2,1)S(1)}, u32[]{:S(2)}, u32[]{:S(2)}) async-start(bf16[16,4,16,128]{3,2,1,0:T(8,128)(2,1)} %copy.100), calls=%async_computation | async-start | bytes 524288 | tf_op jit(solution)/shard_map/all_to_all | solution.py:114
  34.5 12.7 %all-to-all-start.1 = ((bf16[16,4,16,128]{3,2,1,0:T(8,128)(2,1)}), bf16[16,4,16,128]{3,2,1,0:T(8,128)(2,1)S(1)}, u32[]{:S(2)}, u32[]{:S(2)}) async-start(bf16[16,4,16,128]{3,2,1,0:T(8,128)(2,1)} %copy.102), calls=%async_computation.1 | async-start | bytes 524288 | tf_op jit(solution)/shard_map/all_to_all | solution.py:123
  61.3 12.4 %copy-start.1 = (bf16[4,256,256]{1,2,0:T(8,128)(2,1)S(1)}, bf16[4,256,256]{1,2,0:T(8,128)(2,1)}, u32[]{:S(2)}) copy-start(bf16[4,256,256]{1,2,0:T(8,128)(2,1)} %get-tuple-element.25) | copy-start | bytes 1572868
  61.3 12.4 %copy-start.2 = (f32[4,256,64]{1,2,0:T(8,128)S(1)}, f32[4,256,64]{1,2,0:T(8,128)}, u32[]{:S(2)}) copy-start(f32[4,256,64]{1,2,0:T(8,128)} %get-tuple-element.20) | copy-start | bytes 786436
  61.3 12.4 %copy-start.3 = (f32[4,256,64]{1,2,0:T(8,128)S(1)}, f32[4,256,64]{1,2,0:T(8,128)}, u32[]{:S(2)}) copy-start(f32[4,256,64]{1,2,0:T(8,128)} %get-tuple-element.21) | copy-start | bytes 786436
  100.3 12.7 %all-to-all-start.6 = ((bf16[16,4,16,128]{3,2,1,0:T(8,128)(2,1)}), bf16[16,4,16,128]{3,2,1,0:T(8,128)(2,1)S(1)}, u32[]{:S(2)}, u32[]{:S(2)}) async-start(bf16[16,4,16,128]{3,2,1,0:T(8,128)(2,1)} %copy.121), calls=%async_computation.6 | async-start | bytes 524288 | tf_op jit(solution)/shard_map/all_to_all | solution.py:114
  114.4 12.7 %all-to-all-start.7 = ((bf16[16,4,16,128]{3,2,1,0:T(8,128)(2,1)}), bf16[16,4,16,128]{3,2,1,0:T(8,128)(2,1)S(1)}, u32[]{:S(2)}, u32[]{:S(2)}) async-start(bf16[16,4,16,128]{3,2,1,0:T(8,128)(2,1)} %copy.123), calls=%async_computation.7 | async-start | bytes 524288 | tf_op jit(solution)/shard_map/all_to_all | solution.py:123

commit v10 on v9

--- a/solution.py
+++ b/solution.py
@@ -48,6 +48,18 @@
     parts = jnp.moveaxis(value.reshape(*before, lax.axis_size(axis), -1, *after), dim, 0)
     arrived = lax.all_to_all(parts, axis, split_axis=0, concat_axis=0, tiled=True)
     return arrived.sum(axis=0)
+
+
+def rotate(values, angles, power):
+    width_half = values.shape[-1] // 2
+    value_re = values[..., :width_half]
+    value_im = values[..., width_half:]
+    cosine_now = jnp.cos(power * angles)[:, None, None]
+    sine_now = jnp.sin(power * angles)[:, None, None]
+    return jnp.concatenate(
+        [cosine_now * value_re - sine_now * value_im, cosine_now * value_im + sine_now * value_re],
+        axis=-1,
+    )
 
 
 def weight_moments(values, angles):
@@ -125,12 +137,18 @@
             local_points, shared_rows, 2 * probe_width
         )
         gathered_block = complex_block(gathered_rows)
-    part_block = gathered_block.reshape(local_points, 2, shared_rows, 2 * probe_width)
-    states = probe_state.astype(F32) + jnp.einsum(
-        "qris,qrsc->qic", applied[..., probe_width:], part_block, preferred_element_type=F32
+    inner_rows = probe_state.shape[1]
+    gathered_float = gathered_rows.astype(F32)
+    weighted_block = jnp.stack(
+        [complex_block(rotate(gathered_float, angles, power)) for power in (1, 2)]
+    ).astype(BF16)
+    weighted_block = weighted_block.reshape(2, local_points, 2, shared_rows, 2 * probe_width)
+    inner_terms = weight_moments(probe_state.astype(F32), angles) + jnp.einsum(
+        "qris,mqrsc->mic",
+        applied[..., probe_width:],
+        weighted_block,
+        preferred_element_type=F32,
     )
-    inner_rows = states.shape[1]
-    inner_terms = weight_moments(states, angles)
     owned_terms = weight_moments(interface_values, angles)
     inner_parts = jnp.moveaxis(
         inner_terms.reshape(2, quad_count, inner_rows // quad_count, 2 * probe_width), 1, 0

time: 150 us -> 155 us (1.033)
  blocking collectives: 62.9 us -> 39.3 us
  waiting for transfers between devices: 31.4 us -> 48.6 us
  starting transfers between devices: 18.6 us -> 25.7 us
  local copies, waits for them, and re-layouts: 10.1 us -> 12.2 us
  matrix products: 20 us -> 21.7 us
    all_to_all x2 -> x1, blocking collectives: 23.6 us -> 11.8 us  [on_device(): lax.all_to_all(outgoing, 'area', split_axis=0, concat_axis=0, tiled=True)]
    all_to_all x2 -> x1, blocking collectives: 23.6 us -> 11.8 us  [on_device(): lax.all_to_all(parcels, 'area', split_axis=0, concat_axis=0, tiled=True)]
    all_to_all x2 -> x3, waiting for transfers between devices: 16.6 us -> 25.3 us  [on_device(): lax.all_to_all(parcels, 'area', split_axis=0, concat_axis=0, tiled=True)]
    all_to_all x2 -> x3, waiting for transfers between devices: 14.7 us -> 23.3 us  [on_device(): lax.all_to_all(outgoing, 'area', split_axis=0, concat_axis=0, tiled=True)]
    all_to_all x2 -> x3, starting transfers between devices: 11.3 us -> 15.1 us  [on_device(): lax.all_to_all(parcels, 'area', split_axis=0, concat_axis=0, tiled=True)]
    all_to_all x2 -> x3, starting transfers between devices: 7.24 us -> 10.6 us  [on_device(): lax.all_to_all(outgoing, 'area', split_axis=0, concat_axis=0, tiled=True)]
  transfers between devices with their start and end apart: 4 -> 6, of which waited for: 4 -> 6; matrix products, arithmetic and copies ran while one was open for 3% -> 4% of each run, Pallas kernels for 0% -> 0%
where the time goes in v10:
time: 155 us; the launch traced here: 154 us
  waiting for transfers between devices  48.6 us (31%)
  blocking collectives  39.3 us (25%)
  starting transfers between devices  25.7 us (17%)
  matrix products  21.7 us (14%)
  local copies, waits for them, and re-layouts  12.2 us (8%)
  other arithmetic  5.05 us (3%)
  between operations  1.83 us (1%)
    all_to_all x3, waiting for transfers between devices, on_device(): lax.all_to_all(parcels, 'area', split_axis=0, concat_axis=0, tiled=True)  25.3 us
    all_to_all x3, waiting for transfers between devices, on_device(): lax.all_to_all(outgoing, 'area', split_axis=0, concat_axis=0, tiled=True)  23.3 us
    all_to_all x1, blocking collectives, on_device(): lax.all_to_all(both, 'quad', split_axis=0, concat_axis=0, tiled=True)  15.8 us
    all_to_all x3, starting transfers between devices, on_device(): lax.all_to_all(parcels, 'area', split_axis=0, concat_axis=0, tiled=True)  15.1 us
    all_to_all x1, blocking collectives, on_device(): lax.all_to_all(parcels, 'area', split_axis=0, concat_axis=0, tiled=True)  11.8 us
    all_to_all x1, blocking collectives, on_device(): lax.all_to_all(outgoing, 'area', split_axis=0, concat_axis=0, tiled=True)  11.8 us
    all_to_all x3, starting transfers between devices, on_device(): lax.all_to_all(outgoing, 'area', split_axis=0, concat_axis=0, tiled=True)  10.6 us
    dot_general x1, matrix products, on_device(): jnp.einsum('qrij,jc->qric', inverses, right, preferred_element_type=F32)  9.26 us
  transfers between devices with their start and end apart: 6, of which 6 were waited for; matrix products, arithmetic and copies ran while one was open for 4% of the time, Pallas kernels for 0%

profile of v10, /device:TPU:0, one launch (start us, length us, event | category | flops | bytes accessed | tf_op | source)
XLA Modules:
  0.0 154.4 jit_solution(8060432232093764221)
XLA Ops:
  0.6 1.3 copy.53
  2.7 9.3 %convert_bitcast_fusion = bf16[4,2,1024,320]{2,3,1,0:T(8,128)(2,1)S(1)} fusion(bf16[4,2,1024,1024]{3,2,1,0:T(8,128)(2,1)} %param.6, bf16[1024,256]{0,1:T(8,128)(2,1)S(1)} %broadcast_select_fusion, bf16[1024,64]{0,1:T(8,128)(2,1)S(1)} %copy-done.7), kind=kOutput, calls=%fused_computation | convolution fusion | flops 5372641280 | bytes 22675456 | tf_op jit(solution)/shard_map/qrij,jc->qric/dot_general | solution.py:91
  12.0 2.8 %fusion.78 = (bf16[4,2,256,320]{2,3,1,0:T(8,128)(2,1)}, f32[4,2,256,320]{2,3,1,0:T(8,128)S(1)}) fusion(bf16[4,2,1024,320]{2,3,1,0:T(8,128)(2,1)S(1)} %convert_bitcast_fusion, bf16[1024,256]{0,1:T(8,128)(2,1)S(1)} %broadcast_select_fusion), kind=kOutput, calls=%fused_computation.144 | convolution fusion | flops 1342832640 | bytes 9699328 | tf_op jit(solution)/shard_map/ig,qric->qrgc/dot_general | solution.py:93
  16.0 7.8 %all-to-all-start = ((bf16[16,4,16,128]{3,2,1,0:T(8,128)(2,1)}), bf16[16,4,16,128]{3,2,1,0:T(8,128)(2,1)S(1)}, u32[]{:S(2)}, u32[]{:S(2)}) async-start(bf16[16,4,16,128]{3,2,1,0:T(8,128)(2,1)} %copy.60), calls=%async_computation | async-start | bytes 524288 | tf_op jit(solution)/shard_map/all_to_all | solution.py:126
  24.2 8.8 %all-to-all-done = bf16[16,4,16,128]{3,2,1,0:T(8,128)(2,1)S(1)} async-done(((bf16[16,4,16,128]{3,2,1,0:T(8,128)(2,1)}), bf16[16,4,16,128]{3,2,1,0:T(8,128)(2,1)S(1)}, u32[]{:S(2)}, u32[]{:S(2)}) %all-to-all-start) | async-done | bytes 262176 | tf_op jit(solution)/shard_map/all_to_all | solution.py:126
  34.5 3.5 %all-to-all-start.1 = ((bf16[16,4,16,128]{3,2,1,0:T(8,128)(2,1)}), bf16[16,4,16,128]{3,2,1,0:T(8,128)(2,1)S(1)}, u32[]{:S(2)}, u32[]{:S(2)}) async-start(bf16[16,4,16,128]{3,2,1,0:T(8,128)(2,1)} %copy.63), calls=%async_computation.1 | async-start | bytes 524288 | tf_op jit(solution)/shard_map/all_to_all | solution.py:135
  38.0 2.1 %slice_bitcast_fusion.9 = (bf16[4,256,256]{1,2,0:T(8,128)(2,1)S(1)}, bf16[4,256,256]{1,2,0:T(8,128)(2,1)}) fusion(bf16[4,2,256,320]{2,3,1,0:T(8,128)(2,1)} %get-tuple-element.53), kind=kLoop, calls=%fused_computation.40 | loop fusion | bytes 2097152 | tf_op jit(solution)/shard_map/squeeze | solution.py:101
  40.1 0.9 slice_bitcast_fusion.13
  41.0 6.1 %all-to-all-done.1 = bf16[16,4,16,128]{3,2,1,0:T(8,128)(2,1)S(1)} async-done(((bf16[16,4,16,128]{3,2,1,0:T(8,128)(2,1)}), bf16[16,4,16,128]{3,2,1,0:T(8,128)(2,1)S(1)}, u32[]{:S(2)}, u32[]{:S(2)}) %all-to-all-start.1) | async-done | bytes 262176 | tf_op jit(solution)/shard_map/all_to_all | solution.py:135
  47.3 1.6 %fusion.4 = bf16[4,256,128]{1,2,0:T(8,128)(2,1)S(1)} fusion(bf16[4,256,64]{2,1,0:T(8,128)(2,1)S(1)} %get-tuple-element.50, bf16[4,256,64]{2,1,0:T(8,128)(2,1)S(1)} %get-tuple-element.49, bf16[4,256,128]{2,1,0:T(8,128)(2,1)S(1)} %bitcast.164, f32[4,256,64]{1,2,0:T(8,128)} %get-tuple-element.23, f32[4,256,64]{1,2,0:T(8,128)} %get-tuple-element.22, ...), kind=kOutput, calls=%fused_computation.10 | convolution fusion | flops 138280960 | bytes 2359296 | tf_op jit(solution)/shard_map/qgh,qhc->qgc/dot_general | solution.py:17
  49.2 11.8 %all_to_all.45 = bf16[16,4,16,128]{3,2,1,0:T(8,128)(2,1)S(1)} all-to-all(bf16[16,4,16,128]{3,2,1,0:T(8,128)(2,1)S(1)} %copy.68), channel_id=1, replica_groups=mesh['quad'=8,'area'=16] {'area'}, dimensions={0} | all-to-all | bytes 524288 | tf_op jit(solution)/shard_map/all_to_all | solution.py:126
  61.7 11.8 %all_to_all.46 = bf16[16,4,16,128]{3,2,1,0:T(8,128)(2,1)S(1)} all-to-all(bf16[16,4,16,128]{3,2,1,0:T(8,128)(2,1)S(1)} %copy.71), channel_id=1, replica_groups=mesh['quad'=8,'area'=16] {'area'}, dimensions={0} | all-to-all | bytes 524288 | tf_op jit(solution)/shard_map/all_to_all | solution.py:135
  75.1 3.5 %all-to-all-start.4 = ((bf16[16,4,16,128]{3,2,1,0:T(8,128)(2,1)}), bf16[16,4,16,128]{3,2,1,0:T(8,128)(2,1)S(1)}, u32[]{:S(2)}, u32[]{:S(2)}) async-start(bf16[16,4,16,128]{3,2,1,0:T(8,128)(2,1)} %copy.76), calls=%async_computation.4 | async-start | bytes 524288 | tf_op jit(solution)/shard_map/all_to_all | solution.py:126
  78.6 1.3 slice_bitcast_fusion.11
  80.2 7.6 %all-to-all-done.4 = bf16[16,4,16,128]{3,2,1,0:T(8,128)(2,1)S(1)} async-done(((bf16[16,4,16,128]{3,2,1,0:T(8,128)(2,1)}), bf16[16,4,16,128]{3,2,1,0:T(8,128)(2,1)S(1)}, u32[]{:S(2)}, u32[]{:S(2)}) %all-to-all-start.4) | async-done | bytes 262176 | tf_op jit(solution)/shard_map/all_to_all | solution.py:126
  89.2 3.5 %all-to-all-start.5 = ((bf16[16,4,16,128]{3,2,1,0:T(8,128)(2,1)}), bf16[16,4,16,128]{3,2,1,0:T(8,128)(2,1)S(1)}, u32[]{:S(2)}, u32[]{:S(2)}) async-start(bf16[16,4,16,128]{3,2,1,0:T(8,128)(2,1)} %copy.79), calls=%async_computation.5 | async-start | bytes 524288 | tf_op jit(solution)/shard_map/all_to_all | solution.py:135
  93.4 8.5 %all-to-all-done.5 = bf16[16,4,16,128]{3,2,1,0:T(8,128)(2,1)S(1)} async-done(((bf16[16,4,16,128]{3,2,1,0:T(8,128)(2,1)}), bf16[16,4,16,128]{3,2,1,0:T(8,128)(2,1)S(1)}, u32[]{:S(2)}, u32[]{:S(2)}) %all-to-all-start.5) | async-done | bytes 262176 | tf_op jit(solution)/shard_map/all_to_all | solution.py:135
  102.1 1.8 %fusion.6 = bf16[4,256,128]{1,2,0:T(8,128)(2,1)S(1)} fusion(bf16[4,256,64]{2,1,0:T(8,128)(2,1)S(1)} %get-tuple-element.46, bf16[4,256,64]{2,1,0:T(8,128)(2,1)S(1)} %get-tuple-element.45, bf16[4,256,128]{2,1,0:T(8,128)(2,1)S(1)} %bitcast.162, f32[4,256,64]{1,2,0:T(8,128)} %get-tuple-element.23, f32[4,256,64]{1,2,0:T(8,128)} %get-tuple-element.22, ...), kind=kOutput, calls=%fused_computation.12 | convolution fusion | flops 138280960 | bytes 2359296 | tf_op jit(solution)/shard_map/qgh,qhc->qgc/dot_general | solution.py:17
  104.8 3.7 %all-to-all-start.6 = ((bf16[16,4,16,128]{3,2,1,0:T(8,128)(2,1)}), bf16[16,4,16,128]{3,2,1,0:T(8,128)(2,1)S(1)}, u32[]{:S(2)}, u32[]{:S(2)}) async-start(bf16[16,4,16,128]{3,2,1,0:T(8,128)(2,1)} %copy.84), calls=%async_computation.6 | async-start | bytes 524288 | tf_op jit(solution)/shard_map/all_to_all | solution.py:126
  108.6 8.9 %all-to-all-done.6 = bf16[16,4,16,128]{3,2,1,0:T(8,128)(2,1)S(1)} async-done(((bf16[16,4,16,128]{3,2,1,0:T(8,128)(2,1)}), bf16[16,4,16,128]{3,2,1,0:T(8,128)(2,1)S(1)}, u32[]{:S(2)}, u32[]{:S(2)}) %all-to-all-start.6) | async-done | bytes 262176 | tf_op jit(solution)/shard_map/all_to_all | solution.py:126
  119.0 3.5 %all-to-all-start.7 = ((bf16[16,4,16,128]{3,2,1,0:T(8,128)(2,1)}), bf16[16,4,16,128]{3,2,1,0:T(8,128)(2,1)S(1)}, u32[]{:S(2)}, u32[]{:S(2)}) async-start(bf16[16,4,16,128]{3,2,1,0:T(8,128)(2,1)} %copy.87), calls=%async_computation.7 | async-start | bytes 524288 | tf_op jit(solution)/shard_map/all_to_all | solution.py:135
  122.9 8.7 %all-to-all-done.7 = bf16[16,4,16,128]{3,2,1,0:T(8,128)(2,1)S(1)} async-done(((bf16[16,4,16,128]{3,2,1,0:T(8,128)(2,1)}), bf16[16,4,16,128]{3,2,1,0:T(8,128)(2,1)S(1)}, u32[]{:S(2)}, u32[]{:S(2)}) %all-to-all-start.7) | async-done | bytes 262176 | tf_op jit(solution)/shard_map/all_to_all | solution.py:135
  133.3 3.4 %fusion.3 = bf16[2,1024,128]{1,2,0:T(8,128)(2,1)S(1)} fusion(bf16[4,2,1024,320]{2,3,1,0:T(8,128)(2,1)} %copy-done, f32[1,1024,128]{1,2,0:T(8,128)S(1)} %maximum_bitcast_fusion.3, f32[1,1024,128]{1,2,0:T(8,128)S(1)} %maximum_bitcast_fusion.2, bf16[1,4,2,256,128]{3,4,2,0,1:T(8,128)(2,1)S(1)} %copy.90, bf16[1,4,2,256,128]{3,4,2,0,1:T(8,128)(2,1)S(1)} %copy.89), kind=kOutput, calls=%fused_computation.6 | convolution fusion | flops 1075052544 | bytes 6815744 | tf_op jit(solution)/shard_map/qris,mqrsc->mic/dot_general | solution.py:146
  137.3 15.8 %all_to_all.47 = bf16[8,2,144,128]{3,2,1,0:T(8,128)(2,1)S(1)} all-to-all(bf16[8,2,144,128]{3,2,1,0:T(8,128)(2,1)S(1)} %pad_maximum_fusion.1), channel_id=1, replica_groups=mesh['quad'=8,'area'=16] {'quad'}, dimensions={0} | all-to-all | bytes 1179648 | tf_op jit(solution)/shard_map/all_to_all | solution.py:160
  (78 shorter events, 14.5 us)
Async XLA Ops:
  0.6 2.1 %copy-start.7 = (bf16[1024,64]{0,1:T(8,128)(2,1)S(1)}, bf16[1024,64]{0,1:T(8,128)(2,1)}, u32[]{:S(2)}) copy-start(bf16[1024,64]{0,1:T(8,128)(2,1)} %param.8) | copy-start | bytes 393220
  12.0 2.8 %copy-start = (bf16[4,2,1024,320]{2,3,1,0:T(8,128)(2,1)}, bf16[4,2,1024,320]{2,3,1,0:T(8,128)(2,1)S(1)}, u32[]{:S(2)}) copy-start(bf16[4,2,1024,320]{2,3,1,0:T(8,128)(2,1)S(1)} %convert_bitcast_fusion) | copy-start | bytes 15728644
  14.8 9.2 %copy-start.5 = (s32[16,256]{1,0:T(8,128)S(1)}, s32[16,256]{1,0:T(8,128)}, u32[]{:S(2)}) copy-start(s32[16,256]{1,0:T(8,128)} %param.10) | copy-start | bytes 49156
  14.8 9.4 %copy-start.6 = (f32[128]{0:T(128)S(1)}, f32[128]{0:T(128)}, u32[]{:S(2)}) copy-start(f32[128]{0:T(128)} %param.9) | copy-start | bytes 1540
  16.0 17.0 %all-to-all-start = ((bf16[16,4,16,128]{3,2,1,0:T(8,128)(2,1)}), bf16[16,4,16,128]{3,2,1,0:T(8,128)(2,1)S(1)}, u32[]{:S(2)}, u32[]{:S(2)}) async-start(bf16[16,4,16,128]{3,2,1,0:T(8,128)(2,1)} %copy.60), calls=%async_computation | async-start | bytes 524288 | tf_op jit(solution)/shard_map/all_to_all | solution.py:126
  34.5 12.7 %all-to-all-start.1 = ((bf16[16,4,16,128]{3,2,1,0:T(8,128)(2,1)}), bf16[16,4,16,128]{3,2,1,0:T(8,128)(2,1)S(1)}, u32[]{:S(2)}, u32[]{:S(2)}) async-start(bf16[16,4,16,128]{3,2,1,0:T(8,128)(2,1)} %copy.63), calls=%async_computation.1 | async-start | bytes 524288 | tf_op jit(solution)/shard_map/all_to_all | solution.py:135
  40.1 33.6 %copy-start.1 = (bf16[4,256,256]{1,2,0:T(8,128)(2,1)}, bf16[4,256,256]{1,2,0:T(8,128)(2,1)S(1)}, u32[]{:S(2)}) copy-start(bf16[4,256,256]{1,2,0:T(8,128)(2,1)S(1)} %get-tuple-element.26) | copy-start | bytes 1572868
  61.3 12.4 %copy-start.2 = (bf16[4,256,256]{1,2,0:T(8,128)(2,1)S(1)}, bf16[4,256,256]{1,2,0:T(8,128)(2,1)}, u32[]{:S(2)}) copy-start(bf16[4,256,256]{1,2,0:T(8,128)(2,1)} %get-tuple-element.27) | copy-start | bytes 1572868
  61.3 12.4 %copy-start.3 = (f32[4,256,64]{1,2,0:T(8,128)S(1)}, f32[4,256,64]{1,2,0:T(8,128)}, u32[]{:S(2)}) copy-start(f32[4,256,64]{1,2,0:T(8,128)} %get-tuple-element.22) | copy-start | bytes 786436
  61.3 12.4 %copy-start.4 = (f32[4,256,64]{1,2,0:T(8,128)S(1)}, f32[4,256,64]{1,2,0:T(8,128)}, u32[]{:S(2)}) copy-start(f32[4,256,64]{1,2,0:T(8,128)} %get-tuple-element.23) | copy-start | bytes 786436
  75.1 12.7 %all-to-all-start.4 = ((bf16[16,4,16,128]{3,2,1,0:T(8,128)(2,1)}), bf16[16,4,16,128]{3,2,1,0:T(8,128)(2,1)S(1)}, u32[]{:S(2)}, u32[]{:S(2)}) async-start(bf16[16,4,16,128]{3,2,1,0:T(8,128)(2,1)} %copy.76), calls=%async_computation.4 | async-start | bytes 524288 | tf_op jit(solution)/shard_map/all_to_all | solution.py:126
  89.2 12.7 %all-to-all-start.5 = ((bf16[16,4,16,128]{3,2,1,0:T(8,128)(2,1)}), bf16[16,4,16,128]{3,2,1,0:T(8,128)(2,1)S(1)}, u32[]{:S(2)}, u32[]{:S(2)}) async-start(bf16[16,4,16,128]{3,2,1,0:T(8,128)(2,1)} %copy.79), calls=%async_computation.5 | async-start | bytes 524288 | tf_op jit(solution)/shard_map/all_to_all | solution.py:135
  104.8 12.7 %all-to-all-start.6 = ((bf16[16,4,16,128]{3,2,1,0:T(8,128)(2,1)}), bf16[16,4,16,128]{3,2,1,0:T(8,128)(2,1)S(1)}, u32[]{:S(2)}, u32[]{:S(2)}) async-start(bf16[16,4,16,128]{3,2,1,0:T(8,128)(2,1)} %copy.84), calls=%async_computation.6 | async-start | bytes 524288 | tf_op jit(solution)/shard_map/all_to_all | solution.py:126
  119.0 12.7 %all-to-all-start.7 = ((bf16[16,4,16,128]{3,2,1,0:T(8,128)(2,1)}), bf16[16,4,16,128]{3,2,1,0:T(8,128)(2,1)S(1)}, u32[]{:S(2)}, u32[]{:S(2)}) async-start(bf16[16,4,16,128]{3,2,1,0:T(8,128)(2,1)} %copy.87), calls=%async_computation.7 | async-start | bytes 524288 | tf_op jit(solution)/shard_map/all_to_all | solution.py:135

commit v11 on v9

--- a/solution.py
+++ b/solution.py
@@ -78,16 +78,17 @@
     right = jnp.concatenate([probes, coupling_live], axis=1)
     applied = jnp.einsum("qrij,jc->qric", inverses, right, preferred_element_type=F32)
     applied = applied.astype(BF16)
-    projected = jnp.einsum("ig,qric->qrgc", coupling_live, applied, preferred_element_type=F32)
+    projected_probe = jnp.einsum(
+        "ig,qric->qrgc", coupling_live, applied[..., :probe_width], preferred_element_type=F32
+    )
+    projected_map = jnp.einsum(
+        "ig,qric->qrgc", coupling_live, applied[..., probe_width:], preferred_element_type=F32
+    )
     probe_state = jnp.concatenate(
         [applied[:, 0, :, :probe_width], applied[:, 1, :, :probe_width]], axis=-1
     )
-    reply_start = jnp.concatenate(
-        [projected[:, 0, :, :probe_width], projected[:, 1, :, :probe_width]], axis=-1
-    )
-    reply_map = jnp.concatenate(
-        [projected[:, 0, :, probe_width:], projected[:, 1, :, probe_width:]], axis=-1
-    )
+    reply_start = jnp.concatenate([projected_probe[:, 0], projected_probe[:, 1]], axis=-1)
+    reply_map = jnp.concatenate([projected_map[:, 0], projected_map[:, 1]], axis=-1)
     reply_parts = (reply_map.astype(BF16),)
     block_offsets = (
         lax.dynamic_slice_in_dim(area_rows, area_index * bucket, bucket, 1)

time: 150 us -> 148 us (0.987)
    all_to_all x2, waiting for transfers between devices: 16.6 us -> 13.2 us  [on_device(): lax.all_to_all(parcels, 'area', split_axis=0, concat_axis=0, tiled=True)]
    squeeze x2, local copies, waits for them, and re-layouts: 2.94 us -> 0.11 us  [the longest x1 0.07 us: on_device(): projected_map[:, 0]]
    all_to_all x2, waiting for transfers between devices: 14.7 us -> 17.6 us  [on_device(): lax.all_to_all(outgoing, 'area', split_axis=0, concat_axis=0, tiled=True)]
    unnamed x15 -> x9, local copies, waits for them, and re-layouts: 1.31 us -> 3.04 us
    dot_general x1 -> x2, matrix products: 2.77 us -> 3.97 us  [the longest x1 3.49 us: on_device(): jnp.einsum('ig,qric->qrgc', coupling_live, applied[..., probe_width:], pr...]
  transfers between devices with their start and end apart: 4 -> 4, of which waited for: 4 -> 4; matrix products, arithmetic and copies ran while one was open for 3% -> 4% of each run, Pallas kernels for 0% -> 0%
where the time goes in v11:
time: 148 us; the launch traced here: 147 us
  blocking collectives  62.9 us (42%)
  waiting for transfers between devices  30.7 us (21%)
  matrix products  20 us (14%)
  starting transfers between devices  18.6 us (13%)
  local copies, waits for them, and re-layouts  8.97 us (6%)
  other arithmetic  4 us (3%)
  between operations  1.82 us (1%)
    all_to_all x2, blocking collectives, on_device(): lax.all_to_all(outgoing, 'area', split_axis=0, concat_axis=0, tiled=True)  23.6 us
    all_to_all x2, blocking collectives, on_device(): lax.all_to_all(parcels, 'area', split_axis=0, concat_axis=0, tiled=True)  23.6 us
    all_to_all x2, waiting for transfers between devices, on_device(): lax.all_to_all(outgoing, 'area', split_axis=0, concat_axis=0, tiled=True)  17.6 us
    all_to_all x1, blocking collectives, on_device(): lax.all_to_all(both, 'quad', split_axis=0, concat_axis=0, tiled=True)  15.8 us
    all_to_all x2, waiting for transfers between devices, on_device(): lax.all_to_all(parcels, 'area', split_axis=0, concat_axis=0, tiled=True)  13.2 us
    all_to_all x2, starting transfers between devices, on_device(): lax.all_to_all(parcels, 'area', split_axis=0, concat_axis=0, tiled=True)  11.4 us
    dot_general x1, matrix products, on_device(): jnp.einsum('qrij,jc->qric', inverses, right, preferred_element_type=F32)  9.26 us
    all_to_all x2, starting transfers between devices, on_device(): lax.all_to_all(outgoing, 'area', split_axis=0, concat_axis=0, tiled=True)  7.24 us
  transfers between devices with their start and end apart: 4, of which 4 were waited for; matrix products, arithmetic and copies ran while one was open for 4% of the time, Pallas kernels for 0%

profile of v11, /device:TPU:0, one launch (start us, length us, event | category | flops | bytes accessed | tf_op | source)
XLA Modules:
  0.0 147.0 jit_solution(1578991106646812841)
XLA Ops:
  1.3 1.2 copy.96
  2.7 9.3 %convert_bitcast_fusion = bf16[4,2,1024,320]{2,3,1,0:T(8,128)(2,1)S(1)} fusion(bf16[4,2,1024,1024]{3,2,1,0:T(8,128)(2,1)} %param.6, bf16[1024,256]{0,1:T(8,128)(2,1)S(1)} %broadcast_select_fusion, bf16[1024,64]{0,1:T(8,128)(2,1)S(1)} %copy-done.3), kind=kOutput, calls=%fused_computation | convolution fusion | flops 5372641280 | bytes 22675456 | tf_op jit(solution)/shard_map/qrij,jc->qric/dot_general | solution.py:79
  12.5 1.8 %copy-done = bf16[4,2,1024,320]{2,3,1,0:T(8,128)(2,1)} copy-done((bf16[4,2,1024,320]{2,3,1,0:T(8,128)(2,1)}, bf16[4,2,1024,320]{2,3,1,0:T(8,128)(2,1)S(1)}, u32[]{:S(2)}) %copy-start) | copy-done | bytes 5242904
  14.8 0.7 copy.104
  15.5 7.8 %all-to-all-start = ((bf16[16,4,16,128]{3,2,1,0:T(8,128)(2,1)}), bf16[16,4,16,128]{3,2,1,0:T(8,128)(2,1)S(1)}, u32[]{:S(2)}, u32[]{:S(2)}) async-start(bf16[16,4,16,128]{3,2,1,0:T(8,128)(2,1)} %copy.104), calls=%async_computation | async-start | bytes 524288 | tf_op jit(solution)/shard_map/all_to_all | solution.py:115
  23.5 3.5 %fusion.9 = bf16[4,2,256,256]{2,3,1,0:T(8,128)(2,1)S(1)} fusion(bf16[4,2,1024,320]{2,3,1,0:T(8,128)(2,1)} %copy-done, bf16[1024,256]{0,1:T(8,128)(2,1)S(1)} %broadcast_select_fusion), kind=kOutput, calls=%fused_computation.7 | convolution fusion | flops 1074266112 | bytes 5767168 | tf_op jit(solution)/shard_map/ig,qric->qrgc/dot_general | solution.py:84
  27.2 5.3 %all-to-all-done = bf16[16,4,16,128]{3,2,1,0:T(8,128)(2,1)S(1)} async-done(((bf16[16,4,16,128]{3,2,1,0:T(8,128)(2,1)}), bf16[16,4,16,128]{3,2,1,0:T(8,128)(2,1)S(1)}, u32[]{:S(2)}, u32[]{:S(2)}) %all-to-all-start) | async-done | bytes 262176 | tf_op jit(solution)/shard_map/all_to_all | solution.py:115
  33.3 0.7 copy.106
  34.0 3.5 %all-to-all-start.1 = ((bf16[16,4,16,128]{3,2,1,0:T(8,128)(2,1)}), bf16[16,4,16,128]{3,2,1,0:T(8,128)(2,1)S(1)}, u32[]{:S(2)}, u32[]{:S(2)}) async-start(bf16[16,4,16,128]{3,2,1,0:T(8,128)(2,1)} %copy.106), calls=%async_computation.1 | async-start | bytes 524288 | tf_op jit(solution)/shard_map/all_to_all | solution.py:124
  37.7 9.0 %all-to-all-done.1 = bf16[16,4,16,128]{3,2,1,0:T(8,128)(2,1)S(1)} async-done(((bf16[16,4,16,128]{3,2,1,0:T(8,128)(2,1)}), bf16[16,4,16,128]{3,2,1,0:T(8,128)(2,1)S(1)}, u32[]{:S(2)}, u32[]{:S(2)}) %all-to-all-start.1) | async-done | bytes 262176 | tf_op jit(solution)/shard_map/all_to_all | solution.py:124
  47.5 11.8 %all_to_all.45 = bf16[16,4,16,128]{3,2,1,0:T(8,128)(2,1)S(1)} all-to-all(bf16[16,4,16,128]{3,2,1,0:T(8,128)(2,1)S(1)} %copy.111), channel_id=1, replica_groups=mesh['quad'=8,'area'=16] {'area'}, dimensions={0} | all-to-all | bytes 524288 | tf_op jit(solution)/shard_map/all_to_all | solution.py:115
  60.0 11.8 %all_to_all.46 = bf16[16,4,16,128]{3,2,1,0:T(8,128)(2,1)S(1)} all-to-all(bf16[16,4,16,128]{3,2,1,0:T(8,128)(2,1)S(1)} %copy.113), channel_id=1, replica_groups=mesh['quad'=8,'area'=16] {'area'}, dimensions={0} | all-to-all | bytes 524288 | tf_op jit(solution)/shard_map/all_to_all | solution.py:124
  72.7 11.8 %all_to_all.47 = bf16[16,4,16,128]{3,2,1,0:T(8,128)(2,1)S(1)} all-to-all(bf16[16,4,16,128]{3,2,1,0:T(8,128)(2,1)S(1)} %copy.118), channel_id=1, replica_groups=mesh['quad'=8,'area'=16] {'area'}, dimensions={0} | all-to-all | bytes 524288 | tf_op jit(solution)/shard_map/all_to_all | solution.py:115
  85.2 11.8 %all_to_all.48 = bf16[16,4,16,128]{3,2,1,0:T(8,128)(2,1)S(1)} all-to-all(bf16[16,4,16,128]{3,2,1,0:T(8,128)(2,1)S(1)} %copy.120), channel_id=1, replica_groups=mesh['quad'=8,'area'=16] {'area'}, dimensions={0} | all-to-all | bytes 524288 | tf_op jit(solution)/shard_map/all_to_all | solution.py:124
  97.8 0.7 copy.125
  98.5 3.5 %all-to-all-start.6 = ((bf16[16,4,16,128]{3,2,1,0:T(8,128)(2,1)}), bf16[16,4,16,128]{3,2,1,0:T(8,128)(2,1)S(1)}, u32[]{:S(2)}, u32[]{:S(2)}) async-start(bf16[16,4,16,128]{3,2,1,0:T(8,128)(2,1)} %copy.125), calls=%async_computation.6 | async-start | bytes 524288 | tf_op jit(solution)/shard_map/all_to_all | solution.py:115
  102.1 1.3 slice_bitcast_fusion.3
  103.3 7.9 %all-to-all-done.6 = bf16[16,4,16,128]{3,2,1,0:T(8,128)(2,1)S(1)} async-done(((bf16[16,4,16,128]{3,2,1,0:T(8,128)(2,1)}), bf16[16,4,16,128]{3,2,1,0:T(8,128)(2,1)S(1)}, u32[]{:S(2)}, u32[]{:S(2)}) %all-to-all-start.6) | async-done | bytes 262176 | tf_op jit(solution)/shard_map/all_to_all | solution.py:115
  111.9 0.7 copy.127
  112.7 3.7 %all-to-all-start.7 = ((bf16[16,4,16,128]{3,2,1,0:T(8,128)(2,1)}), bf16[16,4,16,128]{3,2,1,0:T(8,128)(2,1)S(1)}, u32[]{:S(2)}, u32[]{:S(2)}) async-start(bf16[16,4,16,128]{3,2,1,0:T(8,128)(2,1)} %copy.127), calls=%async_computation.7 | async-start | bytes 524288 | tf_op jit(solution)/shard_map/all_to_all | solution.py:124
  116.8 8.5 %all-to-all-done.7 = bf16[16,4,16,128]{3,2,1,0:T(8,128)(2,1)S(1)} async-done(((bf16[16,4,16,128]{3,2,1,0:T(8,128)(2,1)}), bf16[16,4,16,128]{3,2,1,0:T(8,128)(2,1)S(1)}, u32[]{:S(2)}, u32[]{:S(2)}) %all-to-all-start.7) | async-done | bytes 262176 | tf_op jit(solution)/shard_map/all_to_all | solution.py:124
  125.7 3.0 %bitcast_add_fusion = f32[4,1024,128]{1,2,0:T(8,128)S(1)} fusion(bf16[4,2,256,128]{3,2,1,0:T(8,128)(2,1)S(1)} %bitcast.155, bf16[4,2,1024,320]{2,3,1,0:T(8,128)(2,1)} %copy-done, bf16[4,1024,64]{1,2,0:T(8,128)(2,1)S(1)} %get-tuple-element.19, bf16[4,1024,64]{1,2,0:T(8,128)(2,1)S(1)} %get-tuple-element.18), kind=kOutput, calls=%fused_computation.5 | convolution fusion | flops 539492352 | bytes 7864320 | tf_op jit(solution)/shard_map/qris,qrsc->qic/dot_general | solution.py:130
  129.9 15.8 %all_to_all.49 = bf16[8,2,144,128]{3,2,1,0:T(8,128)(2,1)S(1)} all-to-all(bf16[8,2,144,128]{3,2,1,0:T(8,128)(2,1)S(1)} %pad_maximum_fusion.1), channel_id=1, replica_groups=mesh['quad'=8,'area'=16] {'quad'}, dimensions={0} | all-to-all | bytes 1179648 | tf_op jit(solution)/shard_map/all_to_all | solution.py:143
  146.3 0.7 convert_reduce_fusion
  (65 shorter events, 9.2 us)
Async XLA Ops:
  0.6 2.1 %copy-start.3 = (bf16[1024,64]{0,1:T(8,128)(2,1)S(1)}, bf16[1024,64]{0,1:T(8,128)(2,1)}, u32[]{:S(2)}) copy-start(bf16[1024,64]{0,1:T(8,128)(2,1)} %param.8) | copy-start | bytes 393220
  12.0 2.3 %copy-start = (bf16[4,2,1024,320]{2,3,1,0:T(8,128)(2,1)}, bf16[4,2,1024,320]{2,3,1,0:T(8,128)(2,1)S(1)}, u32[]{:S(2)}) copy-start(bf16[4,2,1024,320]{2,3,1,0:T(8,128)(2,1)S(1)} %convert_bitcast_fusion) | copy-start | bytes 15728644
  15.5 17.0 %all-to-all-start = ((bf16[16,4,16,128]{3,2,1,0:T(8,128)(2,1)}), bf16[16,4,16,128]{3,2,1,0:T(8,128)(2,1)S(1)}, u32[]{:S(2)}, u32[]{:S(2)}) async-start(bf16[16,4,16,128]{3,2,1,0:T(8,128)(2,1)} %copy.104), calls=%async_computation | async-start | bytes 524288 | tf_op jit(solution)/shard_map/all_to_all | solution.py:115
  23.5 3.5 %copy-start.1 = (s32[16,256]{1,0:T(8,128)S(1)}, s32[16,256]{1,0:T(8,128)}, u32[]{:S(2)}) copy-start(s32[16,256]{1,0:T(8,128)} %param.10) | copy-start | bytes 49156
  23.5 3.6 %copy-start.2 = (f32[128]{0:T(128)S(1)}, f32[128]{0:T(128)}, u32[]{:S(2)}) copy-start(f32[128]{0:T(128)} %param.9) | copy-start | bytes 1540
  34.0 12.7 %all-to-all-start.1 = ((bf16[16,4,16,128]{3,2,1,0:T(8,128)(2,1)}), bf16[16,4,16,128]{3,2,1,0:T(8,128)(2,1)S(1)}, u32[]{:S(2)}, u32[]{:S(2)}) async-start(bf16[16,4,16,128]{3,2,1,0:T(8,128)(2,1)} %copy.106), calls=%async_computation.1 | async-start | bytes 524288 | tf_op jit(solution)/shard_map/all_to_all | solution.py:124
  98.5 12.7 %all-to-all-start.6 = ((bf16[16,4,16,128]{3,2,1,0:T(8,128)(2,1)}), bf16[16,4,16,128]{3,2,1,0:T(8,128)(2,1)S(1)}, u32[]{:S(2)}, u32[]{:S(2)}) async-start(bf16[16,4,16,128]{3,2,1,0:T(8,128)(2,1)} %copy.125), calls=%async_computation.6 | async-start | bytes 524288 | tf_op jit(solution)/shard_map/all_to_all | solution.py:115
  112.7 12.7 %all-to-all-start.7 = ((bf16[16,4,16,128]{3,2,1,0:T(8,128)(2,1)}), bf16[16,4,16,128]{3,2,1,0:T(8,128)(2,1)S(1)}, u32[]{:S(2)}, u32[]{:S(2)}) async-start(bf16[16,4,16,128]{3,2,1,0:T(8,128)(2,1)} %copy.127), calls=%async_computation.7 | async-start | bytes 524288 | tf_op jit(solution)/shard_map/all_to_all | solution.py:124

commit v12 on v11

--- a/solution.py
+++ b/solution.py
@@ -75,18 +75,19 @@
     bucket = shared_rows // area_count
     live_mask = jnp.arange(shared_rows) < live_counts[0]
     coupling_live = jnp.where(live_mask[None, :], coupling, jnp.zeros_like(coupling))
-    right = jnp.concatenate([probes, coupling_live], axis=1)
-    applied = jnp.einsum("qrij,jc->qric", inverses, right, preferred_element_type=F32)
-    applied = applied.astype(BF16)
+    applied_probe = jnp.einsum(
+        "qrij,jc->qric", inverses, probes, preferred_element_type=F32
+    ).astype(BF16)
+    applied_map = jnp.einsum(
+        "qrij,jc->qric", inverses, coupling_live, preferred_element_type=F32
+    ).astype(BF16)
     projected_probe = jnp.einsum(
-        "ig,qric->qrgc", coupling_live, applied[..., :probe_width], preferred_element_type=F32
+        "ig,qric->qrgc", coupling_live, applied_probe, preferred_element_type=F32
     )
     projected_map = jnp.einsum(
-        "ig,qric->qrgc", coupling_live, applied[..., probe_width:], preferred_element_type=F32
+        "ig,qric->qrgc", coupling_live, applied_map, preferred_element_type=F32
     )
-    probe_state = jnp.concatenate(
-        [applied[:, 0, :, :probe_width], applied[:, 1, :, :probe_width]], axis=-1
-    )
+    probe_state = jnp.concatenate([applied_probe[:, 0], applied_probe[:, 1]], axis=-1)
     reply_start = jnp.concatenate([projected_probe[:, 0], projected_probe[:, 1]], axis=-1)
     reply_map = jnp.concatenate([projected_map[:, 0], projected_map[:, 1]], axis=-1)
     reply_parts = (reply_map.astype(BF16),)
@@ -128,7 +129,7 @@
         gathered_block = complex_block(gathered_rows)
     part_block = gathered_block.reshape(local_points, 2, shared_rows, 2 * probe_width)
     states = probe_state.astype(F32) + jnp.einsum(
-        "qris,qrsc->qic", applied[..., probe_width:], part_block, preferred_element_type=F32
+        "qris,qrsc->qic", applied_map, part_block, preferred_element_type=F32
     )
     inner_rows = states.shape[1]
     inner_terms = weight_moments(states, angles)

time: 148 us -> 156 us (1.054)
  matrix products: 20 us -> 31.5 us
  waiting for transfers between devices: 30.7 us -> 26 us
  starting transfers between devices: 18.6 us -> 22.1 us
  local copies, waits for them, and re-layouts: 8.97 us -> 5.78 us
    dot_general x4 -> x5, matrix products: 16.2 us -> 27.8 us  [the longest x1 11 us: on_device(): jnp.einsum('qrij,jc->qric', inverses, probes, preferred_element_type=F32)]
    all_to_all x2, waiting for transfers between devices: 13.2 us -> 9.02 us  [on_device(): lax.all_to_all(parcels, 'area', split_axis=0, concat_axis=0, tiled=True)]
    all_to_all x2, starting transfers between devices: 7.24 us -> 10.7 us  [on_device(): lax.all_to_all(outgoing, 'area', split_axis=0, concat_axis=0, tiled=True)]
    unnamed x9 -> x30, local copies, waits for them, and re-layouts: 3.04 us -> 0.29 us
  transfers between devices with their start and end apart: 4 -> 4, of which waited for: 4 -> 3; matrix products, arithmetic and copies ran while one was open for 4% -> 10% of each run, Pallas kernels for 0% -> 0%
where the time goes in v12:
time: 156 us; the launch traced here: 155 us
  blocking collectives  63 us (40%)
  matrix products  31.5 us (20%)
  waiting for transfers between devices  26 us (17%)
  starting transfers between devices  22.1 us (14%)
  local copies, waits for them, and re-layouts  5.78 us (4%)
  other arithmetic  4.91 us (3%)
  between operations  1.9 us (1%)
    all_to_all x2, blocking collectives, on_device(): lax.all_to_all(parcels, 'area', split_axis=0, concat_axis=0, tiled=True)  23.6 us
    all_to_all x2, blocking collectives, on_device(): lax.all_to_all(outgoing, 'area', split_axis=0, concat_axis=0, tiled=True)  23.6 us
    all_to_all x2, waiting for transfers between devices, on_device(): lax.all_to_all(outgoing, 'area', split_axis=0, concat_axis=0, tiled=True)  16.9 us
    all_to_all x1, blocking collectives, on_device(): lax.all_to_all(both, 'quad', split_axis=0, concat_axis=0, tiled=True)  15.8 us
    all_to_all x2, starting transfers between devices, on_device(): lax.all_to_all(parcels, 'area', split_axis=0, concat_axis=0, tiled=True)  11.4 us
    dot_general x1, matrix products, on_device(): jnp.einsum('qrij,jc->qric', inverses, probes, preferred_element_type=F32)  11 us
    all_to_all x2, starting transfers between devices, on_device(): lax.all_to_all(outgoing, 'area', split_axis=0, concat_axis=0, tiled=True)  10.7 us
    dot_general x1, matrix products, on_device(): jnp.einsum('qrij,jc->qric', inverses, coupling_live, preferred_element_ty...  9.74 us
  transfers between devices with their start and end apart: 4, of which 3 were waited for; matrix products, arithmetic and copies ran while one was open for 10% of the time, Pallas kernels for 0%

profile of v12, /device:TPU:0, one launch (start us, length us, event | category | flops | bytes accessed | tf_op | source)
XLA Modules:
  0.0 155.1 jit_solution(4983759247081114601)
XLA Ops:
  1.6 11.0 %convolution_convert_fusion.1 = bf16[4,2,1024,64]{2,3,1,0:T(8,128)(2,1)S(1)} fusion(bf16[4,2,1024,1024]{3,2,1,0:T(8,128)(2,1)} %param.6, bf16[1024,64]{0,1:T(8,128)(2,1)S(1)} %copy-done), kind=kOutput, calls=%fused_computation.6 | convolution fusion | flops 1074266112 | bytes 17956864 | tf_op jit(solution)/shard_map/qrij,jc->qric/dot_general | solution.py:78
  13.6 0.7 copy.96
  14.3 7.8 %all-to-all-start = ((bf16[16,4,16,128]{3,2,1,0:T(8,128)(2,1)}), bf16[16,4,16,128]{3,2,1,0:T(8,128)(2,1)S(1)}, u32[]{:S(2)}, u32[]{:S(2)}) async-start(bf16[16,4,16,128]{3,2,1,0:T(8,128)(2,1)} %copy.96), calls=%async_computation | async-start | bytes 524288 | tf_op jit(solution)/shard_map/all_to_all | solution.py:116
  23.3 9.7 %convolution_convert_fusion = bf16[256,4,2,1024]{3,0,2,1:T(8,128)(2,1)} fusion(bf16[4,2,1024,1024]{3,2,1,0:T(8,128)(2,1)} %param.6, bf16[1024,256]{1,0:T(8,128)(2,1)} %param.7, pred[256]{0:T(512)(128)(4,1)S(1)} %iota_compare_fusion.1), kind=kOutput, calls=%fused_computation.4 | convolution fusion | flops 4297326592 | bytes 21496064 | tf_op jit(solution)/shard_map/qrij,jc->qric/dot_general | solution.py:81
  33.0 3.6 %fusion.9 = bf16[4,2,256,256]{2,3,1,0:T(8,128)(2,1)S(1)} fusion(bf16[256,4,2,1024]{3,0,2,1:T(8,128)(2,1)} %convolution_convert_fusion, bf16[1024,256]{1,0:T(8,128)(2,1)} %param.7, pred[256]{0:T(512)(128)(4,1)S(1)} %iota_compare_fusion.1), kind=kOutput, calls=%fused_computation.8 | convolution fusion | flops 1074528256 | bytes 5767424 | tf_op jit(solution)/shard_map/ig,qric->qrgc/dot_general | solution.py:87
  37.6 0.7 copy.98
  38.3 7.2 %all-to-all-start.1 = ((bf16[16,4,16,128]{3,2,1,0:T(8,128)(2,1)}), bf16[16,4,16,128]{3,2,1,0:T(8,128)(2,1)S(1)}, u32[]{:S(2)}, u32[]{:S(2)}) async-start(bf16[16,4,16,128]{3,2,1,0:T(8,128)(2,1)} %copy.98), calls=%async_computation.1 | async-start | bytes 524288 | tf_op jit(solution)/shard_map/all_to_all | solution.py:125
  45.5 0.9 slice_bitcast_fusion.1
  46.5 8.2 %all-to-all-done.1 = bf16[16,4,16,128]{3,2,1,0:T(8,128)(2,1)S(1)} async-done(((bf16[16,4,16,128]{3,2,1,0:T(8,128)(2,1)}), bf16[16,4,16,128]{3,2,1,0:T(8,128)(2,1)S(1)}, u32[]{:S(2)}, u32[]{:S(2)}) %all-to-all-start.1) | async-done | bytes 262176 | tf_op jit(solution)/shard_map/all_to_all | solution.py:125
  55.6 11.8 %all_to_all.45 = bf16[16,4,16,128]{3,2,1,0:T(8,128)(2,1)S(1)} all-to-all(bf16[16,4,16,128]{3,2,1,0:T(8,128)(2,1)S(1)} %copy.103), channel_id=1, replica_groups=mesh['quad'=8,'area'=16] {'area'}, dimensions={0} | all-to-all | bytes 524288 | tf_op jit(solution)/shard_map/all_to_all | solution.py:116
  68.1 11.8 %all_to_all.46 = bf16[16,4,16,128]{3,2,1,0:T(8,128)(2,1)S(1)} all-to-all(bf16[16,4,16,128]{3,2,1,0:T(8,128)(2,1)S(1)} %copy.105), channel_id=1, replica_groups=mesh['quad'=8,'area'=16] {'area'}, dimensions={0} | all-to-all | bytes 524288 | tf_op jit(solution)/shard_map/all_to_all | solution.py:125
  80.8 11.8 %all_to_all.47 = bf16[16,4,16,128]{3,2,1,0:T(8,128)(2,1)S(1)} all-to-all(bf16[16,4,16,128]{3,2,1,0:T(8,128)(2,1)S(1)} %copy.110), channel_id=1, replica_groups=mesh['quad'=8,'area'=16] {'area'}, dimensions={0} | all-to-all | bytes 524288 | tf_op jit(solution)/shard_map/all_to_all | solution.py:116
  93.3 11.8 %all_to_all.48 = bf16[16,4,16,128]{3,2,1,0:T(8,128)(2,1)S(1)} all-to-all(bf16[16,4,16,128]{3,2,1,0:T(8,128)(2,1)S(1)} %copy.112), channel_id=1, replica_groups=mesh['quad'=8,'area'=16] {'area'}, dimensions={0} | all-to-all | bytes 524288 | tf_op jit(solution)/shard_map/all_to_all | solution.py:125
  105.9 0.7 copy.117
  106.7 3.5 %all-to-all-start.6 = ((bf16[16,4,16,128]{3,2,1,0:T(8,128)(2,1)}), bf16[16,4,16,128]{3,2,1,0:T(8,128)(2,1)S(1)}, u32[]{:S(2)}, u32[]{:S(2)}) async-start(bf16[16,4,16,128]{3,2,1,0:T(8,128)(2,1)} %copy.117), calls=%async_computation.6 | async-start | bytes 524288 | tf_op jit(solution)/shard_map/all_to_all | solution.py:116
  110.3 9.0 %all-to-all-done.6 = bf16[16,4,16,128]{3,2,1,0:T(8,128)(2,1)S(1)} async-done(((bf16[16,4,16,128]{3,2,1,0:T(8,128)(2,1)}), bf16[16,4,16,128]{3,2,1,0:T(8,128)(2,1)S(1)}, u32[]{:S(2)}, u32[]{:S(2)}) %all-to-all-start.6) | async-done | bytes 262176 | tf_op jit(solution)/shard_map/all_to_all | solution.py:116
  120.1 0.7 copy.119
  120.8 3.5 %all-to-all-start.7 = ((bf16[16,4,16,128]{3,2,1,0:T(8,128)(2,1)}), bf16[16,4,16,128]{3,2,1,0:T(8,128)(2,1)S(1)}, u32[]{:S(2)}, u32[]{:S(2)}) async-start(bf16[16,4,16,128]{3,2,1,0:T(8,128)(2,1)} %copy.119), calls=%async_computation.7 | async-start | bytes 524288 | tf_op jit(solution)/shard_map/all_to_all | solution.py:125
  124.8 8.7 %all-to-all-done.7 = bf16[16,4,16,128]{3,2,1,0:T(8,128)(2,1)S(1)} async-done(((bf16[16,4,16,128]{3,2,1,0:T(8,128)(2,1)}), bf16[16,4,16,128]{3,2,1,0:T(8,128)(2,1)S(1)}, u32[]{:S(2)}, u32[]{:S(2)}) %all-to-all-start.7) | async-done | bytes 262176 | tf_op jit(solution)/shard_map/all_to_all | solution.py:125
  133.8 3.0 %bitcast_add_fusion = f32[4,1024,128]{1,2,0:T(8,128)S(1)} fusion(bf16[4,2,256,128]{3,2,1,0:T(8,128)(2,1)S(1)} %bitcast.153, bf16[256,4,2,1024]{3,0,2,1:T(8,128)(2,1)} %convolution_convert_fusion, bf16[4,1024,64]{1,2,0:T(8,128)(2,1)S(1)} %get-tuple-element.19, bf16[4,1024,64]{1,2,0:T(8,128)(2,1)S(1)} %get-tuple-element.18), kind=kOutput, calls=%fused_computation.5 | convolution fusion | flops 539492352 | bytes 7864320 | tf_op jit(solution)/shard_map/qris,qrsc->qic/dot_general | solution.py:131
  136.8 0.7 subtract_reduce_fusion.1
  138.0 15.8 %all_to_all.49 = bf16[8,2,144,128]{3,2,1,0:T(8,128)(2,1)S(1)} all-to-all(bf16[8,2,144,128]{3,2,1,0:T(8,128)(2,1)S(1)} %pad_maximum_fusion.1), channel_id=1, replica_groups=mesh['quad'=8,'area'=16] {'quad'}, dimensions={0} | all-to-all | bytes 1179648 | tf_op jit(solution)/shard_map/all_to_all | solution.py:144
  153.8 0.6 convert_reduce_fusion.1
  154.4 0.7 convert_reduce_fusion
  (86 shorter events, 9.1 us)
Async XLA Ops:
  0.6 0.9 copy-start
  1.6 11.0 %copy-start.14 = (bf16[1024,256]{1,0:T(8,128)(2,1)S(1)}, bf16[1024,256]{1,0:T(8,128)(2,1)}, u32[]{:S(2)}) copy-start(bf16[1024,256]{1,0:T(8,128)(2,1)} %param.7) | copy-start | bytes 1572868
  14.3 22.5 %all-to-all-start = ((bf16[16,4,16,128]{3,2,1,0:T(8,128)(2,1)}), bf16[16,4,16,128]{3,2,1,0:T(8,128)(2,1)S(1)}, u32[]{:S(2)}, u32[]{:S(2)}) async-start(bf16[16,4,16,128]{3,2,1,0:T(8,128)(2,1)} %copy.96), calls=%async_computation | async-start | bytes 524288 | tf_op jit(solution)/shard_map/all_to_all | solution.py:116
  23.3 13.5 %copy-start.8 = (f32[4]{0:T(128)}, f32[4]{0:T(128)S(1)}, u32[]{:S(2)}) copy-start(f32[4]{0:T(128)S(1)} %get-tuple-element.44) | copy-start | bytes 52
  33.0 3.6 %copy-start.10 = (s32[16,256]{1,0:T(8,128)S(1)}, s32[16,256]{1,0:T(8,128)}, u32[]{:S(2)}) copy-start(s32[16,256]{1,0:T(8,128)} %param.10) | copy-start | bytes 49156
  33.0 3.8 %copy-start.13 = (f32[128]{0:T(128)S(1)}, f32[128]{0:T(128)}, u32[]{:S(2)}) copy-start(f32[128]{0:T(128)} %param.9) | copy-start | bytes 1540
  36.8 1.6 %copy-start.4 = (f32[4]{0:T(128)}, f32[4]{0:T(128)S(1)}, u32[]{:S(2)}) copy-start(f32[4]{0:T(128)S(1)} %fusion.69) | copy-start | bytes 52
  38.3 16.4 %all-to-all-start.1 = ((bf16[16,4,16,128]{3,2,1,0:T(8,128)(2,1)}), bf16[16,4,16,128]{3,2,1,0:T(8,128)(2,1)S(1)}, u32[]{:S(2)}, u32[]{:S(2)}) async-start(bf16[16,4,16,128]{3,2,1,0:T(8,128)(2,1)} %copy.98), calls=%async_computation.1 | async-start | bytes 524288 | tf_op jit(solution)/shard_map/all_to_all | solution.py:125
  46.4 8.5 %copy-start.1 = (bf16[4,256,256]{1,2,0:T(8,128)(2,1)S(1)}, bf16[4,256,256]{1,2,0:T(8,128)(2,1)}, u32[]{:S(2)}) copy-start(bf16[4,256,256]{1,2,0:T(8,128)(2,1)} %get-tuple-element.21) | copy-start | bytes 1572868
  46.5 8.9 %copy-start.2 = (f32[4,256,64]{1,2,0:T(8,128)}, f32[4,256,64]{1,2,0:T(8,128)S(1)}, u32[]{:S(2)}) copy-start(f32[4,256,64]{1,2,0:T(8,128)S(1)} %get-tuple-element.23) | copy-start | bytes 786436
  55.5 12.2 %copy-start.5 = (f32[4]{0:T(128)S(1)}, f32[4]{0:T(128)}, u32[]{:S(2)}) copy-start(f32[4]{0:T(128)} %copy-done.4) | copy-start | bytes 52
  67.7 12.4 %copy-start.3 = (f32[4,256,64]{1,2,0:T(8,128)S(1)}, f32[4,256,64]{1,2,0:T(8,128)}, u32[]{:S(2)}) copy-start(f32[4,256,64]{1,2,0:T(8,128)} %copy-done.2) | copy-start | bytes 786436
  80.7 12.2 %copy-start.6 = (f32[4]{0:T(128)S(1)}, f32[4]{0:T(128)}, u32[]{:S(2)}) copy-start(f32[4]{0:T(128)} %copy-done.4) | copy-start | bytes 52
  106.7 12.7 %all-to-all-start.6 = ((bf16[16,4,16,128]{3,2,1,0:T(8,128)(2,1)}), bf16[16,4,16,128]{3,2,1,0:T(8,128)(2,1)S(1)}, u32[]{:S(2)}, u32[]{:S(2)}) async-start(bf16[16,4,16,128]{3,2,1,0:T(8,128)(2,1)} %copy.117), calls=%async_computation.6 | async-start | bytes 524288 | tf_op jit(solution)/shard_map/all_to_all | solution.py:116
  110.2 9.5 %copy-start.7 = (f32[4]{0:T(128)S(1)}, f32[4]{0:T(128)}, u32[]{:S(2)}) copy-start(f32[4]{0:T(128)} %copy-done.4) | copy-start | bytes 52
  110.3 14.0 %copy-start.9 = (f32[4]{0:T(128)S(1)}, f32[4]{0:T(128)}, u32[]{:S(2)}) copy-start(f32[4]{0:T(128)} %copy-done.8) | copy-start | bytes 52
  110.3 14.0 %copy-start.11 = (f32[4]{0:T(128)S(1)}, f32[4]{0:T(128)}, u32[]{:S(2)}) copy-start(f32[4]{0:T(128)} %get-tuple-element.46) | copy-start | bytes 52
  110.3 14.0 %copy-start.12 = (f32[4]{0:T(128)S(1)}, f32[4]{0:T(128)}, u32[]{:S(2)}) copy-start(f32[4]{0:T(128)} %get-tuple-element.45) | copy-start | bytes 52
  120.8 12.7 %all-to-all-start.7 = ((bf16[16,4,16,128]{3,2,1,0:T(8,128)(2,1)}), bf16[16,4,16,128]{3,2,1,0:T(8,128)(2,1)S(1)}, u32[]{:S(2)}, u32[]{:S(2)}) async-start(bf16[16,4,16,128]{3,2,1,0:T(8,128)(2,1)} %copy.119), calls=%async_computation.7 | async-start | bytes 524288 | tf_op jit(solution)/shard_map/all_to_all | solution.py:125

commit v13 on v11

--- a/solution.py
+++ b/solution.py
@@ -102,6 +102,7 @@
     angles = (point_ids.astype(jnp.float32) + 0.5) * angle_step
     shift_re = jnp.cos(angles)
     shift_im = jnp.sin(angles)
+    probe_terms = weight_moments(probe_state.astype(F32), angles)
     gathered_block = None
     interface_values = None
     for sweep_index in range(ITERS):
@@ -127,11 +128,11 @@
         )
         gathered_block = complex_block(gathered_rows)
     part_block = gathered_block.reshape(local_points, 2, shared_rows, 2 * probe_width)
-    states = probe_state.astype(F32) + jnp.einsum(
+    map_states = jnp.einsum(
         "qris,qrsc->qic", applied[..., probe_width:], part_block, preferred_element_type=F32
     )
-    inner_rows = states.shape[1]
-    inner_terms = weight_moments(states, angles)
+    inner_rows = map_states.shape[1]
+    inner_terms = probe_terms + weight_moments(map_states, angles)
     owned_terms = weight_moments(interface_values, angles)
     inner_parts = jnp.moveaxis(
         inner_terms.reshape(2, quad_count, inner_rows // quad_count, 2 * probe_width), 1, 0

time: 148 us -> 150 us (1.014)
  other arithmetic: 4 us -> 5.67 us
    unnamed x9 -> x11, local copies, waits for them, and re-layouts: 3.04 us -> 3.78 us
where the time goes in v13:
time: 150 us
  blocking collectives  62.9 us (42%)
  waiting for transfers between devices  30.5 us (20%)
  matrix products  20 us (13%)
  starting transfers between devices  18.6 us (12%)
  local copies, waits for them, and re-layouts  10.1 us (7%)
  other arithmetic  5.67 us (4%)
  between operations  1.82 us (1%)
    all_to_all x2, blocking collectives, on_device(): lax.all_to_all(outgoing, 'area', split_axis=0, concat_axis=0, tiled=True)  23.6 us
    all_to_all x2, blocking collectives, on_device(): lax.all_to_all(parcels, 'area', split_axis=0, concat_axis=0, tiled=True)  23.6 us
    all_to_all x2, waiting for transfers between devices, on_device(): lax.all_to_all(outgoing, 'area', split_axis=0, concat_axis=0, tiled=True)  17.6 us
    all_to_all x1, blocking collectives, on_device(): lax.all_to_all(both, 'quad', split_axis=0, concat_axis=0, tiled=True)  15.8 us
    all_to_all x2, waiting for transfers between devices, on_device(): lax.all_to_all(parcels, 'area', split_axis=0, concat_axis=0, tiled=True)  12.9 us
    all_to_all x2, starting transfers between devices, on_device(): lax.all_to_all(parcels, 'area', split_axis=0, concat_axis=0, tiled=True)  11.3 us
    dot_general x1, matrix products, on_device(): jnp.einsum('qrij,jc->qric', inverses, right, preferred_element_type=F32)  9.26 us
    all_to_all x2, starting transfers between devices, on_device(): lax.all_to_all(outgoing, 'area', split_axis=0, concat_axis=0, tiled=True)  7.24 us
  transfers between devices with their start and end apart: 4, of which 4 were waited for; matrix products, arithmetic and copies ran while one was open for 4% of the time, Pallas kernels for 0%

profile of v13, /device:TPU:0, one launch (start us, length us, event | category | flops | bytes accessed | tf_op | source)
XLA Modules:
  0.0 149.6 jit_solution(9401301042124529059)
XLA Ops:
  0.6 1.3 copy.98
  2.7 9.3 %convert_bitcast_fusion = bf16[4,2,1024,320]{2,3,1,0:T(8,128)(2,1)S(1)} fusion(bf16[4,2,1024,1024]{3,2,1,0:T(8,128)(2,1)} %param.6, bf16[1024,256]{0,1:T(8,128)(2,1)S(1)} %broadcast_select_fusion, bf16[1024,64]{0,1:T(8,128)(2,1)S(1)} %copy-done.4), kind=kOutput, calls=%fused_computation | convolution fusion | flops 5372641280 | bytes 22675456 | tf_op jit(solution)/shard_map/qrij,jc->qric/dot_general | solution.py:79
  12.5 1.8 %copy-done.1 = bf16[4,2,1024,320]{2,3,1,0:T(8,128)(2,1)} copy-done((bf16[4,2,1024,320]{2,3,1,0:T(8,128)(2,1)}, bf16[4,2,1024,320]{2,3,1,0:T(8,128)(2,1)S(1)}, u32[]{:S(2)}) %copy-start.1) | copy-done | bytes 5242904
  14.8 0.7 copy.108
  15.5 7.8 %all-to-all-start = ((bf16[16,4,16,128]{3,2,1,0:T(8,128)(2,1)}), bf16[16,4,16,128]{3,2,1,0:T(8,128)(2,1)S(1)}, u32[]{:S(2)}, u32[]{:S(2)}) async-start(bf16[16,4,16,128]{3,2,1,0:T(8,128)(2,1)} %copy.108), calls=%async_computation | async-start | bytes 524288 | tf_op jit(solution)/shard_map/all_to_all | solution.py:116
  23.5 3.5 %fusion.10 = bf16[4,2,256,256]{2,3,1,0:T(8,128)(2,1)S(1)} fusion(bf16[4,2,1024,320]{2,3,1,0:T(8,128)(2,1)} %copy-done.1, bf16[1024,256]{0,1:T(8,128)(2,1)S(1)} %broadcast_select_fusion), kind=kOutput, calls=%fused_computation.7 | convolution fusion | flops 1074266112 | bytes 5767168 | tf_op jit(solution)/shard_map/ig,qric->qrgc/dot_general | solution.py:84
  27.2 5.3 %all-to-all-done = bf16[16,4,16,128]{3,2,1,0:T(8,128)(2,1)S(1)} async-done(((bf16[16,4,16,128]{3,2,1,0:T(8,128)(2,1)}), bf16[16,4,16,128]{3,2,1,0:T(8,128)(2,1)S(1)}, u32[]{:S(2)}, u32[]{:S(2)}) %all-to-all-start) | async-done | bytes 262176 | tf_op jit(solution)/shard_map/all_to_all | solution.py:116
  33.2 0.7 copy.110
  34.0 3.5 %all-to-all-start.1 = ((bf16[16,4,16,128]{3,2,1,0:T(8,128)(2,1)}), bf16[16,4,16,128]{3,2,1,0:T(8,128)(2,1)S(1)}, u32[]{:S(2)}, u32[]{:S(2)}) async-start(bf16[16,4,16,128]{3,2,1,0:T(8,128)(2,1)} %copy.110), calls=%async_computation.1 | async-start | bytes 524288 | tf_op jit(solution)/shard_map/all_to_all | solution.py:125
  37.6 9.0 %all-to-all-done.1 = bf16[16,4,16,128]{3,2,1,0:T(8,128)(2,1)S(1)} async-done(((bf16[16,4,16,128]{3,2,1,0:T(8,128)(2,1)}), bf16[16,4,16,128]{3,2,1,0:T(8,128)(2,1)S(1)}, u32[]{:S(2)}, u32[]{:S(2)}) %all-to-all-start.1) | async-done | bytes 262176 | tf_op jit(solution)/shard_map/all_to_all | solution.py:125
  47.5 11.8 %all_to_all.45 = bf16[16,4,16,128]{3,2,1,0:T(8,128)(2,1)S(1)} all-to-all(bf16[16,4,16,128]{3,2,1,0:T(8,128)(2,1)S(1)} %copy.115), channel_id=1, replica_groups=mesh['quad'=8,'area'=16] {'area'}, dimensions={0} | all-to-all | bytes 524288 | tf_op jit(solution)/shard_map/all_to_all | solution.py:116
  60.0 11.8 %all_to_all.46 = bf16[16,4,16,128]{3,2,1,0:T(8,128)(2,1)S(1)} all-to-all(bf16[16,4,16,128]{3,2,1,0:T(8,128)(2,1)S(1)} %copy.117), channel_id=1, replica_groups=mesh['quad'=8,'area'=16] {'area'}, dimensions={0} | all-to-all | bytes 524288 | tf_op jit(solution)/shard_map/all_to_all | solution.py:125
  72.6 11.8 %all_to_all.47 = bf16[16,4,16,128]{3,2,1,0:T(8,128)(2,1)S(1)} all-to-all(bf16[16,4,16,128]{3,2,1,0:T(8,128)(2,1)S(1)} %copy.122), channel_id=1, replica_groups=mesh['quad'=8,'area'=16] {'area'}, dimensions={0} | all-to-all | bytes 524288 | tf_op jit(solution)/shard_map/all_to_all | solution.py:116
  85.2 11.8 %all_to_all.48 = bf16[16,4,16,128]{3,2,1,0:T(8,128)(2,1)S(1)} all-to-all(bf16[16,4,16,128]{3,2,1,0:T(8,128)(2,1)S(1)} %copy.124), channel_id=1, replica_groups=mesh['quad'=8,'area'=16] {'area'}, dimensions={0} | all-to-all | bytes 524288 | tf_op jit(solution)/shard_map/all_to_all | solution.py:125
  97.8 0.7 copy.129
  98.5 3.5 %all-to-all-start.6 = ((bf16[16,4,16,128]{3,2,1,0:T(8,128)(2,1)}), bf16[16,4,16,128]{3,2,1,0:T(8,128)(2,1)S(1)}, u32[]{:S(2)}, u32[]{:S(2)}) async-start(bf16[16,4,16,128]{3,2,1,0:T(8,128)(2,1)} %copy.129), calls=%async_computation.6 | async-start | bytes 524288 | tf_op jit(solution)/shard_map/all_to_all | solution.py:116
  102.1 1.3 slice_bitcast_fusion.3
  103.6 7.6 %all-to-all-done.6 = bf16[16,4,16,128]{3,2,1,0:T(8,128)(2,1)S(1)} async-done(((bf16[16,4,16,128]{3,2,1,0:T(8,128)(2,1)}), bf16[16,4,16,128]{3,2,1,0:T(8,128)(2,1)S(1)}, u32[]{:S(2)}, u32[]{:S(2)}) %all-to-all-start.6) | async-done | bytes 262176 | tf_op jit(solution)/shard_map/all_to_all | solution.py:116
  111.9 0.7 copy.131
  112.7 3.7 %all-to-all-start.7 = ((bf16[16,4,16,128]{3,2,1,0:T(8,128)(2,1)}), bf16[16,4,16,128]{3,2,1,0:T(8,128)(2,1)S(1)}, u32[]{:S(2)}, u32[]{:S(2)}) async-start(bf16[16,4,16,128]{3,2,1,0:T(8,128)(2,1)} %copy.131), calls=%async_computation.7 | async-start | bytes 524288 | tf_op jit(solution)/shard_map/all_to_all | solution.py:125
  116.8 8.5 %all-to-all-done.7 = bf16[16,4,16,128]{3,2,1,0:T(8,128)(2,1)S(1)} async-done(((bf16[16,4,16,128]{3,2,1,0:T(8,128)(2,1)}), bf16[16,4,16,128]{3,2,1,0:T(8,128)(2,1)S(1)}, u32[]{:S(2)}, u32[]{:S(2)}) %all-to-all-start.7) | async-done | bytes 262176 | tf_op jit(solution)/shard_map/all_to_all | solution.py:125
  125.7 3.0 %fusion.4 = f32[4,1024,128]{1,2,0:T(8,128)S(1)} fusion(bf16[4,2,256,128]{3,2,1,0:T(8,128)(2,1)S(1)} %bitcast.159, bf16[4,2,1024,320]{2,3,1,0:T(8,128)(2,1)} %copy-done.1), kind=kOutput, calls=%fused_computation.5 | convolution fusion | flops 536870912 | bytes 6815744 | tf_op jit(solution)/shard_map/qris,qrsc->qic/dot_general | solution.py:131
  128.7 1.9 %subtract_reduce_fusion.3 = (f32[1024,64]{0,1:T(8,128)S(1)}, f32[1024,64]{0,1:T(8,128)S(1)}, f32[1024,64]{0,1:T(8,128)S(1)}, f32[1024,64]{0,1:T(8,128)}, f32[102...) fusion(f32[4,1024,128]{1,2,0:T(8,128)S(1)} %maximum_convert_fusion, ...), kind=kLoop, calls=%fused_computation.40 | loop fusion | flops 7864320 | bytes 6291520 | tf_op jit(solution)/shard_map/reduce_sum | solution.py:61
  132.4 15.8 %all_to_all.49 = bf16[8,2,144,128]{3,2,1,0:T(8,128)(2,1)S(1)} all-to-all(bf16[8,2,144,128]{3,2,1,0:T(8,128)(2,1)S(1)} %pad_maximum_fusion.1), channel_id=1, replica_groups=mesh['quad'=8,'area'=16] {'quad'}, dimensions={0} | all-to-all | bytes 1179648 | tf_op jit(solution)/shard_map/all_to_all | solution.py:144
  (72 shorter events, 10.9 us)
Async XLA Ops:
  0.6 2.1 %copy-start.4 = (bf16[1024,64]{0,1:T(8,128)(2,1)S(1)}, bf16[1024,64]{0,1:T(8,128)(2,1)}, u32[]{:S(2)}) copy-start(bf16[1024,64]{0,1:T(8,128)(2,1)} %param.8) | copy-start | bytes 393220
  12.0 2.3 %copy-start.1 = (bf16[4,2,1024,320]{2,3,1,0:T(8,128)(2,1)}, bf16[4,2,1024,320]{2,3,1,0:T(8,128)(2,1)S(1)}, u32[]{:S(2)}) copy-start(bf16[4,2,1024,320]{2,3,1,0:T(8,128)(2,1)S(1)} %convert_bitcast_fusion) | copy-start | bytes 15728644
  15.5 17.0 %all-to-all-start = ((bf16[16,4,16,128]{3,2,1,0:T(8,128)(2,1)}), bf16[16,4,16,128]{3,2,1,0:T(8,128)(2,1)S(1)}, u32[]{:S(2)}, u32[]{:S(2)}) async-start(bf16[16,4,16,128]{3,2,1,0:T(8,128)(2,1)} %copy.108), calls=%async_computation | async-start | bytes 524288 | tf_op jit(solution)/shard_map/all_to_all | solution.py:116
  23.5 3.5 %copy-start.2 = (s32[16,256]{1,0:T(8,128)S(1)}, s32[16,256]{1,0:T(8,128)}, u32[]{:S(2)}) copy-start(s32[16,256]{1,0:T(8,128)} %param.10) | copy-start | bytes 49156
  23.5 3.6 %copy-start.3 = (f32[128]{0:T(128)S(1)}, f32[128]{0:T(128)}, u32[]{:S(2)}) copy-start(f32[128]{0:T(128)} %param.9) | copy-start | bytes 1540
  34.0 12.7 %all-to-all-start.1 = ((bf16[16,4,16,128]{3,2,1,0:T(8,128)(2,1)}), bf16[16,4,16,128]{3,2,1,0:T(8,128)(2,1)S(1)}, u32[]{:S(2)}, u32[]{:S(2)}) async-start(bf16[16,4,16,128]{3,2,1,0:T(8,128)(2,1)} %copy.110), calls=%async_computation.1 | async-start | bytes 524288 | tf_op jit(solution)/shard_map/all_to_all | solution.py:125
  98.5 12.7 %all-to-all-start.6 = ((bf16[16,4,16,128]{3,2,1,0:T(8,128)(2,1)}), bf16[16,4,16,128]{3,2,1,0:T(8,128)(2,1)S(1)}, u32[]{:S(2)}, u32[]{:S(2)}) async-start(bf16[16,4,16,128]{3,2,1,0:T(8,128)(2,1)} %copy.129), calls=%async_computation.6 | async-start | bytes 524288 | tf_op jit(solution)/shard_map/all_to_all | solution.py:116
  112.7 12.7 %all-to-all-start.7 = ((bf16[16,4,16,128]{3,2,1,0:T(8,128)(2,1)}), bf16[16,4,16,128]{3,2,1,0:T(8,128)(2,1)S(1)}, u32[]{:S(2)}, u32[]{:S(2)}) async-start(bf16[16,4,16,128]{3,2,1,0:T(8,128)(2,1)} %copy.131), calls=%async_computation.7 | async-start | bytes 524288 | tf_op jit(solution)/shard_map/all_to_all | solution.py:125
  130.5 0.9 copy-start

commit v14 on v11

--- a/solution.py
+++ b/solution.py
@@ -74,15 +74,24 @@
     owned_rows = interface_diagonal.shape[0]
     bucket = shared_rows // area_count
     live_mask = jnp.arange(shared_rows) < live_counts[0]
-    coupling_live = jnp.where(live_mask[None, :], coupling, jnp.zeros_like(coupling))
-    right = jnp.concatenate([probes, coupling_live], axis=1)
+    right = jnp.concatenate([probes, coupling], axis=1)
     applied = jnp.einsum("qrij,jc->qric", inverses, right, preferred_element_type=F32)
-    applied = applied.astype(BF16)
-    projected_probe = jnp.einsum(
-        "ig,qric->qrgc", coupling_live, applied[..., :probe_width], preferred_element_type=F32
+    column_mask = jnp.concatenate([jnp.ones((probe_width,), bool), live_mask])
+    applied = jnp.where(column_mask, applied, 0.0).astype(BF16)
+    row_mask = live_mask[:, None]
+    projected_probe = jnp.where(
+        row_mask,
+        jnp.einsum(
+            "ig,qric->qrgc", coupling, applied[..., :probe_width], preferred_element_type=F32
+        ),
+        0.0,
     )
-    projected_map = jnp.einsum(
-        "ig,qric->qrgc", coupling_live, applied[..., probe_width:], preferred_element_type=F32
+    projected_map = jnp.where(
+        row_mask,
+        jnp.einsum(
+            "ig,qric->qrgc", coupling, applied[..., probe_width:], preferred_element_type=F32
+        ),
+        0.0,
     )
     probe_state = jnp.concatenate(
         [applied[:, 0, :, :probe_width], applied[:, 1, :, :probe_width]], axis=-1

time: 148 us -> 148 us (level)
  no operation moved by 1% of the time
where the time goes in v14:
time: 148 us; the launch traced here: 147 us
  blocking collectives  62.9 us (42%)
  waiting for transfers between devices  30.8 us (21%)
  matrix products  20 us (14%)
  starting transfers between devices  18.6 us (13%)
  local copies, waits for them, and re-layouts  9.07 us (6%)
  other arithmetic  3.9 us (3%)
  between operations  1.76 us (1%)
    all_to_all x2, blocking collectives, on_device(): lax.all_to_all(outgoing, 'area', split_axis=0, concat_axis=0, tiled=True)  23.6 us
    all_to_all x2, blocking collectives, on_device(): lax.all_to_all(parcels, 'area', split_axis=0, concat_axis=0, tiled=True)  23.6 us
    all_to_all x2, waiting for transfers between devices, on_device(): lax.all_to_all(outgoing, 'area', split_axis=0, concat_axis=0, tiled=True)  17.6 us
    all_to_all x1, blocking collectives, on_device(): lax.all_to_all(both, 'quad', split_axis=0, concat_axis=0, tiled=True)  15.8 us
    all_to_all x2, waiting for transfers between devices, on_device(): lax.all_to_all(parcels, 'area', split_axis=0, concat_axis=0, tiled=True)  13.2 us
    all_to_all x2, starting transfers between devices, on_device(): lax.all_to_all(parcels, 'area', split_axis=0, concat_axis=0, tiled=True)  11.4 us
    dot_general x1, matrix products, on_device(): jnp.einsum('qrij,jc->qric', inverses, right, preferred_element_type=F32)  9.31 us
    all_to_all x2, starting transfers between devices, on_device(): lax.all_to_all(outgoing, 'area', split_axis=0, concat_axis=0, tiled=True)  7.24 us
  transfers between devices with their start and end apart: 4, of which 4 were waited for; matrix products, arithmetic and copies ran while one was open for 4% of the time, Pallas kernels for 0%

profile of v14, /device:TPU:0, one launch (start us, length us, event | category | flops | bytes accessed | tf_op | source)
XLA Modules:
  0.0 147.0 jit_solution(14316786255650484395)
XLA Ops:
  1.3 1.2 copy.90
  2.6 9.3 %fusion = bf16[4,2,1024,320]{2,3,1,0:T(8,128)(2,1)S(1)} fusion(pred[320]{0:T(512)(128)(4,1)S(1)} %concatenate.88, bf16[4,2,1024,1024]{3,2,1,0:T(8,128)(2,1)} %param.6, bf16[1024,256]{0,1:T(8,128)(2,1)S(1)} %copy.90, bf16[1024,64]{0,1:T(8,128)(2,1)} %param.8), kind=kOutput, calls=%fused_computation.1 | convolution fusion | flops 5375262720 | bytes 22675776 | tf_op jit(solution)/shard_map/qrij,jc->qric/dot_general | solution.py:78
  12.5 1.8 %copy-done.1 = bf16[4,2,1024,320]{2,3,1,0:T(8,128)(2,1)} copy-done((bf16[4,2,1024,320]{2,3,1,0:T(8,128)(2,1)}, bf16[4,2,1024,320]{2,3,1,0:T(8,128)(2,1)S(1)}, u32[]{:S(2)}) %copy-start.1) | copy-done | bytes 5242904
  14.8 0.7 copy.96
  15.5 7.8 %all-to-all-start = ((bf16[16,4,16,128]{3,2,1,0:T(8,128)(2,1)}), bf16[16,4,16,128]{3,2,1,0:T(8,128)(2,1)S(1)}, u32[]{:S(2)}, u32[]{:S(2)}) async-start(bf16[16,4,16,128]{3,2,1,0:T(8,128)(2,1)} %copy.96), calls=%async_computation | async-start | bytes 524288 | tf_op jit(solution)/shard_map/all_to_all | solution.py:124
  23.5 3.4 %fusion.9 = bf16[4,2,256,256]{2,3,1,0:T(8,128)(2,1)S(1)} fusion(bf16[4,2,1024,320]{2,3,1,0:T(8,128)(2,1)} %copy-done.1, pred[256]{0:T(512)(128)(4,1)S(1)} %iota_compare_fusion.1, bf16[1024,256]{1,0:T(8,128)(2,1)S(1)} %copy-done), kind=kOutput, calls=%fused_computation.8 | convolution fusion | flops 1074790400 | bytes 5767424 | tf_op jit(solution)/shard_map/ig,qric->qrgc/dot_general | solution.py:91
  27.2 5.3 %all-to-all-done = bf16[16,4,16,128]{3,2,1,0:T(8,128)(2,1)S(1)} async-done(((bf16[16,4,16,128]{3,2,1,0:T(8,128)(2,1)}), bf16[16,4,16,128]{3,2,1,0:T(8,128)(2,1)S(1)}, u32[]{:S(2)}, u32[]{:S(2)}) %all-to-all-start) | async-done | bytes 262176 | tf_op jit(solution)/shard_map/all_to_all | solution.py:124
  33.2 0.7 copy.98
  34.0 3.5 %all-to-all-start.1 = ((bf16[16,4,16,128]{3,2,1,0:T(8,128)(2,1)}), bf16[16,4,16,128]{3,2,1,0:T(8,128)(2,1)S(1)}, u32[]{:S(2)}, u32[]{:S(2)}) async-start(bf16[16,4,16,128]{3,2,1,0:T(8,128)(2,1)} %copy.98), calls=%async_computation.1 | async-start | bytes 524288 | tf_op jit(solution)/shard_map/all_to_all | solution.py:133
  37.6 9.0 %all-to-all-done.1 = bf16[16,4,16,128]{3,2,1,0:T(8,128)(2,1)S(1)} async-done(((bf16[16,4,16,128]{3,2,1,0:T(8,128)(2,1)}), bf16[16,4,16,128]{3,2,1,0:T(8,128)(2,1)S(1)}, u32[]{:S(2)}, u32[]{:S(2)}) %all-to-all-start.1) | async-done | bytes 262176 | tf_op jit(solution)/shard_map/all_to_all | solution.py:133
  47.5 11.8 %all_to_all.45 = bf16[16,4,16,128]{3,2,1,0:T(8,128)(2,1)S(1)} all-to-all(bf16[16,4,16,128]{3,2,1,0:T(8,128)(2,1)S(1)} %copy.103), channel_id=1, replica_groups=mesh['quad'=8,'area'=16] {'area'}, dimensions={0} | all-to-all | bytes 524288 | tf_op jit(solution)/shard_map/all_to_all | solution.py:124
  60.0 11.8 %all_to_all.46 = bf16[16,4,16,128]{3,2,1,0:T(8,128)(2,1)S(1)} all-to-all(bf16[16,4,16,128]{3,2,1,0:T(8,128)(2,1)S(1)} %copy.105), channel_id=1, replica_groups=mesh['quad'=8,'area'=16] {'area'}, dimensions={0} | all-to-all | bytes 524288 | tf_op jit(solution)/shard_map/all_to_all | solution.py:133
  72.6 11.8 %all_to_all.47 = bf16[16,4,16,128]{3,2,1,0:T(8,128)(2,1)S(1)} all-to-all(bf16[16,4,16,128]{3,2,1,0:T(8,128)(2,1)S(1)} %copy.110), channel_id=1, replica_groups=mesh['quad'=8,'area'=16] {'area'}, dimensions={0} | all-to-all | bytes 524288 | tf_op jit(solution)/shard_map/all_to_all | solution.py:124
  85.2 11.8 %all_to_all.48 = bf16[16,4,16,128]{3,2,1,0:T(8,128)(2,1)S(1)} all-to-all(bf16[16,4,16,128]{3,2,1,0:T(8,128)(2,1)S(1)} %copy.112), channel_id=1, replica_groups=mesh['quad'=8,'area'=16] {'area'}, dimensions={0} | all-to-all | bytes 524288 | tf_op jit(solution)/shard_map/all_to_all | solution.py:133
  97.8 0.7 copy.117
  98.5 3.5 %all-to-all-start.6 = ((bf16[16,4,16,128]{3,2,1,0:T(8,128)(2,1)}), bf16[16,4,16,128]{3,2,1,0:T(8,128)(2,1)S(1)}, u32[]{:S(2)}, u32[]{:S(2)}) async-start(bf16[16,4,16,128]{3,2,1,0:T(8,128)(2,1)} %copy.117), calls=%async_computation.6 | async-start | bytes 524288 | tf_op jit(solution)/shard_map/all_to_all | solution.py:124
  102.0 1.3 slice_bitcast_fusion.3
  103.3 7.9 %all-to-all-done.6 = bf16[16,4,16,128]{3,2,1,0:T(8,128)(2,1)S(1)} async-done(((bf16[16,4,16,128]{3,2,1,0:T(8,128)(2,1)}), bf16[16,4,16,128]{3,2,1,0:T(8,128)(2,1)S(1)}, u32[]{:S(2)}, u32[]{:S(2)}) %all-to-all-start.6) | async-done | bytes 262176 | tf_op jit(solution)/shard_map/all_to_all | solution.py:124
  111.9 0.7 copy.119
  112.6 3.7 %all-to-all-start.7 = ((bf16[16,4,16,128]{3,2,1,0:T(8,128)(2,1)}), bf16[16,4,16,128]{3,2,1,0:T(8,128)(2,1)S(1)}, u32[]{:S(2)}, u32[]{:S(2)}) async-start(bf16[16,4,16,128]{3,2,1,0:T(8,128)(2,1)} %copy.119), calls=%async_computation.7 | async-start | bytes 524288 | tf_op jit(solution)/shard_map/all_to_all | solution.py:133
  116.8 8.5 %all-to-all-done.7 = bf16[16,4,16,128]{3,2,1,0:T(8,128)(2,1)S(1)} async-done(((bf16[16,4,16,128]{3,2,1,0:T(8,128)(2,1)}), bf16[16,4,16,128]{3,2,1,0:T(8,128)(2,1)S(1)}, u32[]{:S(2)}, u32[]{:S(2)}) %all-to-all-start.7) | async-done | bytes 262176 | tf_op jit(solution)/shard_map/all_to_all | solution.py:133
  125.6 3.0 %bitcast_add_fusion = f32[4,1024,128]{1,2,0:T(8,128)S(1)} fusion(bf16[4,2,256,128]{3,2,1,0:T(8,128)(2,1)S(1)} %bitcast.156, bf16[4,2,1024,320]{2,3,1,0:T(8,128)(2,1)} %copy-done.1, bf16[4,1024,64]{1,2,0:T(8,128)(2,1)S(1)} %get-tuple-element.19, bf16[4,1024,64]{1,2,0:T(8,128)(2,1)S(1)} %get-tuple-element.18), kind=kOutput, calls=%fused_computation.6 | convolution fusion | flops 539492352 | bytes 7864320 | tf_op jit(solution)/shard_map/qris,qrsc->qic/dot_general | solution.py:139
  129.8 15.8 %all_to_all.49 = bf16[8,2,144,128]{3,2,1,0:T(8,128)(2,1)S(1)} all-to-all(bf16[8,2,144,128]{3,2,1,0:T(8,128)(2,1)S(1)} %pad_maximum_fusion.1), channel_id=1, replica_groups=mesh['quad'=8,'area'=16] {'quad'}, dimensions={0} | all-to-all | bytes 1179648 | tf_op jit(solution)/shard_map/all_to_all | solution.py:152
  146.2 0.7 convert_reduce_fusion
  (65 shorter events, 9.2 us)
Async XLA Ops:
  2.6 9.3 %copy-start = (bf16[1024,256]{1,0:T(8,128)(2,1)S(1)}, bf16[1024,256]{1,0:T(8,128)(2,1)}, u32[]{:S(2)}) copy-start(bf16[1024,256]{1,0:T(8,128)(2,1)} %param.7) | copy-start | bytes 1572868
  11.9 2.3 %copy-start.1 = (bf16[4,2,1024,320]{2,3,1,0:T(8,128)(2,1)}, bf16[4,2,1024,320]{2,3,1,0:T(8,128)(2,1)S(1)}, u32[]{:S(2)}) copy-start(bf16[4,2,1024,320]{2,3,1,0:T(8,128)(2,1)S(1)} %fusion) | copy-start | bytes 15728644
  15.5 17.0 %all-to-all-start = ((bf16[16,4,16,128]{3,2,1,0:T(8,128)(2,1)}), bf16[16,4,16,128]{3,2,1,0:T(8,128)(2,1)S(1)}, u32[]{:S(2)}, u32[]{:S(2)}) async-start(bf16[16,4,16,128]{3,2,1,0:T(8,128)(2,1)} %copy.96), calls=%async_computation | async-start | bytes 524288 | tf_op jit(solution)/shard_map/all_to_all | solution.py:124
  23.5 3.5 %copy-start.2 = (s32[16,256]{1,0:T(8,128)S(1)}, s32[16,256]{1,0:T(8,128)}, u32[]{:S(2)}) copy-start(s32[16,256]{1,0:T(8,128)} %param.10) | copy-start | bytes 49156
  23.5 3.6 %copy-start.3 = (f32[128]{0:T(128)S(1)}, f32[128]{0:T(128)}, u32[]{:S(2)}) copy-start(f32[128]{0:T(128)} %param.9) | copy-start | bytes 1540
  34.0 12.7 %all-to-all-start.1 = ((bf16[16,4,16,128]{3,2,1,0:T(8,128)(2,1)}), bf16[16,4,16,128]{3,2,1,0:T(8,128)(2,1)S(1)}, u32[]{:S(2)}, u32[]{:S(2)}) async-start(bf16[16,4,16,128]{3,2,1,0:T(8,128)(2,1)} %copy.98), calls=%async_computation.1 | async-start | bytes 524288 | tf_op jit(solution)/shard_map/all_to_all | solution.py:133
  98.5 12.7 %all-to-all-start.6 = ((bf16[16,4,16,128]{3,2,1,0:T(8,128)(2,1)}), bf16[16,4,16,128]{3,2,1,0:T(8,128)(2,1)S(1)}, u32[]{:S(2)}, u32[]{:S(2)}) async-start(bf16[16,4,16,128]{3,2,1,0:T(8,128)(2,1)} %copy.117), calls=%async_computation.6 | async-start | bytes 524288 | tf_op jit(solution)/shard_map/all_to_all | solution.py:124
  112.6 12.7 %all-to-all-start.7 = ((bf16[16,4,16,128]{3,2,1,0:T(8,128)(2,1)}), bf16[16,4,16,128]{3,2,1,0:T(8,128)(2,1)S(1)}, u32[]{:S(2)}, u32[]{:S(2)}) async-start(bf16[16,4,16,128]{3,2,1,0:T(8,128)(2,1)} %copy.119), calls=%async_computation.7 | async-start | bytes 524288 | tf_op jit(solution)/shard_map/all_to_all | solution.py:133
